TPU v7x, 32 devices: a whole 2x2x4 slice. The times are simulated.
32 devices in a mesh: dp: 8 (over z, y), tensor: 4 (over x, core).
Axes of the slice: x: 2, y: 2, z: 4, core: 2. Of those that a mesh axis runs over, the one named last changes fastest.
Arguments:
- query: bfloat16 [384, 8192], P('dp', 'tensor'), may hold values from -128 to 128
- new_key: bfloat16 [384, 512], P('dp', 'tensor'), may hold values from -6 to 6
- new_value: bfloat16 [384, 512], P('dp', 'tensor'), may hold values from -6 to 6
- cache_key: bfloat16 [384, 128, 512], P('dp', None, 'tensor'), may hold values from -6 to 6
- cache_value: bfloat16 [384, 128, 512], P('dp', None, 'tensor'), may hold values from -6 to 6
- lengths: int32 [384], P('dp'), may hold values from 1 to 128, as said below
- hidden_in: bfloat16 [384, 4096], P(('dp', 'tensor')), may hold values from -60 to 60
- out_weight: bfloat16 [8192, 4096], P('tensor', 'dp'), may hold values from -0.0625 to 0.0625
- norm_gain: float32 [4096], replicated, may hold values from 0.25 to 1.75
- route_ids: int32 [384, 8], P(('dp', 'tensor')), may hold values from 0 to 31, all different within a row; in each aligned block of 12 rows (0 to 11, 12 to 23, ...) at most 9 rows name the same one
- route_weight: float32 [384, 8], P(('dp', 'tensor')), may hold values from 0.03 to 0.3
- w_gate: bfloat16 [32, 4096, 768], P(('dp', 'tensor')), may hold values from -0.09375 to 0.09375
- w_up: bfloat16 [32, 4096, 768], P(('dp', 'tensor')), may hold values from -0.09375 to 0.09375
- w_down: bfloat16 [32, 768, 4096], P(('dp', 'tensor')), may hold values from -0.21875 to 0.21875
Outputs:
- attended: bfloat16 [384, 4096], P(('dp', 'tensor'))
- expert_mix: bfloat16 [384, 4096], P(('dp', 'tensor'))
Inputs may be any that keep to these rules, and one draw needn't show every extreme that they name: `lengths`: row 0 holds 128 positions. `route_ids`: A row names 8 different experts. In each aligned block of 12 rows (the rows of one device along dp+tensor) no expert is named by more than 9 rows, a bound that some block reaches.
All inputs are finite; a program needn't handle non-finite values.
Results may differ from a plain program's by a relative error of at most 0.013.
Values may be sent and summed in bfloat16 or wider, within the bound.
No kernel may reach another device: no remote copies, remote signals or barrier semaphores. Data moves between devices by JAX's collectives and lax.ppermute only.
A program may use at most 128 MiB of HBM per device.

v0:
```python
import math

import jax
import jax.numpy as jnp
from jax import lax
from jax.sharding import PartitionSpec as P

HD = 128


def attend_local(query, new_key, new_value, cache_key, cache_value, lengths):
    row_count = query.shape[0]
    cache_len = cache_key.shape[1]
    kv_here = new_key.shape[1] // HD
    grouping = query.shape[1] // (kv_here * HD)
    queries = query.reshape(row_count, kv_here, grouping, HD)
    cache_keys = cache_key.reshape(row_count, cache_len, kv_here, HD)
    values = cache_value.reshape(row_count, cache_len, kv_here, HD)
    own_key = new_key.reshape(row_count, kv_here, HD)
    own_value = new_value.reshape(row_count, kv_here, HD)
    factor = 1.0 / math.sqrt(HD)
    scores = (
        jnp.einsum("rkgd,rckd->rkgc", queries, cache_keys, preferred_element_type=jnp.float32)
        * factor
    )
    own_score = (
        jnp.einsum("rkgd,rkd->rkg", queries, own_key, preferred_element_type=jnp.float32) * factor
    )
    visible = (jnp.arange(cache_len, dtype=jnp.int32)[None, :] < lengths[:, None])[:, None, None, :]
    highest = jnp.maximum(jnp.max(jnp.where(visible, scores, -1e30), axis=-1), own_score)
    exponent = jnp.where(visible, jnp.exp(scores - highest[..., None]), 0.0)
    own_exponent = jnp.exp(own_score - highest)
    totals = jnp.sum(exponent, axis=-1) + own_exponent
    probability = (exponent / totals[..., None]).astype(jnp.bfloat16)
    own_probability = (own_exponent / totals).astype(jnp.bfloat16)
    combined = jnp.einsum(
        "rkgc,rckd->rkgd", probability, values, preferred_element_type=jnp.float32
    )
    combined = (
        combined
        + own_probability.astype(jnp.float32)[..., None]
        * own_value.astype(jnp.float32)[:, :, None, :]
    )
    return combined.reshape(row_count, kv_here * grouping * HD).astype(jnp.bfloat16)


def shards(
    query,
    new_key,
    new_value,
    cache_key,
    cache_value,
    lengths,
    hidden_in,
    out_weight,
    norm_gain,
    route_ids,
    route_weight,
    w_gate,
    w_up,
    w_down,
):
    heads_out = attend_local(query, new_key, new_value, cache_key, cache_value, lengths)
    n_data = lax.axis_size("dp")
    n_heads_axis = lax.axis_size("tensor")
    tok_here = hidden_in.shape[0]
    width = hidden_in.shape[1]
    partial_cols = jnp.dot(
        lax.all_gather(heads_out, "dp", axis=0, tiled=True),
        out_weight,
        preferred_element_type=jnp.float32,
    )
    by_rows = lax.all_to_all(partial_cols, "dp", split_axis=0, concat_axis=1, tiled=True)
    summed = lax.psum_scatter(by_rows, "tensor", scatter_dimension=0, tiled=True)
    attended = (hidden_in.astype(jnp.float32) + summed).astype(jnp.bfloat16)
    widened = attended.astype(jnp.float32)
    scaled = widened * lax.rsqrt(jnp.mean(widened * widened, axis=-1, keepdims=True) + 1e-06)
    normed = (scaled * norm_gain).astype(jnp.bfloat16)
    chosen_count = route_ids.shape[1]
    experts_all = n_data * n_heads_axis
    pair_count = tok_here * chosen_count
    capacity = max(2, 3 * tok_here * chosen_count // experts_all)
    flat_ids = route_ids.reshape(pair_count)
    expert_hits = (flat_ids[:, None] == jnp.arange(experts_all, dtype=jnp.int32)[None, :]).astype(
        jnp.int32
    )
    earlier = jnp.cumsum(expert_hits, axis=0) - expert_hits
    slot_index = jnp.sum(earlier * expert_hits, axis=1)
    target = flat_ids * capacity + slot_index
    placement = (
        jnp.arange(experts_all * capacity, dtype=jnp.int32)[:, None] == target[None, :]
    ).astype(jnp.bfloat16)
    token_place = jnp.sum(placement.reshape(experts_all * capacity, tok_here, chosen_count), axis=2)
    outgoing = jnp.dot(token_place, normed, preferred_element_type=jnp.float32).astype(jnp.bfloat16)
    outgoing = outgoing.reshape(experts_all, capacity, width)
    received = lax.all_to_all(outgoing, ("dp", "tensor"), split_axis=0, concat_axis=0, tiled=True)
    flat_rows = received.reshape(-1, width)
    gate_part = jnp.dot(flat_rows, w_gate[0], preferred_element_type=jnp.float32)
    up_part = jnp.dot(flat_rows, w_up[0], preferred_element_type=jnp.float32)
    activation = (jax.nn.silu(gate_part) * up_part).astype(jnp.bfloat16)
    result = jnp.dot(activation, w_down[0], preferred_element_type=jnp.float32).astype(jnp.bfloat16)
    returned = lax.all_to_all(
        result.reshape(received.shape), ("dp", "tensor"), split_axis=0, concat_axis=0, tiled=True
    )
    returned = returned.reshape(experts_all * capacity, width)
    pair_rows = jnp.einsum("sp,sd->pd", placement, returned, preferred_element_type=jnp.float32)
    weighted = route_weight[..., None] * pair_rows.reshape(tok_here, chosen_count, width)
    expert_mix = jnp.sum(weighted, axis=1).astype(jnp.bfloat16)
    return (attended, expert_mix)


def solution(mesh):
    in_specs = (
        P("dp", "tensor"),
        P("dp", "tensor"),
        P("dp", "tensor"),
        P("dp", None, "tensor"),
        P("dp", None, "tensor"),
        P("dp"),
        P(("dp", "tensor"), None),
        P("tensor", "dp"),
        P(),
        P(("dp", "tensor"), None),
        P(("dp", "tensor"), None),
        P(("dp", "tensor"), None, None),
        P(("dp", "tensor"), None, None),
        P(("dp", "tensor"), None, None),
    )
    out_specs = (P(("dp", "tensor"), None), P(("dp", "tensor"), None))
    return jax.shard_map(shards, mesh=mesh, in_specs=in_specs, out_specs=out_specs, check_vma=False)
```

profile of v0, /device:TPU:7, one launch (start us, length us, event | category | flops | bytes accessed | tf_op | source)
XLA Modules:
  0.0 353.4 jit_solution(17587841638424498671)
XLA Ops:
  7.2 0.0 copy-start
  7.2 0.0 copy-start.4
  7.2 0.0 all-gather.2.cloned.1.call-start
  7.2 0.0 copy-start.8
  7.2 0.9 iota_compare_fusion.3
  8.1 1.0 copy.35
  9.1 0.9 fusion.39
  10.1 2.4 select_reduce_fusion
  12.5 0.3 fusion.21
  12.8 0.0 copy-done.4
  12.9 0.0 copy-done.8
  12.9 0.6 fusion.17
  13.5 0.7 copy.40
  14.2 0.0 all-gather.2.cloned.1.call-update
  14.2 0.0 copy-start.5
  14.2 43.6 %all-gather.2.cloned.1.call-done = bf16[384,2048]{1,0:T(8,128)(2,1)} async-done(((bf16[48,2048]{1,0:T(8,128)(2,1)}), bf16[384,2048]{1,0:T(8,128)(2,1)}) %all-gather.2.cloned.1.call-update) | async-done | bytes 1572880 | tf_op jit(solution)/shard_map/all_gather | solution.py:69
  57.8 0.0 copy-done
  57.8 3.3 fusion.46
  61.1 4.8 %all-to-all-start = ((f32[8,48,512]{2,1,0:T(8,128)}), f32[8,48,512]{2,1,0:T(8,128)S(1)}, u32[]{:S(2)}, u32[]{:S(2)}) async-start(f32[8,48,512]{2,1,0:T(8,128)} %bitcast.50), calls=%async_computation | async-start | bytes 1572864 | tf_op jit(solution)/shard_map/all_to_all | solution.py:73
  65.9 0.0 copy-done.5
  65.9 0.1 copy.30
  65.9 0.1 reshape.162
  66.0 0.1 fusion.38
  66.1 0.1 reduce_window_sum.11
  66.3 0.2 select_reduce_fusion.1
  66.4 0.1 reduce_sum.52
  66.5 18.7 %all-to-all-done = f32[8,48,512]{2,1,0:T(8,128)S(1)} async-done(((f32[8,48,512]{2,1,0:T(8,128)}), f32[8,48,512]{2,1,0:T(8,128)S(1)}, u32[]{:S(2)}, u32[]{:S(2)}) %all-to-all-start) | async-done | bytes 786464 | tf_op jit(solution)/shard_map/all_to_all | solution.py:73
  85.2 0.9 copy.34
  86.1 14.1 %fusion = f32[16,4096]{1,0:T(8,128)S(1)} fusion(f32[48,4096]{1,0:T(8,128)} %bitcast.47), kind=kCustom, calls=%all-reduce-scatter | all-reduce-scatter fusion | flops 262145 | bytes 1049088
  100.3 1.3 collective-permute-start
  101.6 0.6 dynamic-slice.4
  102.8 0.1 fusion.36
  103.0 1.6 collective-permute-done
  104.6 0.3 concatenate
  104.9 0.2 fusion.22
  105.1 2.2 convolution_convert_fusion
  107.4 4.6 %reshape.163 = bf16[32,9,4096]{2,1,0:T(8,128)(2,1)} reshape(bf16[288,4096]{1,0:T(8,128)(2,1)} %convolution_convert_fusion) | data formatting | bytes 4718592 | tf_op jit(solution)/shard_map/reshape | solution.py:95
  112.0 102.1 %all_to_all.29 = bf16[32,9,4096]{2,1,0:T(8,128)(2,1)} all-to-all(bf16[32,9,4096]{2,1,0:T(8,128)(2,1)} %reshape.163), channel_id=1, replica_groups=mesh['dp'=8,'tensor'=4] {'dp','tensor'}, dimensions={0} | all-to-all | bytes 4718592 | tf_op jit(solution)/shard_map/all_to_all | solution.py:96
  214.1 4.7 %reshape.164 = bf16[288,4096]{1,0:T(8,128)(2,1)} reshape(bf16[32,9,4096]{2,1,0:T(8,128)(2,1)} %all_to_all.29) | data formatting | bytes 4718592 | tf_op jit(solution)/shard_map/reshape | solution.py:97
  218.8 5.5 %fusion.5 = f32[288,768]{1,0:T(8,128)S(1)} fusion(bf16[288,4096]{1,0:T(8,128)(2,1)} %reshape.164, bf16[1,4096,768]{2,1,0:T(8,128)(2,1)} %param.25), kind=kOutput, calls=%fused_computation.4 | convolution fusion | flops 1811939328 | bytes 9535488 | tf_op jit(solution)/shard_map/dot_general | solution.py:98
  224.3 11.8 %fusion.7 = bf16[288,4096]{1,0:T(8,128)(2,1)} fusion(bf16[1,768,4096]{2,1,0:T(8,128)(2,1)} %param.27, bf16[288,4096]{1,0:T(8,128)(2,1)} %reshape.164, bf16[1,4096,768]{2,1,0:T(8,128)(2,1)} %param.26, f32[288,768]{1,0:T(8,128)S(1)} %fusion.5), kind=kOutput, calls=%fused_computation.6 | convolution fusion | flops 3626385408 | bytes 18186240 | tf_op jit(solution)/shard_map/dot_general | solution.py:101
  236.1 4.6 %reshape.165 = bf16[32,9,4096]{2,1,0:T(8,128)(2,1)} reshape(bf16[288,4096]{1,0:T(8,128)(2,1)} %fusion.7) | data formatting | bytes 4718592 | tf_op jit(solution)/shard_map/reshape | solution.py:103
  240.7 4.7 %all-to-all-start.2 = ((bf16[32,9,4096]{2,1,0:T(8,128)(2,1)}), bf16[32,9,4096]{2,1,0:T(8,128)(2,1)}, u32[]{:S(2)}, u32[]{:S(2)}) async-start(bf16[32,9,4096]{2,1,0:T(8,128)(2,1)} %reshape.165), calls=%async_computation.2 | async-start | bytes 8388608 | tf_op jit(solution)/shard_map/all_to_all | solution.py:102
  245.4 0.0 copy-done.6
  245.4 0.1 copy.29
  245.5 93.0 %all-to-all-done.2 = bf16[32,9,4096]{2,1,0:T(8,128)(2,1)} async-done(((bf16[32,9,4096]{2,1,0:T(8,128)(2,1)}), bf16[32,9,4096]{2,1,0:T(8,128)(2,1)}, u32[]{:S(2)}, u32[]{:S(2)}) %all-to-all-start.2) | async-done | bytes 2359328 | tf_op jit(solution)/shard_map/all_to_all | solution.py:102
  338.5 4.7 %reshape.169 = bf16[288,4096,1]{1,0,2:T(8,128)(2,1)} reshape(bf16[32,9,4096]{2,1,0:T(8,128)(2,1)} %all-to-all-done.2) | data formatting | bytes 4718592 | tf_op jit(solution)/shard_map/reshape | solution.py:105
  343.2 3.3 fusion.10
  (16 shorter events, 0.1 us)
Async XLA Ops:
  7.2 50.6 %copy-start = (bf16[2048,512]{1,0:T(8,128)(2,1)S(1)}, bf16[2048,512]{1,0:T(8,128)(2,1)}, u32[]{:S(2)}) copy-start(bf16[2048,512]{1,0:T(8,128)(2,1)} %param.21) | copy-start | bytes 6291460
  7.2 5.7 %copy-start.4 = (bf16[48,128]{1,0:T(8,128)(2,1)S(1)}, bf16[48,128]{1,0:T(8,128)(2,1)}, u32[]{:S(2)}) copy-start(bf16[48,128]{1,0:T(8,128)(2,1)} %param.16) | copy-start | bytes 36868
  7.2 50.6 %all-gather.2.cloned.1.call-start = ((), (), s32[]{:S(2)}) async-start(), calls=%async_computation.3 | async-start | bytes 1769472 | tf_op jit(solution)/shard_map/all_gather | solution.py:69
  7.2 5.6 %copy-start.8 = (bf16[48,128,128]{2,1,0:T(8,128)(2,1)S(1)}, bf16[48,128,128]{2,1,0:T(8,128)(2,1)}, u32[]{:S(2)}) copy-start(bf16[48,128,128]{2,1,0:T(8,128)(2,1)} %param.18) | copy-start | bytes 4718596
  14.2 51.6 %copy-start.5 = (s32[12,8]{0,1:T(8,128)S(1)}, s32[12,8]{0,1:T(8,128)}, u32[]{:S(2)}) copy-start(s32[12,8]{0,1:T(8,128)} %param.23) | copy-start | bytes 1156
  61.1 40.5 %copy-start.7 = (u32[32]{0:T(128)S(1)}, u32[32]{0:T(128)}, u32[]{:S(2)}) copy-start(u32[32]{0:T(128)} %constant.35) | copy-start | bytes 388
  61.1 24.1 %all-to-all-start = ((f32[8,48,512]{2,1,0:T(8,128)}), f32[8,48,512]{2,1,0:T(8,128)S(1)}, u32[]{:S(2)}, u32[]{:S(2)}) async-start(f32[8,48,512]{2,1,0:T(8,128)} %bitcast.50), calls=%async_computation | async-start | bytes 1572864 | tf_op jit(solution)/shard_map/all_to_all | solution.py:73
  65.9 39.1 %copy-start.2 = (bf16[12,4096]{1,0:T(8,128)(2,1)S(1)}, bf16[12,4096]{1,0:T(8,128)(2,1)}, u32[]{:S(2)}) copy-start(bf16[12,4096]{1,0:T(8,128)(2,1)} %param.20) | copy-start | bytes 294916
  85.2 20.0 %copy-start.3 = (f32[4096]{0:T(1024)S(1)}, f32[4096]{0:T(1024)}, u32[]{:S(2)}) copy-start(f32[4096]{0:T(1024)} %param.22) | copy-start | bytes 49156
  100.3 4.3 %collective-permute-start = (f32[12,4096]{1,0:T(8,128)S(1)}, f32[12,4096]{1,0:T(8,128)S(1)}, u32[]{:S(2)}, u32[]{:S(2)}) collective-permute-start(f32[12,4096]{1,0:T(8,128)S(1)} %slice), channel_id=1, source_target_pairs={{0,1},{1,2},{2,3},{4,5},{5,6},{6,7},{8,9},{9,10},{10,11},{12,13},{... | collective-permute-start | bytes 589832
  105.1 6.9 %copy-start.1 = (bf16[12,4096]{1,0:T(8,128)(2,1)}, bf16[12,4096]{1,0:T(8,128)(2,1)S(1)}, u32[]{:S(2)}) copy-start(bf16[12,4096]{1,0:T(8,128)(2,1)S(1)} %get-tuple-element.3) | copy-start | bytes 294916
  240.7 4.7 %copy-start.6 = (f32[12,8]{0,1:T(8,128)S(1)}, f32[12,8]{0,1:T(8,128)}, u32[]{:S(2)}) copy-start(f32[12,8]{0,1:T(8,128)} %param.24) | copy-start | bytes 1156
  240.7 97.8 %all-to-all-start.2 = ((bf16[32,9,4096]{2,1,0:T(8,128)(2,1)}), bf16[32,9,4096]{2,1,0:T(8,128)(2,1)}, u32[]{:S(2)}, u32[]{:S(2)}) async-start(bf16[32,9,4096]{2,1,0:T(8,128)(2,1)} %reshape.165), calls=%async_computation.2 | async-start | bytes 8388608 | tf_op jit(solution)/shard_map/all_to_all | solution.py:102
Sparse Core Ops, SparseCore 0:
  14.3 43.4 all-gather.1
where the time goes:
time: 356 us; the launch traced here: 353 us
  waiting for transfers between devices  157 us (44%)
  blocking collectives  116 us (33%)
  matrix products  30 us (8%)
  local copies, waits for them, and re-layouts  22.6 us (6%)
  between operations  14.9 us (4%)
  starting transfers between devices  10.8 us (3%)
    all_to_all x1, blocking collectives, shards(): lax.all_to_all(outgoing, ('dp', 'tensor'), split_axis=0, concat_axis=0, t...  102 us
    all_to_all x1, waiting for transfers between devices, shards(): lax.all_to_all(result.reshape(received.shape), ('dp', 'tensor'), split_ax...  93 us
    all_gather x1, waiting for transfers between devices, shards(): lax.all_gather(heads_out, 'dp', axis=0, tiled=True)  43.6 us
    all_to_all x1, waiting for transfers between devices, shards(): lax.all_to_all(partial_cols, 'dp', split_axis=0, concat_axis=1, tiled=True)  18.7 us
    unnamed x1, blocking collectives  14.1 us
    dot_general x1, matrix products, shards(): jnp.dot(activation, w_down[0], preferred_element_type=jnp.float32)  11.8 us
  transfers between devices with their start and end apart: 4, of which 4 were waited for; matrix products, arithmetic and copies ran while one was open for 0% of the time, Pallas kernels for 0%

commit v1 on v0

v1 whole, which is shorter than its diff:
```python
import math

import jax
import jax.numpy as jnp
import numpy as np
from jax import lax
from jax.sharding import Mesh
from jax.sharding import PartitionSpec as P

HD = 128
DP = ("zh", "dl")
HALF = ("dl", "tensor")


def attend_local(query, new_key, new_value, cache_key, cache_value, lengths):
    row_count = query.shape[0]
    cache_len = cache_key.shape[1]
    kv_here = new_key.shape[1] // HD
    grouping = query.shape[1] // (kv_here * HD)
    queries = query.reshape(row_count, kv_here, grouping, HD)
    cache_keys = cache_key.reshape(row_count, cache_len, kv_here, HD)
    values = cache_value.reshape(row_count, cache_len, kv_here, HD)
    own_key = new_key.reshape(row_count, kv_here, HD)
    own_value = new_value.reshape(row_count, kv_here, HD)
    factor = 1.0 / math.sqrt(HD)
    scores = (
        jnp.einsum("rkgd,rckd->rkgc", queries, cache_keys, preferred_element_type=jnp.float32)
        * factor
    )
    own_score = (
        jnp.einsum("rkgd,rkd->rkg", queries, own_key, preferred_element_type=jnp.float32) * factor
    )
    visible = (jnp.arange(cache_len, dtype=jnp.int32)[None, :] < lengths[:, None])[:, None, None, :]
    highest = jnp.maximum(jnp.max(jnp.where(visible, scores, -1e30), axis=-1), own_score)
    exponent = jnp.where(visible, jnp.exp(scores - highest[..., None]), 0.0)
    own_exponent = jnp.exp(own_score - highest)
    totals = jnp.sum(exponent, axis=-1) + own_exponent
    probability = (exponent / totals[..., None]).astype(jnp.bfloat16)
    own_probability = (own_exponent / totals).astype(jnp.bfloat16)
    combined = jnp.einsum(
        "rkgc,rckd->rkgd", probability, values, preferred_element_type=jnp.float32
    )
    combined = (
        combined
        + own_probability.astype(jnp.float32)[..., None]
        * own_value.astype(jnp.float32)[:, :, None, :]
    )
    return combined.reshape(row_count, kv_here * grouping * HD).astype(jnp.bfloat16)


def swap_halves(x):
    return lax.ppermute(x, "zh", [(0, 1), (1, 0)])


def expert_layer(normed, route_ids, route_weight, w_gate, w_up, w_down):
    tok_here, width = normed.shape
    chosen_count = route_ids.shape[1]
    n_half = lax.axis_size("dl") * lax.axis_size("tensor")
    experts_all = 2 * n_half
    capacity = 2 * max(2, 3 * tok_here * chosen_count // experts_all)
    side = lax.axis_index("zh")
    other_rows = swap_halves(normed)
    other_ids = swap_halves(route_ids)
    other_weight = swap_halves(route_weight)
    first = side == 0
    rows = jnp.where(first, jnp.concatenate([normed, other_rows]), jnp.concatenate([other_rows, normed]))
    ids = jnp.where(first, jnp.concatenate([route_ids, other_ids]), jnp.concatenate([other_ids, route_ids]))
    weights = jnp.where(
        first,
        jnp.concatenate([route_weight, other_weight]),
        jnp.concatenate([other_weight, route_weight]),
    )
    held = 2 * tok_here
    pair_count = held * chosen_count
    local_ids = ids.reshape(pair_count) - side * n_half
    expert_hits = (local_ids[:, None] == jnp.arange(n_half, dtype=jnp.int32)[None, :]).astype(
        jnp.int32
    )
    earlier = jnp.cumsum(expert_hits, axis=0) - expert_hits
    slot_index = jnp.sum(earlier * expert_hits, axis=1)
    in_half = jnp.sum(expert_hits, axis=1) > 0
    target = jnp.where(in_half, local_ids * capacity + slot_index, -1)
    placement = (
        jnp.arange(n_half * capacity, dtype=jnp.int32)[:, None] == target[None, :]
    ).astype(jnp.bfloat16)
    token_place = jnp.sum(placement.reshape(n_half * capacity, held, chosen_count), axis=2)
    outgoing = jnp.dot(token_place, rows, preferred_element_type=jnp.float32).astype(jnp.bfloat16)
    outgoing = outgoing.reshape(n_half, capacity, width)
    received = lax.all_to_all(outgoing, HALF, split_axis=0, concat_axis=0, tiled=True)
    flat_rows = received.reshape(-1, width)
    gate_part = jnp.dot(flat_rows, w_gate[0], preferred_element_type=jnp.float32)
    up_part = jnp.dot(flat_rows, w_up[0], preferred_element_type=jnp.float32)
    activation = (jax.nn.silu(gate_part) * up_part).astype(jnp.bfloat16)
    result = jnp.dot(activation, w_down[0], preferred_element_type=jnp.float32).astype(jnp.bfloat16)
    returned = lax.all_to_all(
        result.reshape(received.shape), HALF, split_axis=0, concat_axis=0, tiled=True
    )
    returned = returned.reshape(n_half * capacity, width)
    pair_rows = jnp.einsum("sp,sd->pd", placement, returned, preferred_element_type=jnp.float32)
    weighted = weights[..., None] * pair_rows.reshape(held, chosen_count, width)
    partial = jnp.sum(weighted, axis=1)
    mine = jnp.where(first, partial[:tok_here], partial[tok_here:])
    theirs = jnp.where(first, partial[tok_here:], partial[:tok_here])
    return (mine + swap_halves(theirs)).astype(jnp.bfloat16)


def shards(
    query,
    new_key,
    new_value,
    cache_key,
    cache_value,
    lengths,
    hidden_in,
    out_weight,
    norm_gain,
    route_ids,
    route_weight,
    w_gate,
    w_up,
    w_down,
):
    heads_out = attend_local(query, new_key, new_value, cache_key, cache_value, lengths)
    partial_cols = jnp.dot(
        lax.all_gather(heads_out, DP, axis=0, tiled=True),
        out_weight,
        preferred_element_type=jnp.float32,
    )
    by_rows = lax.all_to_all(partial_cols, DP, split_axis=0, concat_axis=1, tiled=True)
    summed = lax.psum_scatter(by_rows, "tensor", scatter_dimension=0, tiled=True)
    attended = (hidden_in.astype(jnp.float32) + summed).astype(jnp.bfloat16)
    widened = attended.astype(jnp.float32)
    scaled = widened * lax.rsqrt(jnp.mean(widened * widened, axis=-1, keepdims=True) + 1e-06)
    normed = (scaled * norm_gain).astype(jnp.bfloat16)
    expert_mix = expert_layer(normed, route_ids, route_weight, w_gate, w_up, w_down)
    return (attended, expert_mix)


def solution(mesh):
    n_dp = mesh.shape["dp"]
    devices = np.asarray(mesh.devices).reshape(2, n_dp // 2, mesh.shape["tensor"])
    split_mesh = Mesh(devices, ("zh", "dl", "tensor"))
    rows = DP + ("tensor",)
    in_specs = (
        P(DP, "tensor"),
        P(DP, "tensor"),
        P(DP, "tensor"),
        P(DP, None, "tensor"),
        P(DP, None, "tensor"),
        P(DP),
        P(rows, None),
        P("tensor", DP),
        P(),
        P(rows, None),
        P(rows, None),
        P(rows, None, None),
        P(rows, None, None),
        P(rows, None, None),
    )
    out_specs = (P(rows, None), P(rows, None))
    return jax.shard_map(
        shards, mesh=split_mesh, in_specs=in_specs, out_specs=out_specs, check_vma=False
    )
```

time: 356 us -> 276 us (0.78)
  blocking collectives: 116 us -> 60.1 us
  waiting for transfers between devices: 157 us -> 128 us
  starting transfers between devices: 10.8 us -> 17.4 us
    all_to_all x2, waiting for transfers between devices: 112 us -> 8.49 us  [the longest x1 8.49 us: expert_layer(): lax.all_to_all(result.reshape(received.shape), HALF, split_axis=0, concat...]
    ppermute x0 -> x4, waiting for transfers between devices: none -> 72.5 us  [swap_halves(): return lax.ppermute(x, 'zh', [(0, 1), (1, 0)])]
    all_to_all x1, blocking collectives: 102 us -> 45.9 us  [expert_layer(): lax.all_to_all(outgoing, HALF, split_axis=0, concat_axis=0, tiled=True)]
    ppermute x0 -> x4, starting transfers between devices: none -> 4.68 us  [swap_halves(): return lax.ppermute(x, 'zh', [(0, 1), (1, 0)])]
    reshape x5 -> x4, local copies, waits for them, and re-layouts: 18.7 us -> 17.3 us  [the longest x1 4.35 us: expert_layer(): result.reshape(received.shape)]
  transfers between devices with their start and end apart: 4 -> 8, of which waited for: 4 -> 7; matrix products, arithmetic and copies ran while one was open for 0% -> 1% of each run, Pallas kernels for 0% -> 0%
where the time goes in v1:
time: 276 us; the launch traced here: 275 us
  waiting for transfers between devices  128 us (46%)
  blocking collectives  60.1 us (22%)
  matrix products  29.8 us (11%)
  local copies, waits for them, and re-layouts  21.7 us (8%)
  starting transfers between devices  17.4 us (6%)
  between operations  15 us (5%)
  other arithmetic  3.34 us (1%)
    ppermute x4, waiting for transfers between devices, swap_halves(): return lax.ppermute(x, 'zh', [(0, 1), (1, 0)])  72.5 us
    all_to_all x1, blocking collectives, expert_layer(): lax.all_to_all(outgoing, HALF, split_axis=0, concat_axis=0, tiled=True)  45.9 us
    all_gather x1, waiting for transfers between devices, shards(): lax.all_gather(heads_out, DP, axis=0, tiled=True)  43.6 us
    unnamed x1, blocking collectives  14.1 us
    dot_general x1, matrix products, expert_layer(): jnp.dot(activation, w_down[0], preferred_element_type=jnp.float32)  11.8 us
    all_to_all x1, waiting for transfers between devices, expert_layer(): lax.all_to_all(result.reshape(received.shape), HALF, split_axis=0, concat...  8.49 us
    all_to_all x1, starting transfers between devices, expert_layer(): lax.all_to_all(result.reshape(received.shape), HALF, split_axis=0, concat...  6.7 us
  transfers between devices with their start and end apart: 8, of which 7 were waited for; matrix products, arithmetic and copies ran while one was open for 1% of the time, Pallas kernels for 0%

profile of v1, /device:TPU:7, one launch (start us, length us, event | category | flops | bytes accessed | tf_op | source)
XLA Modules:
  0.0 274.8 jit_solution(13641257148491333501)
XLA Ops:
  7.2 0.9 iota_compare_fusion.2
  8.1 1.0 copy.47
  9.1 0.9 fusion.43
  10.1 2.4 select_reduce_fusion
  12.5 0.3 fusion.20
  12.9 0.6 fusion.16
  13.5 0.7 copy.54
  14.3 43.6 %all-gather.2.cloned.1.call-done = bf16[384,2048]{1,0:T(8,128)(2,1)} async-done(((bf16[48,2048]{1,0:T(8,128)(2,1)}), bf16[384,2048]{1,0:T(8,128)(2,1)}) %all-gather.2.cloned.1.call-update) | async-done | bytes 1572880 | tf_op jit(solution)/shard_map/all_gather | solution.py:125
  57.8 3.3 %fusion.53 = f32[384,512]{1,0:T(8,128)} fusion(bf16[384,2048]{1,0:T(8,128)(2,1)} %all-gather.2.cloned.1.call-done, bf16[2048,512]{1,0:T(8,128)(2,1)S(1)} %copy-done), kind=kOutput, calls=%fused_computation.79 | convolution fusion | flops 805306368 | bytes 4456448 | tf_op jit(solution)/shard_map/dot_general | solution.py:124
  61.1 4.6 %all-to-all-start = ((f32[8,48,512]{2,1,0:T(8,128)}), f32[8,48,512]{2,1,0:T(8,128)S(1)}, u32[]{:S(2)}, u32[]{:S(2)}) async-start(f32[8,48,512]{2,1,0:T(8,128)} %bitcast.64), calls=%async_computation | async-start | bytes 1572864 | tf_op jit(solution)/shard_map/all_to_all | solution.py:129
  65.7 2.2 collective-permute-start.1
  67.9 0.6 dynamic-slice.4
  69.1 16.1 %collective-permute-done.1 = s32[12,8]{0,1:T(8,128)S(1)} collective-permute-done((s32[12,8]{0,1:T(8,128)S(1)}, s32[12,8]{0,1:T(8,128)S(1)}, u32[]{:S(2)}, u32[]{:S(2)}) %collective-permute-start.1) | collective-permute-done | bytes 416 | tf_op jit(solution)/shard_map/ppermute | solution.py:52
  85.2 0.1 pad_add_fusion.1
  85.3 0.1 copy.38
  85.4 0.1 sub.39
  85.6 0.6 reduce-window.6
  86.2 0.2 slice_reduce_fusion
  86.4 0.1 bitcast_bitcast_fusion
  86.5 0.1 reduce_sum.62
  86.6 0.1 gt.16
  86.7 0.9 copy.45
  87.6 14.1 %fusion = f32[16,4096]{1,0:T(8,128)S(1)} fusion(f32[48,4096]{1,0:T(8,128)} %bitcast.61), kind=kCustom, calls=%all-reduce-scatter | all-reduce-scatter fusion | flops 262145 | bytes 1049088
  101.8 1.3 collective-permute-start.4
  103.1 3.0 %collective-permute-done.4 = f32[12,4096]{1,0:T(8,128)S(1)} collective-permute-done((f32[12,4096]{1,0:T(8,128)S(1)}, f32[12,4096]{1,0:T(8,128)S(1)}, u32[]{:S(2)}, u32[]{:S(2)}) %collective-permute-start.4) | collective-permute-done | bytes 196640
  106.1 0.3 concatenate.32
  106.5 0.2 fusion.27
  106.7 0.1 fusion.29
  106.9 0.2 fusion.41
  107.0 5.8 %collective-permute-done.2 = bf16[12,4096]{1,0:T(8,128)(2,1)S(1)} collective-permute-done((bf16[12,4096]{1,0:T(8,128)(2,1)S(1)}, bf16[12,4096]{1,0:T(8,128)(2,1)S(1)}, u32[]{:S(2)}, u32[]{:S(2)}) %collective-permute-start.2) | collective-permute-done | bytes 98336 | tf_op jit(solution)/shard_map/ppermute | solution.py:52
  112.8 2.2 convolution_convert_fusion
  115.1 4.3 %reshape.229 = bf16[16,18,4096]{2,1,0:T(8,128)(2,1)} reshape(bf16[288,4096]{1,0:T(8,128)(2,1)} %convolution_convert_fusion) | data formatting | bytes 4718592 | tf_op jit(solution)/shard_map/reshape | solution.py:88
  119.4 45.9 %all_to_all.29 = bf16[16,18,4096]{2,1,0:T(8,128)(2,1)} all-to-all(bf16[16,18,4096]{2,1,0:T(8,128)(2,1)} %reshape.229), channel_id=1, replica_groups=mesh['zh'=2,'dl'=4,'tensor'=4] {'dl','tensor'}, dimensions={0} | all-to-all | bytes 4718592 | tf_op jit(solution)/shard_map/all_to_all | solution.py:89
  165.3 4.3 %reshape.230 = bf16[288,4096]{1,0:T(8,128)(2,1)} reshape(bf16[16,18,4096]{2,1,0:T(8,128)(2,1)} %all_to_all.29) | data formatting | bytes 4718592 | tf_op jit(solution)/shard_map/reshape | solution.py:90
  169.6 5.5 %fusion.5 = f32[288,768]{1,0:T(8,128)S(1)} fusion(bf16[288,4096]{1,0:T(8,128)(2,1)} %reshape.230, bf16[1,4096,768]{2,1,0:T(8,128)(2,1)} %param.25), kind=kOutput, calls=%fused_computation.4 | convolution fusion | flops 1811939328 | bytes 9535488 | tf_op jit(solution)/shard_map/dot_general | solution.py:91
  175.1 11.8 %fusion.7 = bf16[288,4096]{1,0:T(8,128)(2,1)} fusion(bf16[1,768,4096]{2,1,0:T(8,128)(2,1)} %param.27, bf16[288,4096]{1,0:T(8,128)(2,1)} %reshape.230, bf16[1,4096,768]{2,1,0:T(8,128)(2,1)} %param.26, f32[288,768]{1,0:T(8,128)S(1)} %fusion.5), kind=kOutput, calls=%fused_computation.6 | convolution fusion | flops 3626385408 | bytes 18186240 | tf_op jit(solution)/shard_map/dot_general | solution.py:94
  186.9 4.3 %reshape.231 = bf16[16,18,4096]{2,1,0:T(8,128)(2,1)} reshape(bf16[288,4096]{1,0:T(8,128)(2,1)} %fusion.7) | data formatting | bytes 4718592 | tf_op jit(solution)/shard_map/reshape | solution.py:96
  191.3 6.7 %all-to-all-start.2 = ((bf16[16,18,4096]{2,1,0:T(8,128)(2,1)}), bf16[16,18,4096]{2,1,0:T(8,128)(2,1)}, u32[]{:S(2)}, u32[]{:S(2)}) async-start(bf16[16,18,4096]{2,1,0:T(8,128)(2,1)} %reshape.231), calls=%async_computation.2 | async-start | bytes 6291456 | tf_op jit(solution)/shard_map/all_to_all | solution.py:95
  198.0 1.3 collective-permute-start
  199.3 37.0 %collective-permute-done = f32[12,8]{0,1:T(8,128)S(1)} collective-permute-done((f32[12,8]{0,1:T(8,128)S(1)}, f32[12,8]{0,1:T(8,128)S(1)}, u32[]{:S(2)}, u32[]{:S(2)}) %collective-permute-start) | collective-permute-done | bytes 416 | tf_op jit(solution)/shard_map/ppermute | solution.py:52
  236.3 0.1 pad_maximum_fusion.1
  236.3 0.1 copy.36
  236.5 8.5 %all-to-all-done.2 = bf16[16,18,4096]{2,1,0:T(8,128)(2,1)} async-done(((bf16[16,18,4096]{2,1,0:T(8,128)(2,1)}), bf16[16,18,4096]{2,1,0:T(8,128)(2,1)}, u32[]{:S(2)}, u32[]{:S(2)}) %all-to-all-start.2) | async-done | bytes 2359328 | tf_op jit(solution)/shard_map/all_to_all | solution.py:95
  245.0 4.3 %reshape.236 = bf16[288,4096,1]{1,0,2:T(8,128)(2,1)} reshape(bf16[16,18,4096]{2,1,0:T(8,128)(2,1)} %all-to-all-done.2) | data formatting | bytes 4718592 | tf_op jit(solution)/shard_map/reshape | solution.py:98
  249.3 3.1 %multiply_reduce_fusion = f32[24,4096]{1,0:T(8,128)S(1)} fusion(f32[24,8]{1,0:T(8,128)S(1)} %broadcast_select_fusion, bf16[288,4096,1]{1,0,2:T(8,128)(2,1)} %reshape.236, s32[192]{0:T(256)S(1)} %get-tuple-element.4), kind=kOutput, calls=%fused_computation.8 | convolution fusion | flops 454514688 | bytes 2754048 | tf_op jit(solution)/shard_map/sp,sd->pd/dot_general | solution.py:99
  252.5 1.1 collective-permute-start.3
  253.6 13.6 %collective-permute-done.3 = f32[12,4096]{1,0:T(8,128)S(1)} collective-permute-done((f32[12,4096]{1,0:T(8,128)S(1)}, f32[12,4096]{1,0:T(8,128)S(1)}, u32[]{:S(2)}, u32[]{:S(2)}) %collective-permute-start.3) | collective-permute-done | bytes 196640 | tf_op jit(solution)/shard_map/ppermute | solution.py:52
  267.2 0.7 add_convert_fusion
  (39 shorter events, 0.5 us)
Async XLA Ops:
  7.2 50.6 %copy-start = (bf16[2048,512]{1,0:T(8,128)(2,1)S(1)}, bf16[2048,512]{1,0:T(8,128)(2,1)}, u32[]{:S(2)}) copy-start(bf16[2048,512]{1,0:T(8,128)(2,1)} %param.21) | copy-start | bytes 6291460
  7.2 5.7 %copy-start.4 = (bf16[48,128]{1,0:T(8,128)(2,1)S(1)}, bf16[48,128]{1,0:T(8,128)(2,1)}, u32[]{:S(2)}) copy-start(bf16[48,128]{1,0:T(8,128)(2,1)} %param.16) | copy-start | bytes 36868
  7.2 50.6 %all-gather.2.cloned.1.call-start = ((), (), s32[]{:S(2)}) async-start(), calls=%async_computation.3 | async-start | bytes 1769472 | tf_op jit(solution)/shard_map/all_gather | solution.py:125
  7.2 5.6 %copy-start.8 = (bf16[48,128,128]{2,1,0:T(8,128)(2,1)S(1)}, bf16[48,128,128]{2,1,0:T(8,128)(2,1)}, u32[]{:S(2)}) copy-start(bf16[48,128,128]{2,1,0:T(8,128)(2,1)} %param.18) | copy-start | bytes 4718596
  14.2 51.5 %copy-start.5 = (s32[12,8]{0,1:T(8,128)S(1)}, s32[12,8]{0,1:T(8,128)}, u32[]{:S(2)}) copy-start(s32[12,8]{0,1:T(8,128)} %param.23) | copy-start | bytes 1156
  14.2 53.7 %copy-start.7 = (u32[32]{0:T(128)S(1)}, u32[32]{0:T(128)}, u32[]{:S(2)}) copy-start(u32[32]{0:T(128)} %constant.50) | copy-start | bytes 388
  61.1 25.6 %all-to-all-start = ((f32[8,48,512]{2,1,0:T(8,128)}), f32[8,48,512]{2,1,0:T(8,128)S(1)}, u32[]{:S(2)}, u32[]{:S(2)}) async-start(f32[8,48,512]{2,1,0:T(8,128)} %bitcast.64), calls=%async_computation | async-start | bytes 1572864 | tf_op jit(solution)/shard_map/all_to_all | solution.py:129
  65.7 40.7 %copy-start.2 = (bf16[12,4096]{1,0:T(8,128)(2,1)S(1)}, bf16[12,4096]{1,0:T(8,128)(2,1)}, u32[]{:S(2)}) copy-start(bf16[12,4096]{1,0:T(8,128)(2,1)} %param.20) | copy-start | bytes 294916
  65.7 19.5 %collective-permute-start.1 = (s32[12,8]{0,1:T(8,128)S(1)}, s32[12,8]{0,1:T(8,128)S(1)}, u32[]{:S(2)}, u32[]{:S(2)}) collective-permute-start(s32[12,8]{0,1:T(8,128)S(1)} %copy-done.5), channel_id=1, source_target_pairs={{0,16},{16,0},{1,17},{17,1},{2,18},{18,2},{3,19},{19,3},{4,20},{20... | collective-permute-start | bytes 1160 | tf_op jit(solution)/shard_map/ppermute | solution.py:52
  86.7 20.0 %copy-start.3 = (f32[4096]{0:T(1024)S(1)}, f32[4096]{0:T(1024)}, u32[]{:S(2)}) copy-start(f32[4096]{0:T(1024)} %param.22) | copy-start | bytes 49156
  101.8 4.3 %collective-permute-start.4 = (f32[12,4096]{1,0:T(8,128)S(1)}, f32[12,4096]{1,0:T(8,128)S(1)}, u32[]{:S(2)}, u32[]{:S(2)}) collective-permute-start(f32[12,4096]{1,0:T(8,128)S(1)} %slice.26), channel_id=1, source_target_pairs={{0,1},{1,2},{2,3},{4,5},{5,6},{6,7},{8,9},{9,10},{10,11},{12,13},{... | collective-permute-start | bytes 589832
  106.7 12.7 %copy-start.1 = (bf16[12,4096]{1,0:T(8,128)(2,1)}, bf16[12,4096]{1,0:T(8,128)(2,1)S(1)}, u32[]{:S(2)}) copy-start(bf16[12,4096]{1,0:T(8,128)(2,1)S(1)} %get-tuple-element.7) | copy-start | bytes 294916
  106.8 6.0 %collective-permute-start.2 = (bf16[12,4096]{1,0:T(8,128)(2,1)S(1)}, bf16[12,4096]{1,0:T(8,128)(2,1)S(1)}, u32[]{:S(2)}, u32[]{:S(2)}) collective-permute-start(bf16[12,4096]{1,0:T(8,128)(2,1)S(1)} %fusion.29), channel_id=1, source_target_pairs={{0,16},{16,0},{1,17},{17,1},{2,18},{18,2},{3,19},{19,3},{4,20},{20... | collective-permute-start | bytes 294920 | tf_op jit(solution)/shard_map/ppermute | solution.py:52
  191.3 6.7 %copy-start.6 = (f32[12,8]{0,1:T(8,128)S(1)}, f32[12,8]{0,1:T(8,128)}, u32[]{:S(2)}) copy-start(f32[12,8]{0,1:T(8,128)} %param.24) | copy-start | bytes 1156
  191.3 53.7 %all-to-all-start.2 = ((bf16[16,18,4096]{2,1,0:T(8,128)(2,1)}), bf16[16,18,4096]{2,1,0:T(8,128)(2,1)}, u32[]{:S(2)}, u32[]{:S(2)}) async-start(bf16[16,18,4096]{2,1,0:T(8,128)(2,1)} %reshape.231), calls=%async_computation.2 | async-start | bytes 6291456 | tf_op jit(solution)/shard_map/all_to_all | solution.py:95
  198.0 38.3 %collective-permute-start = (f32[12,8]{0,1:T(8,128)S(1)}, f32[12,8]{0,1:T(8,128)S(1)}, u32[]{:S(2)}, u32[]{:S(2)}) collective-permute-start(f32[12,8]{0,1:T(8,128)S(1)} %copy-done.6), channel_id=1, source_target_pairs={{0,16},{16,0},{1,17},{17,1},{2,18},{18,2},{3,19},{19,3},{4,20},{20... | collective-permute-start | bytes 1160 | tf_op jit(solution)/shard_map/ppermute | solution.py:52
  252.5 14.8 %collective-permute-start.3 = (f32[12,4096]{1,0:T(8,128)S(1)}, f32[12,4096]{1,0:T(8,128)S(1)}, u32[]{:S(2)}, u32[]{:S(2)}) collective-permute-start(f32[12,4096]{1,0:T(8,128)S(1)} %slice_select_fusion), channel_id=1, source_target_pairs={{0,16},{16,0},{1,17},{17,1},{2,18},{18,2},{3,19},{19,3},{4,20},{20... | collective-permute-start | bytes 589832 | tf_op jit(solution)/shard_map/ppermute | solution.py:52
Sparse Core Ops, SparseCore 0:
  14.3 43.4 all-gather.1

commit v2 on v1

--- a/solution.py
+++ b/solution.py
@@ -121,13 +121,27 @@
     w_down,
 ):
     heads_out = attend_local(query, new_key, new_value, cache_key, cache_value, lengths)
+    n_dl = lax.axis_size("dl")
+    n_t = lax.axis_size("tensor")
+    tok_here = hidden_in.shape[0]
+    first = lax.axis_index("zh") == 0
+    other_heads = swap_halves(heads_out)
+    pair_heads = jnp.where(
+        first,
+        jnp.concatenate([heads_out, other_heads]),
+        jnp.concatenate([other_heads, heads_out]),
+    )
+    spread = jnp.broadcast_to(pair_heads[None], (n_dl,) + pair_heads.shape)
+    gathered = lax.all_to_all(spread, "dl", split_axis=0, concat_axis=0, tiled=True)
     partial_cols = jnp.dot(
-        lax.all_gather(heads_out, DP, axis=0, tiled=True),
-        out_weight,
-        preferred_element_type=jnp.float32,
+        gathered.reshape(-1, gathered.shape[-1]), out_weight, preferred_element_type=jnp.float32
     )
-    by_rows = lax.all_to_all(partial_cols, DP, split_axis=0, concat_axis=1, tiled=True)
-    summed = lax.psum_scatter(by_rows, "tensor", scatter_dimension=0, tiled=True)
+    col_width = partial_cols.shape[-1]
+    by_dest = partial_cols.reshape(n_dl, 2, n_t, tok_here, col_width).transpose(1, 0, 2, 3, 4)
+    by_dest = by_dest.reshape(2 * n_dl * n_t, tok_here, col_width)
+    arrived = lax.all_to_all(by_dest, DP + ("tensor",), split_axis=0, concat_axis=0, tiled=True)
+    summed = jnp.sum(arrived.reshape(2 * n_dl, n_t, tok_here, col_width), axis=1)
+    summed = summed.transpose(1, 0, 2).reshape(tok_here, 2 * n_dl * col_width)
     attended = (hidden_in.astype(jnp.float32) + summed).astype(jnp.bfloat16)
     widened = attended.astype(jnp.float32)
     scaled = widened * lax.rsqrt(jnp.mean(widened * widened, axis=-1, keepdims=True) + 1e-06)

time: 276 us -> 241 us (0.87)
  blocking collectives: 60.1 us -> 41.8 us
  between operations: 15 us -> 0.92 us
  waiting for transfers between devices: 128 us -> 117 us
  starting transfers between devices: 17.4 us -> 24.7 us
  local copies, waits for them, and re-layouts: 21.7 us -> 24.6 us
    all_gather x1 -> x0, waiting for transfers between devices: 43.6 us -> none  [shards(): lax.all_gather(heads_out, DP, axis=0, tiled=True)]
    all_to_all x1 -> x2, waiting for transfers between devices: 0.01 us -> 39.2 us  [the longest x1 23.8 us: shards(): lax.all_to_all(by_dest, DP + ('tensor',), split_axis=0, concat_axis=0, ti...]
    unnamed x1 -> x0, blocking collectives: 14.1 us -> none
    all_to_all x1 -> x2, starting transfers between devices: 4.64 us -> 12.2 us  [the longest x1 7.66 us: shards(): lax.all_to_all(by_dest, DP + ('tensor',), split_axis=0, concat_axis=0, ti...]
    all_to_all x1, blocking collectives: 45.9 us -> 41.8 us  [expert_layer(): lax.all_to_all(outgoing, HALF, split_axis=0, concat_axis=0, tiled=True)]
    ppermute x4 -> x5, waiting for transfers between devices: 72.5 us -> 69.1 us  [swap_halves(): return lax.ppermute(x, 'zh', [(0, 1), (1, 0)])]
    unnamed x2 -> x0, waiting for transfers between devices: 3.02 us -> none
    ppermute x4 -> x5, starting transfers between devices: 4.68 us -> 5.84 us  [swap_halves(): return lax.ppermute(x, 'zh', [(0, 1), (1, 0)])]
  transfers between devices with their start and end apart: 8 -> 8, of which waited for: 7 -> 7; matrix products, arithmetic and copies ran while one was open for 1% -> 3% of each run, Pallas kernels for 0% -> 0%
where the time goes in v2:
time: 241 us; the launch traced here: 240 us
  waiting for transfers between devices  117 us (49%)
  blocking collectives  41.8 us (17%)
  matrix products  27.8 us (12%)
  starting transfers between devices  24.7 us (10%)
  local copies, waits for them, and re-layouts  24.6 us (10%)
  other arithmetic  3.49 us (1%)
    ppermute x5, waiting for transfers between devices, swap_halves(): return lax.ppermute(x, 'zh', [(0, 1), (1, 0)])  69.1 us
    all_to_all x1, blocking collectives, expert_layer(): lax.all_to_all(outgoing, HALF, split_axis=0, concat_axis=0, tiled=True)  41.8 us
    all_to_all x1, waiting for transfers between devices, shards(): lax.all_to_all(by_dest, DP + ('tensor',), split_axis=0, concat_axis=0, ti...  23.8 us
    all_to_all x1, waiting for transfers between devices, shards(): lax.all_to_all(spread, 'dl', split_axis=0, concat_axis=0, tiled=True)  15.5 us
    dot_general x1, matrix products, expert_layer(): jnp.dot(activation, w_down[0], preferred_element_type=jnp.float32)  11.8 us
    all_to_all x1, waiting for transfers between devices, expert_layer(): lax.all_to_all(result.reshape(received.shape), HALF, split_axis=0, concat...  8.49 us
    all_to_all x1, starting transfers between devices, shards(): lax.all_to_all(by_dest, DP + ('tensor',), split_axis=0, concat_axis=0, ti...  7.66 us
    all_to_all x1, starting transfers between devices, expert_layer(): lax.all_to_all(result.reshape(received.shape), HALF, split_axis=0, concat...  6.73 us
  transfers between devices with their start and end apart: 8, of which 7 were waited for; matrix products, arithmetic and copies ran while one was open for 3% of the time, Pallas kernels for 0%

profile of v2, /device:TPU:7, one launch (start us, length us, event | category | flops | bytes accessed | tf_op | source)
XLA Modules:
  0.0 240.1 jit_solution(2237263764154511756)
XLA Ops:
  0.7 0.9 iota_compare_fusion.2
  1.5 1.0 copy.77
  2.6 0.9 fusion.49
  3.5 2.4 %select_reduce_fusion = (f32[48,16]{1,0:T(8,128)S(1)}, f32[48,16,128]{2,1,0:T(8,128)S(1)}) fusion(pred[48,128]{1,0:T(8,128)(4,1)S(1)} %iota_compare_fusion.2, bf16[48,16,128]{2,1,0:T(8,128)(2,1)S(1)} %bitcast.74, bf16[48,128,128]{2,1,0:T(8,128)(2,1)} %param.17), kind=kOutput, calls=%fused_computation.23 | convolution fusion | flops 25459968 | bytes 2171904 | tf_op jit(solution)/shard_map/rkgd,rckd->rkgc/dot_general | solution.py:27
  5.9 0.3 fusion.27
  6.3 0.6 fusion.23
  7.0 2.4 collective-permute-start
  9.4 8.6 %collective-permute-done = bf16[48,2048]{1,0:T(8,128)(2,1)S(1)} collective-permute-done((bf16[48,2048]{1,0:T(8,128)(2,1)S(1)}, bf16[48,2048]{1,0:T(8,128)(2,1)S(1)}, u32[]{:S(2)}, u32[]{:S(2)}) %collective-permute-start) | collective-permute-done | bytes 196640 | tf_op jit(solution)/shard_map/ppermute | solution.py:52
  18.1 1.3 broadcast_in_dim.47
  19.4 4.5 %all-to-all-start = ((bf16[4,96,2048]{2,1,0:T(8,128)(2,1)}), bf16[4,96,2048]{2,1,0:T(8,128)(2,1)}, u32[]{:S(2)}, u32[]{:S(2)}) async-start(bf16[4,96,2048]{2,1,0:T(8,128)(2,1)} %broadcast_in_dim.47), calls=%async_computation | async-start | bytes 3145728 | tf_op jit(solution)/shard_map/all_to_all | solution.py:135
  23.9 2.4 %collective-permute-start.2 = (s32[12,8]{0,1:T(8,128)S(1)}, s32[12,8]{0,1:T(8,128)S(1)}, u32[]{:S(2)}, u32[]{:S(2)}) collective-permute-start(s32[12,8]{0,1:T(8,128)S(1)} %copy-done.5), channel_id=1, source_target_pairs={{0,16},{16,0},{1,17},{17,1},{2,18},{18,2},{3,19},{19,3},{4,20},{20... | collective-permute-start | bytes 1160 | tf_op jit(solution)/shard_map/ppermute | solution.py:52
  26.4 15.5 %all-to-all-done = bf16[4,96,2048]{2,1,0:T(8,128)(2,1)} async-done(((bf16[4,96,2048]{2,1,0:T(8,128)(2,1)}), bf16[4,96,2048]{2,1,0:T(8,128)(2,1)}, u32[]{:S(2)}, u32[]{:S(2)}) %all-to-all-start) | async-done | bytes 1572896 | tf_op jit(solution)/shard_map/all_to_all | solution.py:135
  41.8 2.6 %copy.59 = bf16[4,96,2048]{2,0,1:T(4,128)(2,1)S(1)} copy(bf16[4,96,2048]{2,1,0:T(8,128)(2,1)} %all-to-all-done) | data formatting | bytes 3145728 | tf_op jit(solution)/shard_map/all_to_all | solution.py:135
  44.5 1.3 fusion.12
  45.8 1.1 copy.73
  46.9 7.7 %all-to-all-start.1 = ((f32[32,12,512]{2,1,0:T(8,128)}), f32[32,12,512]{2,1,0:T(8,128)S(1)}, u32[]{:S(2)}, u32[]{:S(2)}) async-start(f32[32,12,512]{2,1,0:T(8,128)} %bitcast.68), calls=%async_computation.1 | async-start | bytes 2097152 | tf_op jit(solution)/shard_map/all_to_all | solution.py:142
  54.5 0.1 pad_add_fusion.1
  54.6 0.1 copy.66
  54.8 0.1 sub.39
  54.9 0.6 reduce-window.6
  55.5 0.2 slice_reduce_fusion
  55.8 0.1 reduce_sum.72
  55.9 0.1 gt.16
  56.0 23.8 %all-to-all-done.1 = f32[32,12,512]{2,1,0:T(8,128)S(1)} async-done(((f32[32,12,512]{2,1,0:T(8,128)}), f32[32,12,512]{2,1,0:T(8,128)S(1)}, u32[]{:S(2)}, u32[]{:S(2)}) %all-to-all-start.1) | async-done | bytes 786464 | tf_op jit(solution)/shard_map/all_to_all | solution.py:142
  79.8 0.1 bitcast_reduce_fusion
  79.9 0.1 copy.63
  80.0 0.2 copy.79
  80.2 0.2 fusion.34
  80.4 0.1 fusion.36
  80.6 0.2 fusion.47
  80.8 8.3 %collective-permute-done.3 = bf16[12,4096]{1,0:T(8,128)(2,1)S(1)} collective-permute-done((bf16[12,4096]{1,0:T(8,128)(2,1)S(1)}, bf16[12,4096]{1,0:T(8,128)(2,1)S(1)}, u32[]{:S(2)}, u32[]{:S(2)}) %collective-permute-start.3) | collective-permute-done | bytes 98336 | tf_op jit(solution)/shard_map/ppermute | solution.py:52
  89.1 2.2 convolution_convert_fusion
  91.4 4.3 %reshape.270 = bf16[16,18,4096]{2,1,0:T(8,128)(2,1)} reshape(bf16[288,4096]{1,0:T(8,128)(2,1)} %convolution_convert_fusion) | data formatting | bytes 4718592 | tf_op jit(solution)/shard_map/reshape | solution.py:88
  95.7 41.8 %all_to_all.20 = bf16[16,18,4096]{2,1,0:T(8,128)(2,1)} all-to-all(bf16[16,18,4096]{2,1,0:T(8,128)(2,1)} %reshape.270), channel_id=1, replica_groups=mesh['zh'=2,'dl'=4,'tensor'=4] {'dl','tensor'}, dimensions={0} | all-to-all | bytes 4718592 | tf_op jit(solution)/shard_map/all_to_all | solution.py:89
  137.4 4.3 %reshape.271 = bf16[288,4096]{1,0:T(8,128)(2,1)} reshape(bf16[16,18,4096]{2,1,0:T(8,128)(2,1)} %all_to_all.20) | data formatting | bytes 4718592 | tf_op jit(solution)/shard_map/reshape | solution.py:90
  141.8 5.5 %fusion.4 = f32[288,768]{1,0:T(8,128)S(1)} fusion(bf16[288,4096]{1,0:T(8,128)(2,1)} %reshape.271, bf16[1,4096,768]{2,1,0:T(8,128)(2,1)} %param.25), kind=kOutput, calls=%fused_computation.4 | convolution fusion | flops 1811939328 | bytes 9535488 | tf_op jit(solution)/shard_map/dot_general | solution.py:91
  147.3 11.8 %fusion.6 = bf16[288,4096]{1,0:T(8,128)(2,1)} fusion(bf16[1,768,4096]{2,1,0:T(8,128)(2,1)} %param.27, bf16[288,4096]{1,0:T(8,128)(2,1)} %reshape.271, bf16[1,4096,768]{2,1,0:T(8,128)(2,1)} %param.26, f32[288,768]{1,0:T(8,128)S(1)} %fusion.4), kind=kOutput, calls=%fused_computation.6 | convolution fusion | flops 3626385408 | bytes 18186240 | tf_op jit(solution)/shard_map/dot_general | solution.py:94
  159.1 4.3 %reshape.272 = bf16[16,18,4096]{2,1,0:T(8,128)(2,1)} reshape(bf16[288,4096]{1,0:T(8,128)(2,1)} %fusion.6) | data formatting | bytes 4718592 | tf_op jit(solution)/shard_map/reshape | solution.py:96
  163.4 6.7 %all-to-all-start.3 = ((bf16[16,18,4096]{2,1,0:T(8,128)(2,1)}), bf16[16,18,4096]{2,1,0:T(8,128)(2,1)}, u32[]{:S(2)}, u32[]{:S(2)}) async-start(bf16[16,18,4096]{2,1,0:T(8,128)(2,1)} %reshape.272), calls=%async_computation.3 | async-start | bytes 6291456 | tf_op jit(solution)/shard_map/all_to_all | solution.py:95
  170.1 0.6 collective-permute-start.1
  170.7 37.7 %collective-permute-done.1 = f32[12,8]{0,1:T(8,128)S(1)} collective-permute-done((f32[12,8]{0,1:T(8,128)S(1)}, f32[12,8]{0,1:T(8,128)S(1)}, u32[]{:S(2)}, u32[]{:S(2)}) %collective-permute-start.1) | collective-permute-done | bytes 416 | tf_op jit(solution)/shard_map/ppermute | solution.py:52
  208.5 0.1 copy.64
  208.7 8.5 %all-to-all-done.3 = bf16[16,18,4096]{2,1,0:T(8,128)(2,1)} async-done(((bf16[16,18,4096]{2,1,0:T(8,128)(2,1)}), bf16[16,18,4096]{2,1,0:T(8,128)(2,1)}, u32[]{:S(2)}, u32[]{:S(2)}) %all-to-all-start.3) | async-done | bytes 2359328 | tf_op jit(solution)/shard_map/all_to_all | solution.py:95
  217.2 4.3 %reshape.278 = bf16[288,4096,1]{1,0,2:T(8,128)(2,1)} reshape(bf16[16,18,4096]{2,1,0:T(8,128)(2,1)} %all-to-all-done.3) | data formatting | bytes 4718592 | tf_op jit(solution)/shard_map/reshape | solution.py:98
  221.5 3.1 %multiply_reduce_fusion = f32[24,4096]{1,0:T(8,128)S(1)} fusion(f32[24,8]{1,0:T(8,128)S(1)} %broadcast_select_fusion, bf16[288,4096,1]{1,0,2:T(8,128)(2,1)} %reshape.278, s32[192]{0:T(256)S(1)} %get-tuple-element.4), kind=kOutput, calls=%fused_computation.8 | convolution fusion | flops 454514688 | bytes 2754048 | tf_op jit(solution)/shard_map/sp,sd->pd/dot_general | solution.py:99
  224.7 0.4 collective-permute-start.4
  225.1 14.4 %collective-permute-done.4 = f32[12,4096]{1,0:T(8,128)S(1)} collective-permute-done((f32[12,4096]{1,0:T(8,128)S(1)}, f32[12,4096]{1,0:T(8,128)S(1)}, u32[]{:S(2)}, u32[]{:S(2)}) %collective-permute-start.4) | collective-permute-done | bytes 196640 | tf_op jit(solution)/shard_map/ppermute | solution.py:52
  239.4 0.7 add_convert_fusion
  (39 shorter events, 0.8 us)
Async XLA Ops:
  0.6 43.8 %copy-start = (bf16[2048,512]{1,0:T(8,128)(2,1)S(1)}, bf16[2048,512]{1,0:T(8,128)(2,1)}, u32[]{:S(2)}) copy-start(bf16[2048,512]{1,0:T(8,128)(2,1)} %param.21) | copy-start | bytes 6291460
  0.6 5.6 %copy-start.4 = (bf16[48,128]{1,0:T(8,128)(2,1)S(1)}, bf16[48,128]{1,0:T(8,128)(2,1)}, u32[]{:S(2)}) copy-start(bf16[48,128]{1,0:T(8,128)(2,1)} %param.16) | copy-start | bytes 36868
  0.7 5.6 %copy-start.7 = (bf16[48,128,128]{2,1,0:T(8,128)(2,1)S(1)}, bf16[48,128,128]{2,1,0:T(8,128)(2,1)}, u32[]{:S(2)}) copy-start(bf16[48,128,128]{2,1,0:T(8,128)(2,1)} %param.18) | copy-start | bytes 4718596
  7.0 11.0 %collective-permute-start = (bf16[48,2048]{1,0:T(8,128)(2,1)S(1)}, bf16[48,2048]{1,0:T(8,128)(2,1)S(1)}, u32[]{:S(2)}, u32[]{:S(2)}) collective-permute-start(bf16[48,2048]{1,0:T(8,128)(2,1)S(1)} %bitcast.75), channel_id=1, source_target_pairs={{0,16},{16,0},{1,17},{17,1},{2,18},{18,2},{3,19},{19,3},{4,20},{20... | collective-permute-start | bytes 589832 | tf_op jit(solution)/shard_map/ppermute | solution.py:52
  18.1 5.9 %copy-start.5 = (s32[12,8]{0,1:T(8,128)S(1)}, s32[12,8]{0,1:T(8,128)}, u32[]{:S(2)}) copy-start(s32[12,8]{0,1:T(8,128)} %param.23) | copy-start | bytes 1156
  19.4 22.4 %all-to-all-start = ((bf16[4,96,2048]{2,1,0:T(8,128)(2,1)}), bf16[4,96,2048]{2,1,0:T(8,128)(2,1)}, u32[]{:S(2)}, u32[]{:S(2)}) async-start(bf16[4,96,2048]{2,1,0:T(8,128)(2,1)} %broadcast_in_dim.47), calls=%async_computation | async-start | bytes 3145728 | tf_op jit(solution)/shard_map/all_to_all | solution.py:135
  23.9 30.6 %collective-permute-start.2 = (s32[12,8]{0,1:T(8,128)S(1)}, s32[12,8]{0,1:T(8,128)S(1)}, u32[]{:S(2)}, u32[]{:S(2)}) collective-permute-start(s32[12,8]{0,1:T(8,128)S(1)} %copy-done.5), channel_id=1, source_target_pairs={{0,16},{16,0},{1,17},{17,1},{2,18},{18,2},{3,19},{19,3},{4,20},{20... | collective-permute-start | bytes 1160 | tf_op jit(solution)/shard_map/ppermute | solution.py:52
  46.9 33.3 %copy-start.2 = (bf16[12,4096]{1,0:T(8,128)(2,1)S(1)}, bf16[12,4096]{1,0:T(8,128)(2,1)}, u32[]{:S(2)}) copy-start(bf16[12,4096]{1,0:T(8,128)(2,1)} %param.20) | copy-start | bytes 294916
  46.9 33.5 %copy-start.3 = (f32[4096]{0:T(1024)S(1)}, f32[4096]{0:T(1024)}, u32[]{:S(2)}) copy-start(f32[4096]{0:T(1024)} %param.22) | copy-start | bytes 49156
  46.9 32.9 %all-to-all-start.1 = ((f32[32,12,512]{2,1,0:T(8,128)}), f32[32,12,512]{2,1,0:T(8,128)S(1)}, u32[]{:S(2)}, u32[]{:S(2)}) async-start(f32[32,12,512]{2,1,0:T(8,128)} %bitcast.68), calls=%async_computation.1 | async-start | bytes 2097152 | tf_op jit(solution)/shard_map/all_to_all | solution.py:142
  80.4 15.3 %copy-start.1 = (bf16[12,4096]{1,0:T(8,128)(2,1)}, bf16[12,4096]{1,0:T(8,128)(2,1)S(1)}, u32[]{:S(2)}) copy-start(bf16[12,4096]{1,0:T(8,128)(2,1)S(1)} %get-tuple-element.7) | copy-start | bytes 294916
  80.5 8.6 %collective-permute-start.3 = (bf16[12,4096]{1,0:T(8,128)(2,1)S(1)}, bf16[12,4096]{1,0:T(8,128)(2,1)S(1)}, u32[]{:S(2)}, u32[]{:S(2)}) collective-permute-start(bf16[12,4096]{1,0:T(8,128)(2,1)S(1)} %fusion.36), channel_id=1, source_target_pairs={{0,16},{16,0},{1,17},{17,1},{2,18},{18,2},{3,19},{19,3},{4,20},{20... | collective-permute-start | bytes 294920 | tf_op jit(solution)/shard_map/ppermute | solution.py:52
  163.4 6.7 %copy-start.6 = (f32[12,8]{0,1:T(8,128)S(1)}, f32[12,8]{0,1:T(8,128)}, u32[]{:S(2)}) copy-start(f32[12,8]{0,1:T(8,128)} %param.24) | copy-start | bytes 1156
  163.4 53.8 %all-to-all-start.3 = ((bf16[16,18,4096]{2,1,0:T(8,128)(2,1)}), bf16[16,18,4096]{2,1,0:T(8,128)(2,1)}, u32[]{:S(2)}, u32[]{:S(2)}) async-start(bf16[16,18,4096]{2,1,0:T(8,128)(2,1)} %reshape.272), calls=%async_computation.3 | async-start | bytes 6291456 | tf_op jit(solution)/shard_map/all_to_all | solution.py:95
  170.1 38.3 %collective-permute-start.1 = (f32[12,8]{0,1:T(8,128)S(1)}, f32[12,8]{0,1:T(8,128)S(1)}, u32[]{:S(2)}, u32[]{:S(2)}) collective-permute-start(f32[12,8]{0,1:T(8,128)S(1)} %copy-done.6), channel_id=1, source_target_pairs={{0,16},{16,0},{1,17},{17,1},{2,18},{18,2},{3,19},{19,3},{4,20},{20... | collective-permute-start | bytes 1160 | tf_op jit(solution)/shard_map/ppermute | solution.py:52
  224.7 14.8 %collective-permute-start.4 = (f32[12,4096]{1,0:T(8,128)S(1)}, f32[12,4096]{1,0:T(8,128)S(1)}, u32[]{:S(2)}, u32[]{:S(2)}) collective-permute-start(f32[12,4096]{1,0:T(8,128)S(1)} %slice_select_fusion), channel_id=1, source_target_pairs={{0,16},{16,0},{1,17},{17,1},{2,18},{18,2},{3,19},{19,3},{4,20},{20... | collective-permute-start | bytes 589832 | tf_op jit(solution)/shard_map/ppermute | solution.py:52

commit v3 on v2

--- a/solution.py
+++ b/solution.py
@@ -83,20 +83,24 @@
     placement = (
         jnp.arange(n_half * capacity, dtype=jnp.int32)[:, None] == target[None, :]
     ).astype(jnp.bfloat16)
-    token_place = jnp.sum(placement.reshape(n_half * capacity, held, chosen_count), axis=2)
-    outgoing = jnp.dot(token_place, rows, preferred_element_type=jnp.float32).astype(jnp.bfloat16)
-    outgoing = outgoing.reshape(n_half, capacity, width)
+    token_place = jnp.sum(placement.reshape(n_half, capacity, held, chosen_count), axis=3)
+    outgoing = jnp.einsum(
+        "hcp,pd->hcd", token_place, rows, preferred_element_type=jnp.float32
+    ).astype(jnp.bfloat16)
     received = lax.all_to_all(outgoing, HALF, split_axis=0, concat_axis=0, tiled=True)
-    flat_rows = received.reshape(-1, width)
-    gate_part = jnp.dot(flat_rows, w_gate[0], preferred_element_type=jnp.float32)
-    up_part = jnp.dot(flat_rows, w_up[0], preferred_element_type=jnp.float32)
+    gate_part = jnp.einsum("hcd,df->hcf", received, w_gate[0], preferred_element_type=jnp.float32)
+    up_part = jnp.einsum("hcd,df->hcf", received, w_up[0], preferred_element_type=jnp.float32)
     activation = (jax.nn.silu(gate_part) * up_part).astype(jnp.bfloat16)
-    result = jnp.dot(activation, w_down[0], preferred_element_type=jnp.float32).astype(jnp.bfloat16)
-    returned = lax.all_to_all(
-        result.reshape(received.shape), HALF, split_axis=0, concat_axis=0, tiled=True
+    result = jnp.einsum(
+        "hcf,fd->hcd", activation, w_down[0], preferred_element_type=jnp.float32
+    ).astype(jnp.bfloat16)
+    returned = lax.all_to_all(result, HALF, split_axis=0, concat_axis=0, tiled=True)
+    pair_rows = jnp.einsum(
+        "hcp,hcd->pd",
+        placement.reshape(n_half, capacity, pair_count),
+        returned,
+        preferred_element_type=jnp.float32,
     )
-    returned = returned.reshape(n_half * capacity, width)
-    pair_rows = jnp.einsum("sp,sd->pd", placement, returned, preferred_element_type=jnp.float32)
     weighted = weights[..., None] * pair_rows.reshape(held, chosen_count, width)
     partial = jnp.sum(weighted, axis=1)
     mine = jnp.where(first, partial[:tok_here], partial[tok_here:])

time: 241 us -> 224 us (0.929)
  local copies, waits for them, and re-layouts: 24.6 us -> 9.02 us
    reshape x4 -> x0, local copies, waits for them, and re-layouts: 17.3 us -> none  [the longest x1 4.35 us: expert_layer(): result.reshape(received.shape)]
where the time goes in v3:
time: 224 us
  waiting for transfers between devices  115 us (51%)
  blocking collectives  40.6 us (18%)
  matrix products  28.3 us (13%)
  starting transfers between devices  26.5 us (12%)
  local copies, waits for them, and re-layouts  9.02 us (4%)
  other arithmetic  3.91 us (2%)
    ppermute x5, waiting for transfers between devices, swap_halves(): return lax.ppermute(x, 'zh', [(0, 1), (1, 0)])  66.9 us
    all_to_all x1, blocking collectives, expert_layer(): lax.all_to_all(outgoing, HALF, split_axis=0, concat_axis=0, tiled=True)  40.6 us
    all_to_all x1, waiting for transfers between devices, shards(): lax.all_to_all(by_dest, DP + ('tensor',), split_axis=0, concat_axis=0, ti...  23.7 us
    all_to_all x1, waiting for transfers between devices, shards(): lax.all_to_all(spread, 'dl', split_axis=0, concat_axis=0, tiled=True)  15.5 us
    dot_general x1, matrix products, expert_layer(): jnp.einsum('hcf,fd->hcd', activation, w_down[0], preferred_element_type=j...  14.3 us
    all_to_all x1, waiting for transfers between devices, expert_layer(): lax.all_to_all(result, HALF, split_axis=0, concat_axis=0, tiled=True)  8.49 us
    all_to_all x1, starting transfers between devices, shards(): lax.all_to_all(by_dest, DP + ('tensor',), split_axis=0, concat_axis=0, ti...  7.66 us
    ppermute x5, starting transfers between devices, swap_halves(): return lax.ppermute(x, 'zh', [(0, 1), (1, 0)])  7.6 us
  transfers between devices with their start and end apart: 8, of which 7 were waited for; matrix products, arithmetic and copies ran while one was open for 3% of the time, Pallas kernels for 0%

profile of v3, /device:TPU:7, one launch (start us, length us, event | category | flops | bytes accessed | tf_op | source)
XLA Modules:
  0.0 223.8 jit_solution(4167706863716373870)
XLA Ops:
  0.7 0.9 iota_compare_fusion
  1.5 1.0 copy.80
  2.6 0.9 fusion.49
  3.5 2.4 %select_reduce_fusion = (f32[48,16]{1,0:T(8,128)S(1)}, f32[48,16,128]{2,1,0:T(8,128)S(1)}) fusion(pred[48,128]{1,0:T(8,128)(4,1)S(1)} %iota_compare_fusion, bf16[48,16,128]{2,1,0:T(8,128)(2,1)S(1)} %bitcast.91, bf16[48,128,128]{2,1,0:T(8,128)(2,1)} %param.17), kind=kOutput, calls=%fused_computation.29 | convolution fusion | flops 25459968 | bytes 2171904 | tf_op jit(solution)/shard_map/rkgd,rckd->rkgc/dot_general | solution.py:27
  5.9 0.3 fusion.33
  6.3 0.6 fusion.25
  7.0 2.4 %collective-permute-start = (bf16[48,2048]{1,0:T(8,128)(2,1)S(1)}, bf16[48,2048]{1,0:T(8,128)(2,1)S(1)}, u32[]{:S(2)}, u32[]{:S(2)}) collective-permute-start(bf16[48,2048]{1,0:T(8,128)(2,1)S(1)} %bitcast.92), channel_id=1, source_target_pairs={{0,16},{16,0},{1,17},{17,1},{2,18},{18,2},{3,19},{19,3},{4,20},{20... | collective-permute-start | bytes 589832 | tf_op jit(solution)/shard_map/ppermute | solution.py:52
  9.4 8.6 %collective-permute-done = bf16[48,2048]{1,0:T(8,128)(2,1)S(1)} collective-permute-done((bf16[48,2048]{1,0:T(8,128)(2,1)S(1)}, bf16[48,2048]{1,0:T(8,128)(2,1)S(1)}, u32[]{:S(2)}, u32[]{:S(2)}) %collective-permute-start) | collective-permute-done | bytes 196640 | tf_op jit(solution)/shard_map/ppermute | solution.py:52
  18.1 1.3 broadcast_in_dim.27
  19.4 4.5 %all-to-all-start = ((bf16[4,96,2048]{2,1,0:T(8,128)(2,1)}), bf16[4,96,2048]{2,1,0:T(8,128)(2,1)}, u32[]{:S(2)}, u32[]{:S(2)}) async-start(bf16[4,96,2048]{2,1,0:T(8,128)(2,1)} %broadcast_in_dim.27), calls=%async_computation | async-start | bytes 3145728 | tf_op jit(solution)/shard_map/all_to_all | solution.py:139
  23.9 2.4 %collective-permute-start.2 = (s32[12,8]{0,1:T(8,128)S(1)}, s32[12,8]{0,1:T(8,128)S(1)}, u32[]{:S(2)}, u32[]{:S(2)}) collective-permute-start(s32[12,8]{0,1:T(8,128)S(1)} %copy-done.6), channel_id=1, source_target_pairs={{0,16},{16,0},{1,17},{17,1},{2,18},{18,2},{3,19},{19,3},{4,20},{20... | collective-permute-start | bytes 1160 | tf_op jit(solution)/shard_map/ppermute | solution.py:52
  26.4 15.5 %all-to-all-done = bf16[4,96,2048]{2,1,0:T(8,128)(2,1)} async-done(((bf16[4,96,2048]{2,1,0:T(8,128)(2,1)}), bf16[4,96,2048]{2,1,0:T(8,128)(2,1)}, u32[]{:S(2)}, u32[]{:S(2)}) %all-to-all-start) | async-done | bytes 1572896 | tf_op jit(solution)/shard_map/all_to_all | solution.py:139
  41.8 2.6 %copy.60 = bf16[4,96,2048]{2,0,1:T(4,128)(2,1)S(1)} copy(bf16[4,96,2048]{2,1,0:T(8,128)(2,1)} %all-to-all-done) | data formatting | bytes 3145728 | tf_op jit(solution)/shard_map/all_to_all | solution.py:139
  44.5 1.3 fusion.17
  45.8 1.1 copy.76
  46.9 7.7 %all-to-all-start.1 = ((f32[32,12,512]{2,1,0:T(8,128)}), f32[32,12,512]{2,1,0:T(8,128)S(1)}, u32[]{:S(2)}, u32[]{:S(2)}) async-start(f32[32,12,512]{2,1,0:T(8,128)} %bitcast.85), calls=%async_computation.1 | async-start | bytes 2097152 | tf_op jit(solution)/shard_map/all_to_all | solution.py:146
  54.6 0.1 pad_add_fusion.1
  54.6 0.1 copy.67
  54.7 0.1 copy.68
  54.8 0.1 sub.40
  54.9 0.6 reduce-window.6
  55.5 0.2 slice_reduce_fusion
  55.7 0.1 bitcast_bitcast_fusion
  55.8 0.1 reduce_sum.72
  55.9 0.1 gt.17
  56.1 23.7 %all-to-all-done.1 = f32[32,12,512]{2,1,0:T(8,128)S(1)} async-done(((f32[32,12,512]{2,1,0:T(8,128)}), f32[32,12,512]{2,1,0:T(8,128)S(1)}, u32[]{:S(2)}, u32[]{:S(2)}) %all-to-all-start.1) | async-done | bytes 786464 | tf_op jit(solution)/shard_map/all_to_all | solution.py:146
  79.8 0.1 bitcast_reduce_fusion
  79.9 0.1 copy.64
  80.0 0.2 copy.82
  80.2 0.2 fusion.34
  80.4 0.1 fusion.36
  80.6 0.6 fusion.32
  81.2 7.9 %collective-permute-done.3 = bf16[12,4096]{1,0:T(8,128)(2,1)S(1)} collective-permute-done((bf16[12,4096]{1,0:T(8,128)(2,1)S(1)}, bf16[12,4096]{1,0:T(8,128)(2,1)S(1)}, u32[]{:S(2)}, u32[]{:S(2)}) %collective-permute-start.3) | collective-permute-done | bytes 98336 | tf_op jit(solution)/shard_map/ppermute | solution.py:52
  89.1 1.0 convolution_convert_fusion
  90.1 40.6 %all_to_all.20 = bf16[16,18,4096]{2,1,0:T(8,128)(2,1)S(1)} all-to-all(bf16[16,18,4096]{2,1,0:T(8,128)(2,1)S(1)} %convolution_convert_fusion), channel_id=1, replica_groups=mesh['zh'=2,'dl'=4,'tensor'=4] {'dl','tensor'}, dimensions={0} | all-to-all | bytes 4718592 | tf_op jit(solution)/shard_map/all_to_all | solution.py:90
  130.7 1.7 copy-done.1
  132.4 3.8 %fusion.4 = f32[16,18,768]{2,1,0:T(8,128)} fusion(bf16[16,18,4096]{2,1,0:T(8,128)(2,1)S(1)} %all_to_all.20, bf16[1,4096,768]{2,1,0:T(8,128)(2,1)S(1)} %bitcast.99), kind=kOutput, calls=%fused_computation.4 | convolution fusion | flops 1811939328 | bytes 9535488 | tf_op jit(solution)/shard_map/hcd,df->hcf/dot_general | solution.py:91
  136.2 14.3 %fusion.6 = bf16[16,18,4096]{2,1,0:T(8,128)(2,1)} fusion(bf16[1,768,4096]{2,1,0:T(8,128)(2,1)} %param.27, bf16[16,18,4096]{2,1,0:T(8,128)(2,1)} %copy-done.1, bf16[1,4096,768]{2,1,0:T(8,128)(2,1)} %param.26, f32[16,18,768]{2,1,0:T(8,128)} %fusion.4), kind=kOutput, calls=%fused_computation.7 | convolution fusion | flops 3626385408 | bytes 18186240 | tf_op jit(solution)/shard_map/hcf,fd->hcd/dot_general | solution.py:94
  150.5 6.7 %all-to-all-start.3 = ((bf16[16,18,4096]{2,1,0:T(8,128)(2,1)}), bf16[16,18,4096]{2,1,0:T(8,128)(2,1)}, u32[]{:S(2)}, u32[]{:S(2)}) async-start(bf16[16,18,4096]{2,1,0:T(8,128)(2,1)} %fusion.6), calls=%async_computation.3 | async-start | bytes 6291456 | tf_op jit(solution)/shard_map/all_to_all | solution.py:97
  157.2 1.4 collective-permute-start.1
  158.6 36.9 %collective-permute-done.1 = f32[12,8]{0,1:T(8,128)S(1)} collective-permute-done((f32[12,8]{0,1:T(8,128)S(1)}, f32[12,8]{0,1:T(8,128)S(1)}, u32[]{:S(2)}, u32[]{:S(2)}) %collective-permute-start.1) | collective-permute-done | bytes 416 | tf_op jit(solution)/shard_map/ppermute | solution.py:52
  195.5 0.1 pad_maximum_fusion.1
  195.6 0.1 copy.65
  195.7 8.5 %all-to-all-done.3 = bf16[16,18,4096]{2,1,0:T(8,128)(2,1)} async-done(((bf16[16,18,4096]{2,1,0:T(8,128)(2,1)}), bf16[16,18,4096]{2,1,0:T(8,128)(2,1)}, u32[]{:S(2)}, u32[]{:S(2)}) %all-to-all-start.3) | async-done | bytes 2359328 | tf_op jit(solution)/shard_map/all_to_all | solution.py:97
  204.2 4.0 %multiply_reduce_fusion = f32[24,4096]{1,0:T(8,128)S(1)} fusion(f32[24,8]{1,0:T(8,128)S(1)} %broadcast_select_fusion, bf16[16,18,4096]{2,1,0:T(8,128)(2,1)} %all-to-all-done.3, s32[24,8]{1,0:T(8,128)S(1)} %add_select_fusion, s32[18,16]{0,1:T(8,128)S(1)} %multiply_add_fusion.1), kind=kOutput, calls=%fused_computation.10 | convolution fusion | flops 454514688 | bytes 2755200 | tf_op jit(solution)/shard_map/hcp,hcd->pd/dot_general | solution.py:98
  208.3 1.3 collective-permute-start.4
  209.6 13.5 %collective-permute-done.4 = f32[12,4096]{1,0:T(8,128)S(1)} collective-permute-done((f32[12,4096]{1,0:T(8,128)S(1)}, f32[12,4096]{1,0:T(8,128)S(1)}, u32[]{:S(2)}, u32[]{:S(2)}) %collective-permute-start.4) | collective-permute-done | bytes 196640 | tf_op jit(solution)/shard_map/ppermute | solution.py:52
  223.1 0.7 add_convert_fusion
  (45 shorter events, 0.6 us)
Async XLA Ops:
  0.6 43.8 %copy-start = (bf16[2048,512]{1,0:T(8,128)(2,1)S(1)}, bf16[2048,512]{1,0:T(8,128)(2,1)}, u32[]{:S(2)}) copy-start(bf16[2048,512]{1,0:T(8,128)(2,1)} %param.21) | copy-start | bytes 6291460
  0.6 5.6 %copy-start.5 = (bf16[48,128]{1,0:T(8,128)(2,1)S(1)}, bf16[48,128]{1,0:T(8,128)(2,1)}, u32[]{:S(2)}) copy-start(bf16[48,128]{1,0:T(8,128)(2,1)} %param.16) | copy-start | bytes 36868
  0.7 5.6 %copy-start.8 = (bf16[48,128,128]{2,1,0:T(8,128)(2,1)S(1)}, bf16[48,128,128]{2,1,0:T(8,128)(2,1)}, u32[]{:S(2)}) copy-start(bf16[48,128,128]{2,1,0:T(8,128)(2,1)} %param.18) | copy-start | bytes 4718596
  7.0 11.0 %collective-permute-start = (bf16[48,2048]{1,0:T(8,128)(2,1)S(1)}, bf16[48,2048]{1,0:T(8,128)(2,1)S(1)}, u32[]{:S(2)}, u32[]{:S(2)}) collective-permute-start(bf16[48,2048]{1,0:T(8,128)(2,1)S(1)} %bitcast.92), channel_id=1, source_target_pairs={{0,16},{16,0},{1,17},{17,1},{2,18},{18,2},{3,19},{19,3},{4,20},{20... | collective-permute-start | bytes 589832 | tf_op jit(solution)/shard_map/ppermute | solution.py:52
  18.1 5.9 %copy-start.6 = (s32[12,8]{0,1:T(8,128)S(1)}, s32[12,8]{0,1:T(8,128)}, u32[]{:S(2)}) copy-start(s32[12,8]{0,1:T(8,128)} %param.23) | copy-start | bytes 1156
  19.4 22.4 %all-to-all-start = ((bf16[4,96,2048]{2,1,0:T(8,128)(2,1)}), bf16[4,96,2048]{2,1,0:T(8,128)(2,1)}, u32[]{:S(2)}, u32[]{:S(2)}) async-start(bf16[4,96,2048]{2,1,0:T(8,128)(2,1)} %broadcast_in_dim.27), calls=%async_computation | async-start | bytes 3145728 | tf_op jit(solution)/shard_map/all_to_all | solution.py:139
  23.9 30.6 %collective-permute-start.2 = (s32[12,8]{0,1:T(8,128)S(1)}, s32[12,8]{0,1:T(8,128)S(1)}, u32[]{:S(2)}, u32[]{:S(2)}) collective-permute-start(s32[12,8]{0,1:T(8,128)S(1)} %copy-done.6), channel_id=1, source_target_pairs={{0,16},{16,0},{1,17},{17,1},{2,18},{18,2},{3,19},{19,3},{4,20},{20... | collective-permute-start | bytes 1160 | tf_op jit(solution)/shard_map/ppermute | solution.py:52
  46.9 33.3 %copy-start.3 = (bf16[12,4096]{1,0:T(8,128)(2,1)S(1)}, bf16[12,4096]{1,0:T(8,128)(2,1)}, u32[]{:S(2)}) copy-start(bf16[12,4096]{1,0:T(8,128)(2,1)} %param.20) | copy-start | bytes 294916
  46.9 32.9 %all-to-all-start.1 = ((f32[32,12,512]{2,1,0:T(8,128)}), f32[32,12,512]{2,1,0:T(8,128)S(1)}, u32[]{:S(2)}, u32[]{:S(2)}) async-start(f32[32,12,512]{2,1,0:T(8,128)} %bitcast.85), calls=%async_computation.1 | async-start | bytes 2097152 | tf_op jit(solution)/shard_map/all_to_all | solution.py:146
  54.5 25.9 %copy-start.4 = (f32[4096]{0:T(1024)S(1)}, f32[4096]{0:T(1024)}, u32[]{:S(2)}) copy-start(f32[4096]{0:T(1024)} %param.22) | copy-start | bytes 49156
  79.8 52.7 %slice-start = ((s8[6291456]{0:T(1024)(128)(4,1)}), s8[4194304]{0:T(1024)(128)(4,1)S(1)}, s32[]{:S(2)}) async-start(s8[6291456]{0:T(1024)(128)(4,1)} %bitcast.98), calls=%async_computation.4 | async-start | bytes 8388608
  80.4 50.4 %copy-start.2 = (bf16[12,4096]{1,0:T(8,128)(2,1)}, bf16[12,4096]{1,0:T(8,128)(2,1)S(1)}, u32[]{:S(2)}) copy-start(bf16[12,4096]{1,0:T(8,128)(2,1)S(1)} %get-tuple-element.5) | copy-start | bytes 294916
  80.5 8.6 %collective-permute-start.3 = (bf16[12,4096]{1,0:T(8,128)(2,1)S(1)}, bf16[12,4096]{1,0:T(8,128)(2,1)S(1)}, u32[]{:S(2)}, u32[]{:S(2)}) collective-permute-start(bf16[12,4096]{1,0:T(8,128)(2,1)S(1)} %fusion.36), channel_id=1, source_target_pairs={{0,16},{16,0},{1,17},{17,1},{2,18},{18,2},{3,19},{19,3},{4,20},{20... | collective-permute-start | bytes 294920 | tf_op jit(solution)/shard_map/ppermute | solution.py:52
  81.2 51.3 %slice-start.1 = ((s8[6291456]{0:T(1024)(128)(4,1)}), s8[2097152]{0:T(1024)(128)(4,1)S(1)}, s32[]{:S(2)}) async-start(s8[6291456]{0:T(1024)(128)(4,1)} %bitcast.98), calls=%async_computation.5 | async-start | bytes 4194304
  130.7 1.7 copy-start.1
  150.5 6.7 %copy-start.7 = (f32[12,8]{0,1:T(8,128)S(1)}, f32[12,8]{0,1:T(8,128)}, u32[]{:S(2)}) copy-start(f32[12,8]{0,1:T(8,128)} %param.24) | copy-start | bytes 1156
  150.5 53.7 %all-to-all-start.3 = ((bf16[16,18,4096]{2,1,0:T(8,128)(2,1)}), bf16[16,18,4096]{2,1,0:T(8,128)(2,1)}, u32[]{:S(2)}, u32[]{:S(2)}) async-start(bf16[16,18,4096]{2,1,0:T(8,128)(2,1)} %fusion.6), calls=%async_computation.3 | async-start | bytes 6291456 | tf_op jit(solution)/shard_map/all_to_all | solution.py:97
  157.2 38.3 %collective-permute-start.1 = (f32[12,8]{0,1:T(8,128)S(1)}, f32[12,8]{0,1:T(8,128)S(1)}, u32[]{:S(2)}, u32[]{:S(2)}) collective-permute-start(f32[12,8]{0,1:T(8,128)S(1)} %copy-done.7), channel_id=1, source_target_pairs={{0,16},{16,0},{1,17},{17,1},{2,18},{18,2},{3,19},{19,3},{4,20},{20... | collective-permute-start | bytes 1160 | tf_op jit(solution)/shard_map/ppermute | solution.py:52
  208.3 14.8 %collective-permute-start.4 = (f32[12,4096]{1,0:T(8,128)S(1)}, f32[12,4096]{1,0:T(8,128)S(1)}, u32[]{:S(2)}, u32[]{:S(2)}) collective-permute-start(f32[12,4096]{1,0:T(8,128)S(1)} %slice_select_fusion), channel_id=1, source_target_pairs={{0,16},{16,0},{1,17},{17,1},{2,18},{18,2},{3,19},{19,3},{4,20},{20... | collective-permute-start | bytes 589832 | tf_op jit(solution)/shard_map/ppermute | solution.py:52

commit v4 on v3

--- a/solution.py
+++ b/solution.py
@@ -105,7 +105,8 @@
     partial = jnp.sum(weighted, axis=1)
     mine = jnp.where(first, partial[:tok_here], partial[tok_here:])
     theirs = jnp.where(first, partial[tok_here:], partial[:tok_here])
-    return (mine + swap_halves(theirs)).astype(jnp.bfloat16)
+    sent = swap_halves(theirs.astype(jnp.bfloat16)).astype(jnp.float32)
+    return (mine + sent).astype(jnp.bfloat16)
 
 
 def shards(
@@ -143,8 +144,11 @@
     col_width = partial_cols.shape[-1]
     by_dest = partial_cols.reshape(n_dl, 2, n_t, tok_here, col_width).transpose(1, 0, 2, 3, 4)
     by_dest = by_dest.reshape(2 * n_dl * n_t, tok_here, col_width)
-    arrived = lax.all_to_all(by_dest, DP + ("tensor",), split_axis=0, concat_axis=0, tiled=True)
-    summed = jnp.sum(arrived.reshape(2 * n_dl, n_t, tok_here, col_width), axis=1)
+    arrived = lax.all_to_all(
+        by_dest.astype(jnp.bfloat16), DP + ("tensor",), split_axis=0, concat_axis=0, tiled=True
+    )
+    arrived = arrived.astype(jnp.float32).reshape(2 * n_dl, n_t, tok_here, col_width)
+    summed = jnp.sum(arrived, axis=1)
     summed = summed.transpose(1, 0, 2).reshape(tok_here, 2 * n_dl * col_width)
     attended = (hidden_in.astype(jnp.float32) + summed).astype(jnp.bfloat16)
     widened = attended.astype(jnp.float32)

time: 224 us -> 208 us (0.929)
  waiting for transfers between devices: 115 us -> 99 us
    all_to_all x1, waiting for transfers between devices: 15.5 us -> 0.96 us  [shards(): lax.all_to_all(spread, 'dl', split_axis=0, concat_axis=0, tiled=True)]
    all_to_all x1, waiting for transfers between devices: 23.7 us -> 13.8 us  [shards(): lax.all_to_all(by_dest.astype(jnp.bfloat16), DP + ('tensor',), split_axis...]
    ppermute x5, waiting for transfers between devices: 66.9 us -> 75.7 us  [swap_halves(): return lax.ppermute(x, 'zh', [(0, 1), (1, 0)])]
  transfers between devices with their start and end apart: 8 -> 8, of which waited for: 7 -> 8; matrix products, arithmetic and copies ran while one was open for 3% -> 1% of each run, Pallas kernels for 0% -> 0%
where the time goes in v4:
time: 208 us; the launch traced here: 207 us
  waiting for transfers between devices  99 us (48%)
  blocking collectives  40.8 us (20%)
  matrix products  26.9 us (13%)
  starting transfers between devices  26.8 us (13%)
  local copies, waits for them, and re-layouts  8.73 us (4%)
  other arithmetic  3.91 us (2%)
    ppermute x5, waiting for transfers between devices, swap_halves(): return lax.ppermute(x, 'zh', [(0, 1), (1, 0)])  75.7 us
    all_to_all x1, blocking collectives, expert_layer(): lax.all_to_all(outgoing, HALF, split_axis=0, concat_axis=0, tiled=True)  40.8 us
    dot_general x1, matrix products, expert_layer(): jnp.einsum('hcf,fd->hcd', activation, w_down[0], preferred_element_type=j...  14 us
    all_to_all x1, waiting for transfers between devices, shards(): lax.all_to_all(by_dest.astype(jnp.bfloat16), DP + ('tensor',), split_axis...  13.8 us
    all_to_all x1, starting transfers between devices, shards(): lax.all_to_all(by_dest.astype(jnp.bfloat16), DP + ('tensor',), split_axis...  8.77 us
    all_to_all x1, waiting for transfers between devices, expert_layer(): lax.all_to_all(result, HALF, split_axis=0, concat_axis=0, tiled=True)  8.49 us
    ppermute x5, starting transfers between devices, swap_halves(): return lax.ppermute(x, 'zh', [(0, 1), (1, 0)])  6.74 us
    all_to_all x1, starting transfers between devices, expert_layer(): lax.all_to_all(result, HALF, split_axis=0, concat_axis=0, tiled=True)  6.74 us
  transfers between devices with their start and end apart: 8, of which 8 were waited for; matrix products, arithmetic and copies ran while one was open for 1% of the time, Pallas kernels for 0%

profile of v4, /device:TPU:7, one launch (start us, length us, event | category | flops | bytes accessed | tf_op | source)
XLA Modules:
  0.0 207.0 jit_solution(2157611543230404855)
XLA Ops:
  0.7 0.9 iota_compare_fusion
  1.5 1.0 copy.80
  2.6 0.9 fusion.54
  3.5 2.4 %select_reduce_fusion = (f32[48,16]{1,0:T(8,128)S(1)}, f32[48,16,128]{2,1,0:T(8,128)S(1)}) fusion(pred[48,128]{1,0:T(8,128)(4,1)S(1)} %iota_compare_fusion, bf16[48,16,128]{2,1,0:T(8,128)(2,1)S(1)} %bitcast.93, bf16[48,128,128]{2,1,0:T(8,128)(2,1)} %param.17), kind=kOutput, calls=%fused_computation.30 | convolution fusion | flops 25459968 | bytes 2171904 | tf_op jit(solution)/shard_map/rkgd,rckd->rkgc/dot_general | solution.py:27
  5.9 0.3 fusion.38
  6.3 0.6 fusion.30
  7.0 2.4 %collective-permute-start = (bf16[48,2048]{1,0:T(8,128)(2,1)S(1)}, bf16[48,2048]{1,0:T(8,128)(2,1)S(1)}, u32[]{:S(2)}, u32[]{:S(2)}) collective-permute-start(bf16[48,2048]{1,0:T(8,128)(2,1)S(1)} %bitcast.94), channel_id=1, source_target_pairs={{0,16},{16,0},{1,17},{17,1},{2,18},{18,2},{3,19},{19,3},{4,20},{20... | collective-permute-start | bytes 589832 | tf_op jit(solution)/shard_map/ppermute | solution.py:52
  9.4 8.6 %collective-permute-done = bf16[48,2048]{1,0:T(8,128)(2,1)S(1)} collective-permute-done((bf16[48,2048]{1,0:T(8,128)(2,1)S(1)}, bf16[48,2048]{1,0:T(8,128)(2,1)S(1)}, u32[]{:S(2)}, u32[]{:S(2)}) %collective-permute-start) | collective-permute-done | bytes 196640 | tf_op jit(solution)/shard_map/ppermute | solution.py:52
  18.1 1.3 broadcast_in_dim.27
  19.4 4.5 %all-to-all-start = ((bf16[4,96,2048]{2,1,0:T(8,128)(2,1)}), bf16[4,96,2048]{2,1,0:T(8,128)(2,1)}, u32[]{:S(2)}, u32[]{:S(2)}) async-start(bf16[4,96,2048]{2,1,0:T(8,128)(2,1)} %broadcast_in_dim.27), calls=%async_computation | async-start | bytes 3145728 | tf_op jit(solution)/shard_map/all_to_all | solution.py:140
  23.9 2.4 %collective-permute-start.2 = (s32[12,8]{0,1:T(8,128)S(1)}, s32[12,8]{0,1:T(8,128)S(1)}, u32[]{:S(2)}, u32[]{:S(2)}) collective-permute-start(s32[12,8]{0,1:T(8,128)S(1)} %copy-done.6), channel_id=1, source_target_pairs={{0,16},{16,0},{1,17},{17,1},{2,18},{18,2},{3,19},{19,3},{4,20},{20... | collective-permute-start | bytes 1160 | tf_op jit(solution)/shard_map/ppermute | solution.py:52
  26.4 13.3 %collective-permute-done.2 = s32[12,8]{0,1:T(8,128)S(1)} collective-permute-done((s32[12,8]{0,1:T(8,128)S(1)}, s32[12,8]{0,1:T(8,128)S(1)}, u32[]{:S(2)}, u32[]{:S(2)}) %collective-permute-start.2) | collective-permute-done | bytes 416 | tf_op jit(solution)/shard_map/ppermute | solution.py:52
  39.7 0.1 pad_add_fusion.1
  39.8 0.1 copy.67
  39.9 0.1 copy.68
  40.0 0.1 sub.40
  40.1 0.6 reduce-window.6
  40.7 0.2 slice_reduce_fusion
  40.9 1.0 all-to-all-done
  41.8 2.6 %copy.60 = bf16[4,96,2048]{2,0,1:T(4,128)(2,1)S(1)} copy(bf16[4,96,2048]{2,1,0:T(8,128)(2,1)} %all-to-all-done) | data formatting | bytes 3145728 | tf_op jit(solution)/shard_map/all_to_all | solution.py:140
  44.5 1.3 fusion.25
  45.8 0.8 copy.76
  46.6 8.8 %all-to-all-start.1 = ((bf16[32,12,512]{2,1,0:T(8,128)(2,1)}), bf16[32,12,512]{2,1,0:T(8,128)(2,1)S(1)}, u32[]{:S(2)}, u32[]{:S(2)}) async-start(bf16[32,12,512]{2,1,0:T(8,128)(2,1)} %bitcast.7), calls=%async_computation.1 | async-start | bytes 1048576 | tf_op jit(solution)/shard_map/all_to_all | solution.py:147
  55.5 0.1 reduce_sum.72
  55.6 0.1 gt.17
  55.8 13.8 %all-to-all-done.1 = bf16[32,12,512]{2,1,0:T(8,128)(2,1)S(1)} async-done(((bf16[32,12,512]{2,1,0:T(8,128)(2,1)}), bf16[32,12,512]{2,1,0:T(8,128)(2,1)S(1)}, u32[]{:S(2)}, u32[]{:S(2)}) %all-to-all-start.1) | async-done | bytes 393248 | tf_op jit(solution)/shard_map/all_to_all | solution.py:147
  69.6 0.1 convert_reduce_fusion
  69.7 0.1 copy.64
  69.8 0.2 copy.82
  70.0 0.2 fusion.39
  70.2 0.1 fusion.41
  70.4 0.6 fusion.37
  71.0 8.2 %collective-permute-done.3 = bf16[12,4096]{1,0:T(8,128)(2,1)S(1)} collective-permute-done((bf16[12,4096]{1,0:T(8,128)(2,1)S(1)}, bf16[12,4096]{1,0:T(8,128)(2,1)S(1)}, u32[]{:S(2)}, u32[]{:S(2)}) %collective-permute-start.3) | collective-permute-done | bytes 98336 | tf_op jit(solution)/shard_map/ppermute | solution.py:52
  79.1 1.0 convolution_convert_fusion
  80.1 40.8 %all_to_all.20 = bf16[16,18,4096]{2,1,0:T(8,128)(2,1)S(1)} all-to-all(bf16[16,18,4096]{2,1,0:T(8,128)(2,1)S(1)} %convolution_convert_fusion), channel_id=1, replica_groups=mesh['zh'=2,'dl'=4,'tensor'=4] {'dl','tensor'}, dimensions={0} | all-to-all | bytes 4718592 | tf_op jit(solution)/shard_map/all_to_all | solution.py:90
  120.9 1.7 copy-done.1
  122.6 2.7 %fusion.4 = f32[16,18,768]{2,1,0:T(8,128)S(1)} fusion(bf16[16,18,4096]{2,1,0:T(8,128)(2,1)S(1)} %all_to_all.20, bf16[1,4096,768]{2,1,0:T(8,128)(2,1)S(1)} %bitcast.101), kind=kOutput, calls=%fused_computation.4 | convolution fusion | flops 1811939328 | bytes 9535488 | tf_op jit(solution)/shard_map/hcd,df->hcf/dot_general | solution.py:91
  125.4 14.0 %fusion.6 = bf16[16,18,4096]{2,1,0:T(8,128)(2,1)} fusion(bf16[1,768,4096]{2,1,0:T(8,128)(2,1)} %param.27, bf16[16,18,4096]{2,1,0:T(8,128)(2,1)} %copy-done.1, bf16[1,4096,768]{2,1,0:T(8,128)(2,1)} %param.26, f32[16,18,768]{2,1,0:T(8,128)S(1)} %fusion.4), kind=kOutput, calls=%fused_computation.7 | convolution fusion | flops 3626385408 | bytes 18186240 | tf_op jit(solution)/shard_map/hcf,fd->hcd/dot_general | solution.py:94
  139.3 6.7 %all-to-all-start.3 = ((bf16[16,18,4096]{2,1,0:T(8,128)(2,1)}), bf16[16,18,4096]{2,1,0:T(8,128)(2,1)}, u32[]{:S(2)}, u32[]{:S(2)}) async-start(bf16[16,18,4096]{2,1,0:T(8,128)(2,1)} %fusion.6), calls=%async_computation.3 | async-start | bytes 6291456 | tf_op jit(solution)/shard_map/all_to_all | solution.py:97
  146.1 1.0 collective-permute-start.1
  147.1 37.3 %collective-permute-done.1 = f32[12,8]{0,1:T(8,128)S(1)} collective-permute-done((f32[12,8]{0,1:T(8,128)S(1)}, f32[12,8]{0,1:T(8,128)S(1)}, u32[]{:S(2)}, u32[]{:S(2)}) %collective-permute-start.1) | collective-permute-done | bytes 416 | tf_op jit(solution)/shard_map/ppermute | solution.py:52
  184.4 0.1 pad_maximum_fusion.1
  184.4 0.1 copy.65
  184.6 8.5 %all-to-all-done.3 = bf16[16,18,4096]{2,1,0:T(8,128)(2,1)} async-done(((bf16[16,18,4096]{2,1,0:T(8,128)(2,1)}), bf16[16,18,4096]{2,1,0:T(8,128)(2,1)}, u32[]{:S(2)}, u32[]{:S(2)}) %all-to-all-start.3) | async-done | bytes 2359328 | tf_op jit(solution)/shard_map/all_to_all | solution.py:97
  193.1 4.0 %multiply_reduce_fusion = f32[24,4096]{1,0:T(8,128)S(1)} fusion(f32[24,8]{1,0:T(8,128)S(1)} %broadcast_select_fusion, bf16[16,18,4096]{2,1,0:T(8,128)(2,1)} %all-to-all-done.3, s32[24,8]{1,0:T(8,128)S(1)} %add_select_fusion, s32[18,16]{0,1:T(8,128)S(1)} %multiply_add_fusion.1), kind=kOutput, calls=%fused_computation.10 | convolution fusion | flops 454514688 | bytes 2755200 | tf_op jit(solution)/shard_map/hcp,hcd->pd/dot_general | solution.py:98
  197.2 0.9 collective-permute-start.4
  198.0 8.3 %collective-permute-done.4 = bf16[12,4096]{1,0:T(8,128)(2,1)S(1)} collective-permute-done((bf16[12,4096]{1,0:T(8,128)(2,1)S(1)}, bf16[12,4096]{1,0:T(8,128)(2,1)S(1)}, u32[]{:S(2)}, u32[]{:S(2)}) %collective-permute-start.4) | collective-permute-done | bytes 98336 | tf_op jit(solution)/shard_map/ppermute | solution.py:52
  206.3 0.7 add_convert_fusion
  (45 shorter events, 0.7 us)
Async XLA Ops:
  0.6 43.8 %copy-start = (bf16[2048,512]{1,0:T(8,128)(2,1)S(1)}, bf16[2048,512]{1,0:T(8,128)(2,1)}, u32[]{:S(2)}) copy-start(bf16[2048,512]{1,0:T(8,128)(2,1)} %param.21) | copy-start | bytes 6291460
  0.6 5.6 %copy-start.5 = (bf16[48,128]{1,0:T(8,128)(2,1)S(1)}, bf16[48,128]{1,0:T(8,128)(2,1)}, u32[]{:S(2)}) copy-start(bf16[48,128]{1,0:T(8,128)(2,1)} %param.16) | copy-start | bytes 36868
  0.7 5.7 %copy-start.8 = (bf16[48,128,128]{2,1,0:T(8,128)(2,1)S(1)}, bf16[48,128,128]{2,1,0:T(8,128)(2,1)}, u32[]{:S(2)}) copy-start(bf16[48,128,128]{2,1,0:T(8,128)(2,1)} %param.18) | copy-start | bytes 4718596
  7.0 11.0 %collective-permute-start = (bf16[48,2048]{1,0:T(8,128)(2,1)S(1)}, bf16[48,2048]{1,0:T(8,128)(2,1)S(1)}, u32[]{:S(2)}, u32[]{:S(2)}) collective-permute-start(bf16[48,2048]{1,0:T(8,128)(2,1)S(1)} %bitcast.94), channel_id=1, source_target_pairs={{0,16},{16,0},{1,17},{17,1},{2,18},{18,2},{3,19},{19,3},{4,20},{20... | collective-permute-start | bytes 589832 | tf_op jit(solution)/shard_map/ppermute | solution.py:52
  18.1 5.9 %copy-start.6 = (s32[12,8]{0,1:T(8,128)S(1)}, s32[12,8]{0,1:T(8,128)}, u32[]{:S(2)}) copy-start(s32[12,8]{0,1:T(8,128)} %param.23) | copy-start | bytes 1156
  19.4 22.4 %all-to-all-start = ((bf16[4,96,2048]{2,1,0:T(8,128)(2,1)}), bf16[4,96,2048]{2,1,0:T(8,128)(2,1)}, u32[]{:S(2)}, u32[]{:S(2)}) async-start(bf16[4,96,2048]{2,1,0:T(8,128)(2,1)} %broadcast_in_dim.27), calls=%async_computation | async-start | bytes 3145728 | tf_op jit(solution)/shard_map/all_to_all | solution.py:140
  23.9 15.8 %collective-permute-start.2 = (s32[12,8]{0,1:T(8,128)S(1)}, s32[12,8]{0,1:T(8,128)S(1)}, u32[]{:S(2)}, u32[]{:S(2)}) collective-permute-start(s32[12,8]{0,1:T(8,128)S(1)} %copy-done.6), channel_id=1, source_target_pairs={{0,16},{16,0},{1,17},{17,1},{2,18},{18,2},{3,19},{19,3},{4,20},{20... | collective-permute-start | bytes 1160 | tf_op jit(solution)/shard_map/ppermute | solution.py:52
  45.8 24.2 %copy-start.3 = (bf16[12,4096]{1,0:T(8,128)(2,1)S(1)}, bf16[12,4096]{1,0:T(8,128)(2,1)}, u32[]{:S(2)}) copy-start(bf16[12,4096]{1,0:T(8,128)(2,1)} %param.20) | copy-start | bytes 294916
  46.6 23.6 %copy-start.4 = (f32[4096]{0:T(1024)S(1)}, f32[4096]{0:T(1024)}, u32[]{:S(2)}) copy-start(f32[4096]{0:T(1024)} %param.22) | copy-start | bytes 49156
  46.6 23.0 %all-to-all-start.1 = ((bf16[32,12,512]{2,1,0:T(8,128)(2,1)}), bf16[32,12,512]{2,1,0:T(8,128)(2,1)S(1)}, u32[]{:S(2)}, u32[]{:S(2)}) async-start(bf16[32,12,512]{2,1,0:T(8,128)(2,1)} %bitcast.7), calls=%async_computation.1 | async-start | bytes 1048576 | tf_op jit(solution)/shard_map/all_to_all | solution.py:147
  69.6 53.0 %slice-start = ((s8[6291456]{0:T(1024)(128)(4,1)}), s8[4194304]{0:T(1024)(128)(4,1)S(1)}, s32[]{:S(2)}) async-start(s8[6291456]{0:T(1024)(128)(4,1)} %bitcast.100), calls=%async_computation.4 | async-start | bytes 8388608
  70.2 50.7 %copy-start.2 = (bf16[12,4096]{1,0:T(8,128)(2,1)}, bf16[12,4096]{1,0:T(8,128)(2,1)S(1)}, u32[]{:S(2)}) copy-start(bf16[12,4096]{1,0:T(8,128)(2,1)S(1)} %get-tuple-element.5) | copy-start | bytes 294916
  70.3 8.8 %collective-permute-start.3 = (bf16[12,4096]{1,0:T(8,128)(2,1)S(1)}, bf16[12,4096]{1,0:T(8,128)(2,1)S(1)}, u32[]{:S(2)}, u32[]{:S(2)}) collective-permute-start(bf16[12,4096]{1,0:T(8,128)(2,1)S(1)} %fusion.41), channel_id=1, source_target_pairs={{0,16},{16,0},{1,17},{17,1},{2,18},{18,2},{3,19},{19,3},{4,20},{20... | collective-permute-start | bytes 294920 | tf_op jit(solution)/shard_map/ppermute | solution.py:52
  71.0 51.7 %slice-start.1 = ((s8[6291456]{0:T(1024)(128)(4,1)}), s8[2097152]{0:T(1024)(128)(4,1)S(1)}, s32[]{:S(2)}) async-start(s8[6291456]{0:T(1024)(128)(4,1)} %bitcast.100), calls=%async_computation.5 | async-start | bytes 4194304
  120.9 1.7 copy-start.1
  139.3 6.7 %copy-start.7 = (f32[12,8]{0,1:T(8,128)S(1)}, f32[12,8]{0,1:T(8,128)}, u32[]{:S(2)}) copy-start(f32[12,8]{0,1:T(8,128)} %param.24) | copy-start | bytes 1156
  139.3 53.8 %all-to-all-start.3 = ((bf16[16,18,4096]{2,1,0:T(8,128)(2,1)}), bf16[16,18,4096]{2,1,0:T(8,128)(2,1)}, u32[]{:S(2)}, u32[]{:S(2)}) async-start(bf16[16,18,4096]{2,1,0:T(8,128)(2,1)} %fusion.6), calls=%async_computation.3 | async-start | bytes 6291456 | tf_op jit(solution)/shard_map/all_to_all | solution.py:97
  146.1 38.3 %collective-permute-start.1 = (f32[12,8]{0,1:T(8,128)S(1)}, f32[12,8]{0,1:T(8,128)S(1)}, u32[]{:S(2)}, u32[]{:S(2)}) collective-permute-start(f32[12,8]{0,1:T(8,128)S(1)} %copy-done.7), channel_id=1, source_target_pairs={{0,16},{16,0},{1,17},{17,1},{2,18},{18,2},{3,19},{19,3},{4,20},{20... | collective-permute-start | bytes 1160 | tf_op jit(solution)/shard_map/ppermute | solution.py:52
  197.2 9.2 %collective-permute-start.4 = (bf16[12,4096]{1,0:T(8,128)(2,1)S(1)}, bf16[12,4096]{1,0:T(8,128)(2,1)S(1)}, u32[]{:S(2)}, u32[]{:S(2)}) collective-permute-start(bf16[12,4096]{1,0:T(8,128)(2,1)S(1)} %select_convert_fusion), channel_id=1, source_target_pairs={{0,16},{16,0},{1,17},{17,1},{2,18},{18,2},{3,19},{19,3},{4,20},{20... | collective-permute-start | bytes 294920 | tf_op jit(solution)/shard_map/ppermute | solution.py:52

commit v5 on v4

--- a/solution.py
+++ b/solution.py
@@ -60,8 +60,9 @@
     capacity = 2 * max(2, 3 * tok_here * chosen_count // experts_all)
     side = lax.axis_index("zh")
     other_rows = swap_halves(normed)
-    other_ids = swap_halves(route_ids)
-    other_weight = swap_halves(route_weight)
+    packed = swap_halves(jnp.concatenate([route_ids.astype(jnp.float32), route_weight], axis=1))
+    other_ids = packed[:, :chosen_count].astype(jnp.int32)
+    other_weight = packed[:, chosen_count:]
     first = side == 0
     rows = jnp.where(first, jnp.concatenate([normed, other_rows]), jnp.concatenate([other_rows, normed]))
     ids = jnp.where(first, jnp.concatenate([route_ids, other_ids]), jnp.concatenate([other_ids, route_ids]))
@@ -138,8 +139,8 @@
     )
     spread = jnp.broadcast_to(pair_heads[None], (n_dl,) + pair_heads.shape)
     gathered = lax.all_to_all(spread, "dl", split_axis=0, concat_axis=0, tiled=True)
-    partial_cols = jnp.dot(
-        gathered.reshape(-1, gathered.shape[-1]), out_weight, preferred_element_type=jnp.float32
+    partial_cols = jnp.einsum(
+        "sqd,df->sqf", gathered, out_weight, preferred_element_type=jnp.float32
     )
     col_width = partial_cols.shape[-1]
     by_dest = partial_cols.reshape(n_dl, 2, n_t, tok_here, col_width).transpose(1, 0, 2, 3, 4)

time: 208 us -> 206 us (level)
  local copies, waits for them, and re-layouts: 8.73 us -> 6.48 us
    all_to_all x1, waiting for transfers between devices: 8.49 us -> 46.6 us  [expert_layer(): lax.all_to_all(result, HALF, split_axis=0, concat_axis=0, tiled=True)]
    ppermute x5 -> x4, waiting for transfers between devices: 75.7 us -> 38.3 us  [swap_halves(): return lax.ppermute(x, 'zh', [(0, 1), (1, 0)])]
    all_to_all x1 -> x0, local copies, waits for them, and re-layouts: 2.62 us -> none  [shards(): lax.all_to_all(spread, 'dl', split_axis=0, concat_axis=0, tiled=True)]
    ppermute x5 -> x4, starting transfers between devices: 6.74 us -> 5.95 us  [swap_halves(): return lax.ppermute(x, 'zh', [(0, 1), (1, 0)])]
  transfers between devices with their start and end apart: 8 -> 7, of which waited for: 8 -> 7; matrix products, arithmetic and copies ran while one was open for 1% -> 1% of each run, Pallas kernels for 0% -> 0%
where the time goes in v5:
time: 206 us
  waiting for transfers between devices  99.7 us (48%)
  blocking collectives  40.8 us (20%)
  matrix products  28 us (14%)
  starting transfers between devices  25.8 us (13%)
  local copies, waits for them, and re-layouts  6.48 us (3%)
  other arithmetic  3.93 us (2%)
    all_to_all x1, waiting for transfers between devices, expert_layer(): lax.all_to_all(result, HALF, split_axis=0, concat_axis=0, tiled=True)  46.6 us
    all_to_all x1, blocking collectives, expert_layer(): lax.all_to_all(outgoing, HALF, split_axis=0, concat_axis=0, tiled=True)  40.8 us
    ppermute x4, waiting for transfers between devices, swap_halves(): return lax.ppermute(x, 'zh', [(0, 1), (1, 0)])  38.3 us
    dot_general x1, matrix products, expert_layer(): jnp.einsum('hcf,fd->hcd', activation, w_down[0], preferred_element_type=j...  14 us
    all_to_all x1, waiting for transfers between devices, shards(): lax.all_to_all(by_dest.astype(jnp.bfloat16), DP + ('tensor',), split_axis...  13.8 us
    all_to_all x1, starting transfers between devices, shards(): lax.all_to_all(by_dest.astype(jnp.bfloat16), DP + ('tensor',), split_axis...  8.73 us
    all_to_all x1, starting transfers between devices, expert_layer(): lax.all_to_all(result, HALF, split_axis=0, concat_axis=0, tiled=True)  6.61 us
    ppermute x4, starting transfers between devices, swap_halves(): return lax.ppermute(x, 'zh', [(0, 1), (1, 0)])  5.95 us
  transfers between devices with their start and end apart: 7, of which 7 were waited for; matrix products, arithmetic and copies ran while one was open for 1% of the time, Pallas kernels for 0%

profile of v5, /device:TPU:7, one launch (start us, length us, event | category | flops | bytes accessed | tf_op | source)
XLA Modules:
  0.0 205.7 jit_solution(1695474922262071574)
XLA Ops:
  0.7 0.9 iota_compare_fusion
  1.5 1.0 copy.75
  2.6 0.9 fusion.48
  3.5 2.4 %select_reduce_fusion = (f32[48,16]{1,0:T(8,128)S(1)}, f32[48,16,128]{2,1,0:T(8,128)S(1)}) fusion(pred[48,128]{1,0:T(8,128)(4,1)S(1)} %iota_compare_fusion, bf16[48,16,128]{2,1,0:T(8,128)(2,1)S(1)} %bitcast.92, bf16[48,128,128]{2,1,0:T(8,128)(2,1)} %param.17), kind=kOutput, calls=%fused_computation.29 | convolution fusion | flops 25459968 | bytes 2171904 | tf_op jit(solution)/shard_map/rkgd,rckd->rkgc/dot_general | solution.py:27
  5.9 0.3 fusion.32
  6.3 0.6 fusion.28
  7.0 2.4 %collective-permute-start = (bf16[48,2048]{1,0:T(8,128)(2,1)S(1)}, bf16[48,2048]{1,0:T(8,128)(2,1)S(1)}, u32[]{:S(2)}, u32[]{:S(2)}) collective-permute-start(bf16[48,2048]{1,0:T(8,128)(2,1)S(1)} %bitcast.93), channel_id=1, source_target_pairs={{0,16},{16,0},{1,17},{17,1},{2,18},{18,2},{3,19},{19,3},{4,20},{20... | collective-permute-start | bytes 589832 | tf_op jit(solution)/shard_map/ppermute | solution.py:52
  9.4 8.6 %collective-permute-done = bf16[48,2048]{1,0:T(8,128)(2,1)S(1)} collective-permute-done((bf16[48,2048]{1,0:T(8,128)(2,1)S(1)}, bf16[48,2048]{1,0:T(8,128)(2,1)S(1)}, u32[]{:S(2)}, u32[]{:S(2)}) %collective-permute-start) | collective-permute-done | bytes 196640 | tf_op jit(solution)/shard_map/ppermute | solution.py:52
  18.0 1.3 broadcast_in_dim.27
  19.4 4.5 %all-to-all-start = ((bf16[4,96,2048]{2,1,0:T(8,128)(2,1)}), bf16[4,96,2048]{2,1,0:T(8,128)(2,1)}, u32[]{:S(2)}, u32[]{:S(2)}) async-start(bf16[4,96,2048]{2,1,0:T(8,128)(2,1)} %broadcast_in_dim.27), calls=%async_computation | async-start | bytes 3145728 | tf_op jit(solution)/shard_map/all_to_all | solution.py:141
  23.9 2.5 %collective-permute-start.1 = (f32[12,16]{0,1:T(8,128)S(1)}, f32[12,16]{0,1:T(8,128)S(1)}, u32[]{:S(2)}, u32[]{:S(2)}) collective-permute-start(f32[12,16]{0,1:T(8,128)S(1)} %pad_maximum_fusion), channel_id=1, source_target_pairs={{0,16},{16,0},{1,17},{17,1},{2,18},{18,2},{3,19},{19,3},{4,20},{20... | collective-permute-start | bytes 2312 | tf_op jit(solution)/shard_map/ppermute | solution.py:52
  26.4 13.3 %collective-permute-done.1 = f32[12,16]{0,1:T(8,128)S(1)} collective-permute-done((f32[12,16]{0,1:T(8,128)S(1)}, f32[12,16]{0,1:T(8,128)S(1)}, u32[]{:S(2)}, u32[]{:S(2)}) %collective-permute-start.1) | collective-permute-done | bytes 800 | tf_op jit(solution)/shard_map/ppermute | solution.py:52
  39.8 0.1 pad_add_fusion.1
  39.8 0.1 copy.63
  39.9 0.1 copy.64
  40.0 0.1 sub.40
  40.1 0.6 reduce-window.6
  40.7 0.2 slice_reduce_fusion
  40.9 1.0 all-to-all-done
  42.0 2.4 %fusion.25 = bf16[4,96,512]{2,1,0:T(8,128)(2,1)S(1)} fusion(bf16[4,96,2048]{2,1,0:T(8,128)(2,1)} %all-to-all-done, bf16[2048,512]{1,0:T(8,128)(2,1)S(1)} %copy-done), kind=kOutput, calls=%fused_computation.17 | convolution fusion | flops 805502976 | bytes 4063232 | tf_op jit(solution)/shard_map/sqd,df->sqf/dot_general | solution.py:142
  44.4 0.3 copy.57
  44.7 0.9 copy.71
  45.6 8.7 %all-to-all-start.1 = ((bf16[32,12,512]{2,1,0:T(8,128)(2,1)}), bf16[32,12,512]{2,1,0:T(8,128)(2,1)S(1)}, u32[]{:S(2)}, u32[]{:S(2)}) async-start(bf16[32,12,512]{2,1,0:T(8,128)(2,1)} %bitcast.6), calls=%async_computation.1 | async-start | bytes 1048576 | tf_op jit(solution)/shard_map/all_to_all | solution.py:148
  54.3 0.1 bitcast_bitcast_fusion
  54.4 0.1 reduce_sum.72
  54.5 0.1 gt.17
  54.7 13.8 %all-to-all-done.1 = bf16[32,12,512]{2,1,0:T(8,128)(2,1)S(1)} async-done(((bf16[32,12,512]{2,1,0:T(8,128)(2,1)}), bf16[32,12,512]{2,1,0:T(8,128)(2,1)S(1)}, u32[]{:S(2)}, u32[]{:S(2)}) %all-to-all-start.1) | async-done | bytes 393248 | tf_op jit(solution)/shard_map/all_to_all | solution.py:148
  68.5 0.1 convert_reduce_fusion
  68.6 0.1 copy.60
  68.8 0.2 copy.77
  68.9 0.2 fusion.33
  69.1 0.1 fusion.35
  69.3 0.6 fusion.31
  69.9 8.2 %collective-permute-done.2 = bf16[12,4096]{1,0:T(8,128)(2,1)S(1)} collective-permute-done((bf16[12,4096]{1,0:T(8,128)(2,1)S(1)}, bf16[12,4096]{1,0:T(8,128)(2,1)S(1)}, u32[]{:S(2)}, u32[]{:S(2)}) %collective-permute-start.2) | collective-permute-done | bytes 98336 | tf_op jit(solution)/shard_map/ppermute | solution.py:52
  78.1 1.0 convolution_convert_fusion
  79.1 40.8 %all_to_all.20 = bf16[16,18,4096]{2,1,0:T(8,128)(2,1)S(1)} all-to-all(bf16[16,18,4096]{2,1,0:T(8,128)(2,1)S(1)} %convolution_convert_fusion), channel_id=1, replica_groups=mesh['zh'=2,'dl'=4,'tensor'=4] {'dl','tensor'}, dimensions={0} | all-to-all | bytes 4718592 | tf_op jit(solution)/shard_map/all_to_all | solution.py:91
  119.8 1.7 copy-done.1
  121.6 2.8 %fusion.4 = f32[16,18,768]{2,1,0:T(8,128)S(1)} fusion(bf16[16,18,4096]{2,1,0:T(8,128)(2,1)S(1)} %all_to_all.20, bf16[1,4096,768]{2,1,0:T(8,128)(2,1)S(1)} %bitcast.100), kind=kOutput, calls=%fused_computation.4 | convolution fusion | flops 1811939328 | bytes 9535488 | tf_op jit(solution)/shard_map/hcd,df->hcf/dot_general | solution.py:92
  124.3 14.0 %fusion.6 = bf16[16,18,4096]{2,1,0:T(8,128)(2,1)} fusion(bf16[1,768,4096]{2,1,0:T(8,128)(2,1)} %param.27, bf16[16,18,4096]{2,1,0:T(8,128)(2,1)} %copy-done.1, bf16[1,4096,768]{2,1,0:T(8,128)(2,1)} %param.26, f32[16,18,768]{2,1,0:T(8,128)S(1)} %fusion.4), kind=kOutput, calls=%fused_computation.7 | convolution fusion | flops 3626385408 | bytes 18186240 | tf_op jit(solution)/shard_map/hcf,fd->hcd/dot_general | solution.py:95
  138.3 6.6 %all-to-all-start.3 = ((bf16[16,18,4096]{2,1,0:T(8,128)(2,1)}), bf16[16,18,4096]{2,1,0:T(8,128)(2,1)}, u32[]{:S(2)}, u32[]{:S(2)}) async-start(bf16[16,18,4096]{2,1,0:T(8,128)(2,1)} %fusion.6), calls=%async_computation.3 | async-start | bytes 6291456 | tf_op jit(solution)/shard_map/all_to_all | solution.py:98
  144.9 0.1 pad_maximum_fusion.2
  145.0 0.1 copy.61
  145.0 0.1 copy.62
  145.1 46.6 %all-to-all-done.3 = bf16[16,18,4096]{2,1,0:T(8,128)(2,1)} async-done(((bf16[16,18,4096]{2,1,0:T(8,128)(2,1)}), bf16[16,18,4096]{2,1,0:T(8,128)(2,1)}, u32[]{:S(2)}, u32[]{:S(2)}) %all-to-all-start.3) | async-done | bytes 2359328 | tf_op jit(solution)/shard_map/all_to_all | solution.py:98
  191.8 4.0 %fusion.14 = f32[24,4096]{1,0:T(8,128)S(1)} fusion(bf16[16,18,4096]{2,1,0:T(8,128)(2,1)} %all-to-all-done.3, f32[24,8]{1,0:T(8,128)S(1)} %broadcast_select_fusion, s32[24,8]{1,0:T(8,128)S(1)} %add_select_fusion, s32[18,16]{0,1:T(8,128)S(1)} %multiply_add_fusion.1), kind=kOutput, calls=%fused_computation.14 | convolution fusion | flops 454514688 | bytes 2755200 | tf_op jit(solution)/shard_map/hcp,hcd->pd/dot_general | solution.py:99
  195.9 1.0 collective-permute-start.3
  196.9 8.2 %collective-permute-done.3 = bf16[12,4096]{1,0:T(8,128)(2,1)S(1)} collective-permute-done((bf16[12,4096]{1,0:T(8,128)(2,1)S(1)}, bf16[12,4096]{1,0:T(8,128)(2,1)S(1)}, u32[]{:S(2)}, u32[]{:S(2)}) %collective-permute-start.3) | collective-permute-done | bytes 98336 | tf_op jit(solution)/shard_map/ppermute | solution.py:52
  205.0 0.7 add_convert_fusion
  (46 shorter events, 0.6 us)
Async XLA Ops:
  0.6 41.3 %copy-start = (bf16[2048,512]{1,0:T(8,128)(2,1)S(1)}, bf16[2048,512]{1,0:T(8,128)(2,1)}, u32[]{:S(2)}) copy-start(bf16[2048,512]{1,0:T(8,128)(2,1)} %param.21) | copy-start | bytes 6291460
  0.6 5.6 %copy-start.7 = (bf16[48,128]{1,0:T(8,128)(2,1)S(1)}, bf16[48,128]{1,0:T(8,128)(2,1)}, u32[]{:S(2)}) copy-start(bf16[48,128]{1,0:T(8,128)(2,1)} %param.16) | copy-start | bytes 36868
  0.7 5.6 %copy-start.8 = (bf16[48,128,128]{2,1,0:T(8,128)(2,1)S(1)}, bf16[48,128,128]{2,1,0:T(8,128)(2,1)}, u32[]{:S(2)}) copy-start(bf16[48,128,128]{2,1,0:T(8,128)(2,1)} %param.18) | copy-start | bytes 4718596
  6.9 17.0 %copy-start.5 = (s32[12,8]{0,1:T(8,128)S(1)}, s32[12,8]{0,1:T(8,128)}, u32[]{:S(2)}) copy-start(s32[12,8]{0,1:T(8,128)} %param.23) | copy-start | bytes 1156
  6.9 17.0 %copy-start.6 = (f32[12,8]{0,1:T(8,128)S(1)}, f32[12,8]{0,1:T(8,128)}, u32[]{:S(2)}) copy-start(f32[12,8]{0,1:T(8,128)} %param.24) | copy-start | bytes 1156
  7.0 11.0 %collective-permute-start = (bf16[48,2048]{1,0:T(8,128)(2,1)S(1)}, bf16[48,2048]{1,0:T(8,128)(2,1)S(1)}, u32[]{:S(2)}, u32[]{:S(2)}) collective-permute-start(bf16[48,2048]{1,0:T(8,128)(2,1)S(1)} %bitcast.93), channel_id=1, source_target_pairs={{0,16},{16,0},{1,17},{17,1},{2,18},{18,2},{3,19},{19,3},{4,20},{20... | collective-permute-start | bytes 589832 | tf_op jit(solution)/shard_map/ppermute | solution.py:52
  19.4 22.6 %all-to-all-start = ((bf16[4,96,2048]{2,1,0:T(8,128)(2,1)}), bf16[4,96,2048]{2,1,0:T(8,128)(2,1)}, u32[]{:S(2)}, u32[]{:S(2)}) async-start(bf16[4,96,2048]{2,1,0:T(8,128)(2,1)} %broadcast_in_dim.27), calls=%async_computation | async-start | bytes 3145728 | tf_op jit(solution)/shard_map/all_to_all | solution.py:141
  23.9 15.8 %collective-permute-start.1 = (f32[12,16]{0,1:T(8,128)S(1)}, f32[12,16]{0,1:T(8,128)S(1)}, u32[]{:S(2)}, u32[]{:S(2)}) collective-permute-start(f32[12,16]{0,1:T(8,128)S(1)} %pad_maximum_fusion), channel_id=1, source_target_pairs={{0,16},{16,0},{1,17},{17,1},{2,18},{18,2},{3,19},{19,3},{4,20},{20... | collective-permute-start | bytes 2312 | tf_op jit(solution)/shard_map/ppermute | solution.py:52
  44.3 24.6 %copy-start.3 = (bf16[12,4096]{1,0:T(8,128)(2,1)S(1)}, bf16[12,4096]{1,0:T(8,128)(2,1)}, u32[]{:S(2)}) copy-start(bf16[12,4096]{1,0:T(8,128)(2,1)} %param.20) | copy-start | bytes 294916
  44.4 24.8 %copy-start.4 = (f32[4096]{0:T(1024)S(1)}, f32[4096]{0:T(1024)}, u32[]{:S(2)}) copy-start(f32[4096]{0:T(1024)} %param.22) | copy-start | bytes 49156
  45.6 22.9 %all-to-all-start.1 = ((bf16[32,12,512]{2,1,0:T(8,128)(2,1)}), bf16[32,12,512]{2,1,0:T(8,128)(2,1)S(1)}, u32[]{:S(2)}, u32[]{:S(2)}) async-start(bf16[32,12,512]{2,1,0:T(8,128)(2,1)} %bitcast.6), calls=%async_computation.1 | async-start | bytes 1048576 | tf_op jit(solution)/shard_map/all_to_all | solution.py:148
  68.5 53.0 %slice-start = ((s8[6291456]{0:T(1024)(128)(4,1)}), s8[4194304]{0:T(1024)(128)(4,1)S(1)}, s32[]{:S(2)}) async-start(s8[6291456]{0:T(1024)(128)(4,1)} %bitcast.99), calls=%async_computation.4 | async-start | bytes 8388608
  69.1 50.7 %copy-start.2 = (bf16[12,4096]{1,0:T(8,128)(2,1)}, bf16[12,4096]{1,0:T(8,128)(2,1)S(1)}, u32[]{:S(2)}) copy-start(bf16[12,4096]{1,0:T(8,128)(2,1)S(1)} %get-tuple-element.5) | copy-start | bytes 294916
  69.2 8.8 %collective-permute-start.2 = (bf16[12,4096]{1,0:T(8,128)(2,1)S(1)}, bf16[12,4096]{1,0:T(8,128)(2,1)S(1)}, u32[]{:S(2)}, u32[]{:S(2)}) collective-permute-start(bf16[12,4096]{1,0:T(8,128)(2,1)S(1)} %fusion.35), channel_id=1, source_target_pairs={{0,16},{16,0},{1,17},{17,1},{2,18},{18,2},{3,19},{19,3},{4,20},{20... | collective-permute-start | bytes 294920 | tf_op jit(solution)/shard_map/ppermute | solution.py:52
  69.9 51.7 %slice-start.1 = ((s8[6291456]{0:T(1024)(128)(4,1)}), s8[2097152]{0:T(1024)(128)(4,1)S(1)}, s32[]{:S(2)}) async-start(s8[6291456]{0:T(1024)(128)(4,1)} %bitcast.99), calls=%async_computation.5 | async-start | bytes 4194304
  119.8 1.7 copy-start.1
  138.3 53.5 %all-to-all-start.3 = ((bf16[16,18,4096]{2,1,0:T(8,128)(2,1)}), bf16[16,18,4096]{2,1,0:T(8,128)(2,1)}, u32[]{:S(2)}, u32[]{:S(2)}) async-start(bf16[16,18,4096]{2,1,0:T(8,128)(2,1)} %fusion.6), calls=%async_computation.3 | async-start | bytes 6291456 | tf_op jit(solution)/shard_map/all_to_all | solution.py:98
  195.9 9.2 %collective-permute-start.3 = (bf16[12,4096]{1,0:T(8,128)(2,1)S(1)}, bf16[12,4096]{1,0:T(8,128)(2,1)S(1)}, u32[]{:S(2)}, u32[]{:S(2)}) collective-permute-start(bf16[12,4096]{1,0:T(8,128)(2,1)S(1)} %select_convert_fusion), channel_id=1, source_target_pairs={{0,16},{16,0},{1,17},{17,1},{2,18},{18,2},{3,19},{19,3},{4,20},{20... | collective-permute-start | bytes 294920 | tf_op jit(solution)/shard_map/ppermute | solution.py:52

commit v6 on v5

--- a/solution.py
+++ b/solution.py
@@ -58,6 +58,7 @@
     n_half = lax.axis_size("dl") * lax.axis_size("tensor")
     experts_all = 2 * n_half
     capacity = 2 * max(2, 3 * tok_here * chosen_count // experts_all)
+    capacity = -(-capacity // 8) * 8
     side = lax.axis_index("zh")
     other_rows = swap_halves(normed)
     packed = swap_halves(jnp.concatenate([route_ids.astype(jnp.float32), route_weight], axis=1))

time: 206 us -> 206 us (level)
  no operation moved by 1% of the time
where the time goes in v6:
time: 206 us
  waiting for transfers between devices  99.6 us (48%)
  blocking collectives  40.8 us (20%)
  matrix products  28 us (14%)
  starting transfers between devices  25.8 us (13%)
  local copies, waits for them, and re-layouts  6.48 us (3%)
  other arithmetic  4.06 us (2%)
    all_to_all x1, waiting for transfers between devices, expert_layer(): lax.all_to_all(result, HALF, split_axis=0, concat_axis=0, tiled=True)  46.6 us
    all_to_all x1, blocking collectives, expert_layer(): lax.all_to_all(outgoing, HALF, split_axis=0, concat_axis=0, tiled=True)  40.8 us
    ppermute x4, waiting for transfers between devices, swap_halves(): return lax.ppermute(x, 'zh', [(0, 1), (1, 0)])  38.1 us
    dot_general x1, matrix products, expert_layer(): jnp.einsum('hcf,fd->hcd', activation, w_down[0], preferred_element_type=j...  14 us
    all_to_all x1, waiting for transfers between devices, shards(): lax.all_to_all(by_dest.astype(jnp.bfloat16), DP + ('tensor',), split_axis...  13.8 us
    all_to_all x1, starting transfers between devices, shards(): lax.all_to_all(by_dest.astype(jnp.bfloat16), DP + ('tensor',), split_axis...  8.73 us
    all_to_all x1, starting transfers between devices, expert_layer(): lax.all_to_all(result, HALF, split_axis=0, concat_axis=0, tiled=True)  6.61 us
    ppermute x4, starting transfers between devices, swap_halves(): return lax.ppermute(x, 'zh', [(0, 1), (1, 0)])  5.95 us
  transfers between devices with their start and end apart: 7, of which 7 were waited for; matrix products, arithmetic and copies ran while one was open for 1% of the time, Pallas kernels for 0%

profile of v6, /device:TPU:7, one launch (start us, length us, event | category | flops | bytes accessed | tf_op | source)
XLA Modules:
  0.0 205.7 jit_solution(16470478778083975984)
XLA Ops:
  0.7 0.9 iota_compare_fusion
  1.5 1.0 copy.75
  2.6 0.9 fusion.48
  3.5 2.4 %select_reduce_fusion = (f32[48,16]{1,0:T(8,128)S(1)}, f32[48,16,128]{2,1,0:T(8,128)S(1)}) fusion(pred[48,128]{1,0:T(8,128)(4,1)S(1)} %iota_compare_fusion, bf16[48,16,128]{2,1,0:T(8,128)(2,1)S(1)} %bitcast.92, bf16[48,128,128]{2,1,0:T(8,128)(2,1)} %param.17), kind=kOutput, calls=%fused_computation.29 | convolution fusion | flops 25459968 | bytes 2171904 | tf_op jit(solution)/shard_map/rkgd,rckd->rkgc/dot_general | solution.py:27
  5.9 0.3 fusion.32
  6.3 0.6 fusion.28
  7.0 2.4 %collective-permute-start = (bf16[48,2048]{1,0:T(8,128)(2,1)S(1)}, bf16[48,2048]{1,0:T(8,128)(2,1)S(1)}, u32[]{:S(2)}, u32[]{:S(2)}) collective-permute-start(bf16[48,2048]{1,0:T(8,128)(2,1)S(1)} %bitcast.93), channel_id=1, source_target_pairs={{0,16},{16,0},{1,17},{17,1},{2,18},{18,2},{3,19},{19,3},{4,20},{20... | collective-permute-start | bytes 589832 | tf_op jit(solution)/shard_map/ppermute | solution.py:52
  9.4 8.6 %collective-permute-done = bf16[48,2048]{1,0:T(8,128)(2,1)S(1)} collective-permute-done((bf16[48,2048]{1,0:T(8,128)(2,1)S(1)}, bf16[48,2048]{1,0:T(8,128)(2,1)S(1)}, u32[]{:S(2)}, u32[]{:S(2)}) %collective-permute-start) | collective-permute-done | bytes 196640 | tf_op jit(solution)/shard_map/ppermute | solution.py:52
  18.0 1.3 broadcast_in_dim.27
  19.4 4.5 %all-to-all-start = ((bf16[4,96,2048]{2,1,0:T(8,128)(2,1)}), bf16[4,96,2048]{2,1,0:T(8,128)(2,1)}, u32[]{:S(2)}, u32[]{:S(2)}) async-start(bf16[4,96,2048]{2,1,0:T(8,128)(2,1)} %broadcast_in_dim.27), calls=%async_computation | async-start | bytes 3145728 | tf_op jit(solution)/shard_map/all_to_all | solution.py:142
  23.9 2.5 %collective-permute-start.1 = (f32[12,16]{0,1:T(8,128)S(1)}, f32[12,16]{0,1:T(8,128)S(1)}, u32[]{:S(2)}, u32[]{:S(2)}) collective-permute-start(f32[12,16]{0,1:T(8,128)S(1)} %pad_maximum_fusion), channel_id=1, source_target_pairs={{0,16},{16,0},{1,17},{17,1},{2,18},{18,2},{3,19},{19,3},{4,20},{20... | collective-permute-start | bytes 2312 | tf_op jit(solution)/shard_map/ppermute | solution.py:52
  26.4 13.3 %collective-permute-done.1 = f32[12,16]{0,1:T(8,128)S(1)} collective-permute-done((f32[12,16]{0,1:T(8,128)S(1)}, f32[12,16]{0,1:T(8,128)S(1)}, u32[]{:S(2)}, u32[]{:S(2)}) %collective-permute-start.1) | collective-permute-done | bytes 800 | tf_op jit(solution)/shard_map/ppermute | solution.py:52
  39.8 0.1 pad_add_fusion.1
  39.8 0.1 copy.63
  39.9 0.1 copy.64
  40.0 0.1 sub.40
  40.1 0.6 reduce-window.6
  40.7 0.2 slice_reduce_fusion
  40.9 1.0 all-to-all-done
  42.0 2.4 %fusion.25 = bf16[4,96,512]{2,1,0:T(8,128)(2,1)S(1)} fusion(bf16[4,96,2048]{2,1,0:T(8,128)(2,1)} %all-to-all-done, bf16[2048,512]{1,0:T(8,128)(2,1)S(1)} %copy-done), kind=kOutput, calls=%fused_computation.18 | convolution fusion | flops 805502976 | bytes 4063232 | tf_op jit(solution)/shard_map/sqd,df->sqf/dot_general | solution.py:143
  44.4 0.3 copy.57
  44.7 0.9 copy.71
  45.6 8.7 %all-to-all-start.1 = ((bf16[32,12,512]{2,1,0:T(8,128)(2,1)}), bf16[32,12,512]{2,1,0:T(8,128)(2,1)S(1)}, u32[]{:S(2)}, u32[]{:S(2)}) async-start(bf16[32,12,512]{2,1,0:T(8,128)(2,1)} %bitcast.6), calls=%async_computation.1 | async-start | bytes 1048576 | tf_op jit(solution)/shard_map/all_to_all | solution.py:149
  54.3 0.1 bitcast_bitcast_fusion
  54.4 0.1 reduce_sum.72
  54.5 0.1 gt.17
  54.7 13.8 %all-to-all-done.1 = bf16[32,12,512]{2,1,0:T(8,128)(2,1)S(1)} async-done(((bf16[32,12,512]{2,1,0:T(8,128)(2,1)}), bf16[32,12,512]{2,1,0:T(8,128)(2,1)S(1)}, u32[]{:S(2)}, u32[]{:S(2)}) %all-to-all-start.1) | async-done | bytes 393248 | tf_op jit(solution)/shard_map/all_to_all | solution.py:149
  68.5 0.1 convert_reduce_fusion
  68.6 0.1 copy.60
  68.8 0.2 copy.77
  68.9 0.2 fusion.33
  69.1 0.1 fusion.35
  69.3 0.7 fusion.29
  70.0 8.0 %collective-permute-done.2 = bf16[12,4096]{1,0:T(8,128)(2,1)S(1)} collective-permute-done((bf16[12,4096]{1,0:T(8,128)(2,1)S(1)}, bf16[12,4096]{1,0:T(8,128)(2,1)S(1)}, u32[]{:S(2)}, u32[]{:S(2)}) %collective-permute-start.2) | collective-permute-done | bytes 98336 | tf_op jit(solution)/shard_map/ppermute | solution.py:52
  78.1 1.0 convolution_convert_fusion
  79.1 40.8 %all_to_all.20 = bf16[16,24,4096]{2,1,0:T(8,128)(2,1)S(1)} all-to-all(bf16[16,24,4096]{2,1,0:T(8,128)(2,1)S(1)} %convolution_convert_fusion), channel_id=1, replica_groups=mesh['zh'=2,'dl'=4,'tensor'=4] {'dl','tensor'}, dimensions={0} | all-to-all | bytes 6291456 | tf_op jit(solution)/shard_map/all_to_all | solution.py:92
  119.8 1.7 copy-done.1
  121.6 2.8 %fusion.4 = f32[16,24,768]{2,1,0:T(8,128)S(1)} fusion(bf16[16,24,4096]{2,1,0:T(8,128)(2,1)S(1)} %all_to_all.20, bf16[1,4096,768]{2,1,0:T(8,128)(2,1)S(1)} %bitcast.100), kind=kOutput, calls=%fused_computation.4 | convolution fusion | flops 2415919104 | bytes 10616832 | tf_op jit(solution)/shard_map/hcd,df->hcf/dot_general | solution.py:93
  124.3 14.0 %fusion.6 = bf16[16,24,4096]{2,1,0:T(8,128)(2,1)} fusion(bf16[1,768,4096]{2,1,0:T(8,128)(2,1)} %param.27, bf16[16,24,4096]{2,1,0:T(8,128)(2,1)} %copy-done.1, bf16[1,4096,768]{2,1,0:T(8,128)(2,1)} %param.26, f32[16,24,768]{2,1,0:T(8,128)S(1)} %fusion.4), kind=kOutput, calls=%fused_computation.7 | convolution fusion | flops 4835180544 | bytes 20054016 | tf_op jit(solution)/shard_map/hcf,fd->hcd/dot_general | solution.py:96
  138.3 6.6 %all-to-all-start.3 = ((bf16[16,24,4096]{2,1,0:T(8,128)(2,1)}), bf16[16,24,4096]{2,1,0:T(8,128)(2,1)}, u32[]{:S(2)}, u32[]{:S(2)}) async-start(bf16[16,24,4096]{2,1,0:T(8,128)(2,1)} %fusion.6), calls=%async_computation.3 | async-start | bytes 6291456 | tf_op jit(solution)/shard_map/all_to_all | solution.py:99
  144.9 0.1 pad_maximum_fusion.2
  145.0 0.1 copy.61
  145.0 0.1 copy.62
  145.1 46.6 %all-to-all-done.3 = bf16[16,24,4096]{2,1,0:T(8,128)(2,1)} async-done(((bf16[16,24,4096]{2,1,0:T(8,128)(2,1)}), bf16[16,24,4096]{2,1,0:T(8,128)(2,1)}, u32[]{:S(2)}, u32[]{:S(2)}) %all-to-all-start.3) | async-done | bytes 3145760 | tf_op jit(solution)/shard_map/all_to_all | solution.py:99
  191.8 4.0 %fusion.14 = f32[24,4096]{1,0:T(8,128)S(1)} fusion(bf16[16,24,4096]{2,1,0:T(8,128)(2,1)} %all-to-all-done.3, f32[24,8]{1,0:T(8,128)S(1)} %broadcast_select_fusion, s32[24,8]{1,0:T(8,128)S(1)} %add_select_fusion, s32[24,16]{0,1:T(8,128)S(1)} %multiply_add_fusion.1), kind=kOutput, calls=%fused_computation.15 | convolution fusion | flops 605528064 | bytes 3542016 | tf_op jit(solution)/shard_map/hcp,hcd->pd/dot_general | solution.py:100
  195.8 1.0 collective-permute-start.3
  196.8 8.2 %collective-permute-done.3 = bf16[12,4096]{1,0:T(8,128)(2,1)S(1)} collective-permute-done((bf16[12,4096]{1,0:T(8,128)(2,1)S(1)}, bf16[12,4096]{1,0:T(8,128)(2,1)S(1)}, u32[]{:S(2)}, u32[]{:S(2)}) %collective-permute-start.3) | collective-permute-done | bytes 98336 | tf_op jit(solution)/shard_map/ppermute | solution.py:52
  205.0 0.7 add_convert_fusion
  (46 shorter events, 0.6 us)
Async XLA Ops:
  0.6 41.3 %copy-start = (bf16[2048,512]{1,0:T(8,128)(2,1)S(1)}, bf16[2048,512]{1,0:T(8,128)(2,1)}, u32[]{:S(2)}) copy-start(bf16[2048,512]{1,0:T(8,128)(2,1)} %param.21) | copy-start | bytes 6291460
  0.6 5.6 %copy-start.7 = (bf16[48,128]{1,0:T(8,128)(2,1)S(1)}, bf16[48,128]{1,0:T(8,128)(2,1)}, u32[]{:S(2)}) copy-start(bf16[48,128]{1,0:T(8,128)(2,1)} %param.16) | copy-start | bytes 36868
  0.7 5.6 %copy-start.8 = (bf16[48,128,128]{2,1,0:T(8,128)(2,1)S(1)}, bf16[48,128,128]{2,1,0:T(8,128)(2,1)}, u32[]{:S(2)}) copy-start(bf16[48,128,128]{2,1,0:T(8,128)(2,1)} %param.18) | copy-start | bytes 4718596
  6.9 17.0 %copy-start.5 = (s32[12,8]{0,1:T(8,128)S(1)}, s32[12,8]{0,1:T(8,128)}, u32[]{:S(2)}) copy-start(s32[12,8]{0,1:T(8,128)} %param.23) | copy-start | bytes 1156
  6.9 17.0 %copy-start.6 = (f32[12,8]{0,1:T(8,128)S(1)}, f32[12,8]{0,1:T(8,128)}, u32[]{:S(2)}) copy-start(f32[12,8]{0,1:T(8,128)} %param.24) | copy-start | bytes 1156
  7.0 11.0 %collective-permute-start = (bf16[48,2048]{1,0:T(8,128)(2,1)S(1)}, bf16[48,2048]{1,0:T(8,128)(2,1)S(1)}, u32[]{:S(2)}, u32[]{:S(2)}) collective-permute-start(bf16[48,2048]{1,0:T(8,128)(2,1)S(1)} %bitcast.93), channel_id=1, source_target_pairs={{0,16},{16,0},{1,17},{17,1},{2,18},{18,2},{3,19},{19,3},{4,20},{20... | collective-permute-start | bytes 589832 | tf_op jit(solution)/shard_map/ppermute | solution.py:52
  19.4 22.6 %all-to-all-start = ((bf16[4,96,2048]{2,1,0:T(8,128)(2,1)}), bf16[4,96,2048]{2,1,0:T(8,128)(2,1)}, u32[]{:S(2)}, u32[]{:S(2)}) async-start(bf16[4,96,2048]{2,1,0:T(8,128)(2,1)} %broadcast_in_dim.27), calls=%async_computation | async-start | bytes 3145728 | tf_op jit(solution)/shard_map/all_to_all | solution.py:142
  23.9 15.8 %collective-permute-start.1 = (f32[12,16]{0,1:T(8,128)S(1)}, f32[12,16]{0,1:T(8,128)S(1)}, u32[]{:S(2)}, u32[]{:S(2)}) collective-permute-start(f32[12,16]{0,1:T(8,128)S(1)} %pad_maximum_fusion), channel_id=1, source_target_pairs={{0,16},{16,0},{1,17},{17,1},{2,18},{18,2},{3,19},{19,3},{4,20},{20... | collective-permute-start | bytes 2312 | tf_op jit(solution)/shard_map/ppermute | solution.py:52
  44.3 24.6 %copy-start.3 = (bf16[12,4096]{1,0:T(8,128)(2,1)S(1)}, bf16[12,4096]{1,0:T(8,128)(2,1)}, u32[]{:S(2)}) copy-start(bf16[12,4096]{1,0:T(8,128)(2,1)} %param.20) | copy-start | bytes 294916
  44.4 24.8 %copy-start.4 = (f32[4096]{0:T(1024)S(1)}, f32[4096]{0:T(1024)}, u32[]{:S(2)}) copy-start(f32[4096]{0:T(1024)} %param.22) | copy-start | bytes 49156
  45.6 22.9 %all-to-all-start.1 = ((bf16[32,12,512]{2,1,0:T(8,128)(2,1)}), bf16[32,12,512]{2,1,0:T(8,128)(2,1)S(1)}, u32[]{:S(2)}, u32[]{:S(2)}) async-start(bf16[32,12,512]{2,1,0:T(8,128)(2,1)} %bitcast.6), calls=%async_computation.1 | async-start | bytes 1048576 | tf_op jit(solution)/shard_map/all_to_all | solution.py:149
  68.5 53.0 %slice-start = ((s8[6291456]{0:T(1024)(128)(4,1)}), s8[4194304]{0:T(1024)(128)(4,1)S(1)}, s32[]{:S(2)}) async-start(s8[6291456]{0:T(1024)(128)(4,1)} %bitcast.99), calls=%async_computation.4 | async-start | bytes 8388608
  69.1 50.7 %copy-start.2 = (bf16[12,4096]{1,0:T(8,128)(2,1)}, bf16[12,4096]{1,0:T(8,128)(2,1)S(1)}, u32[]{:S(2)}) copy-start(bf16[12,4096]{1,0:T(8,128)(2,1)S(1)} %get-tuple-element.5) | copy-start | bytes 294916
  69.2 8.8 %collective-permute-start.2 = (bf16[12,4096]{1,0:T(8,128)(2,1)S(1)}, bf16[12,4096]{1,0:T(8,128)(2,1)S(1)}, u32[]{:S(2)}, u32[]{:S(2)}) collective-permute-start(bf16[12,4096]{1,0:T(8,128)(2,1)S(1)} %fusion.35), channel_id=1, source_target_pairs={{0,16},{16,0},{1,17},{17,1},{2,18},{18,2},{3,19},{19,3},{4,20},{20... | collective-permute-start | bytes 294920 | tf_op jit(solution)/shard_map/ppermute | solution.py:52
  70.0 51.5 %slice-start.1 = ((s8[6291456]{0:T(1024)(128)(4,1)}), s8[2097152]{0:T(1024)(128)(4,1)S(1)}, s32[]{:S(2)}) async-start(s8[6291456]{0:T(1024)(128)(4,1)} %bitcast.99), calls=%async_computation.5 | async-start | bytes 4194304
  119.8 1.7 copy-start.1
  138.3 53.5 %all-to-all-start.3 = ((bf16[16,24,4096]{2,1,0:T(8,128)(2,1)}), bf16[16,24,4096]{2,1,0:T(8,128)(2,1)}, u32[]{:S(2)}, u32[]{:S(2)}) async-start(bf16[16,24,4096]{2,1,0:T(8,128)(2,1)} %fusion.6), calls=%async_computation.3 | async-start | bytes 6291456 | tf_op jit(solution)/shard_map/all_to_all | solution.py:99
  195.8 9.2 %collective-permute-start.3 = (bf16[12,4096]{1,0:T(8,128)(2,1)S(1)}, bf16[12,4096]{1,0:T(8,128)(2,1)S(1)}, u32[]{:S(2)}, u32[]{:S(2)}) collective-permute-start(bf16[12,4096]{1,0:T(8,128)(2,1)S(1)} %select_convert_fusion), channel_id=1, source_target_pairs={{0,16},{16,0},{1,17},{17,1},{2,18},{18,2},{3,19},{19,3},{4,20},{20... | collective-permute-start | bytes 294920 | tf_op jit(solution)/shard_map/ppermute | solution.py:52

commit v7 on v6

--- a/solution.py
+++ b/solution.py
@@ -93,6 +93,7 @@
     gate_part = jnp.einsum("hcd,df->hcf", received, w_gate[0], preferred_element_type=jnp.float32)
     up_part = jnp.einsum("hcd,df->hcf", received, w_up[0], preferred_element_type=jnp.float32)
     activation = (jax.nn.silu(gate_part) * up_part).astype(jnp.bfloat16)
+    activation = lax.optimization_barrier(activation)
     result = jnp.einsum(
         "hcf,fd->hcd", activation, w_down[0], preferred_element_type=jnp.float32
     ).astype(jnp.bfloat16)

time: 206 us -> 198 us (0.961)
  matrix products: 28 us -> 21 us
    dot_general x1, matrix products: 14 us -> 4.13 us  [expert_layer(): jnp.einsum('hcf,fd->hcd', activation, w_down[0], preferred_element_type=j...]
    dot_general x0 -> x1, matrix products: none -> 2.8 us  [expert_layer(): jnp.einsum('hcd,df->hcf', received, w_up[0], preferred_element_type=jnp.f...]
where the time goes in v7:
time: 198 us; the launch traced here: 197 us
  waiting for transfers between devices  99.6 us (50%)
  blocking collectives  41 us (21%)
  starting transfers between devices  25.8 us (13%)
  matrix products  21 us (11%)
  local copies, waits for them, and re-layouts  4.82 us (2%)
  other arithmetic  4.05 us (2%)
    all_to_all x1, waiting for transfers between devices, expert_layer(): lax.all_to_all(result, HALF, split_axis=0, concat_axis=0, tiled=True)  46.6 us
    all_to_all x1, blocking collectives, expert_layer(): lax.all_to_all(outgoing, HALF, split_axis=0, concat_axis=0, tiled=True)  41 us
    ppermute x4, waiting for transfers between devices, swap_halves(): return lax.ppermute(x, 'zh', [(0, 1), (1, 0)])  38.1 us
    all_to_all x1, waiting for transfers between devices, shards(): lax.all_to_all(by_dest.astype(jnp.bfloat16), DP + ('tensor',), split_axis...  13.8 us
    all_to_all x1, starting transfers between devices, shards(): lax.all_to_all(by_dest.astype(jnp.bfloat16), DP + ('tensor',), split_axis...  8.75 us
    all_to_all x1, starting transfers between devices, expert_layer(): lax.all_to_all(result, HALF, split_axis=0, concat_axis=0, tiled=True)  6.6 us
    ppermute x4, starting transfers between devices, swap_halves(): return lax.ppermute(x, 'zh', [(0, 1), (1, 0)])  5.95 us
    all_to_all x1, starting transfers between devices, shards(): lax.all_to_all(spread, 'dl', split_axis=0, concat_axis=0, tiled=True)  4.53 us
  transfers between devices with their start and end apart: 7, of which 7 were waited for; matrix products, arithmetic and copies ran while one was open for 1% of the time, Pallas kernels for 0%

profile of v7, /device:TPU:7, one launch (start us, length us, event | category | flops | bytes accessed | tf_op | source)
XLA Modules:
  0.0 197.4 jit_solution(2963980793730466008)
XLA Ops:
  0.7 0.9 iota_compare_fusion
  1.5 1.0 copy.75
  2.6 0.9 fusion.48
  3.5 2.4 %select_reduce_fusion = (f32[48,16]{1,0:T(8,128)S(1)}, f32[48,16,128]{2,1,0:T(8,128)S(1)}) fusion(pred[48,128]{1,0:T(8,128)(4,1)S(1)} %iota_compare_fusion, bf16[48,16,128]{2,1,0:T(8,128)(2,1)S(1)} %bitcast.84, bf16[48,128,128]{2,1,0:T(8,128)(2,1)} %param.17), kind=kOutput, calls=%fused_computation.29 | convolution fusion | flops 25459968 | bytes 2171904 | tf_op jit(solution)/shard_map/rkgd,rckd->rkgc/dot_general | solution.py:27
  5.9 0.3 fusion.32
  6.3 0.6 fusion.28
  7.0 2.4 %collective-permute-start = (bf16[48,2048]{1,0:T(8,128)(2,1)S(1)}, bf16[48,2048]{1,0:T(8,128)(2,1)S(1)}, u32[]{:S(2)}, u32[]{:S(2)}) collective-permute-start(bf16[48,2048]{1,0:T(8,128)(2,1)S(1)} %bitcast.85), channel_id=1, source_target_pairs={{0,16},{16,0},{1,17},{17,1},{2,18},{18,2},{3,19},{19,3},{4,20},{20... | collective-permute-start | bytes 589832 | tf_op jit(solution)/shard_map/ppermute | solution.py:52
  9.4 8.6 %collective-permute-done = bf16[48,2048]{1,0:T(8,128)(2,1)S(1)} collective-permute-done((bf16[48,2048]{1,0:T(8,128)(2,1)S(1)}, bf16[48,2048]{1,0:T(8,128)(2,1)S(1)}, u32[]{:S(2)}, u32[]{:S(2)}) %collective-permute-start) | collective-permute-done | bytes 196640 | tf_op jit(solution)/shard_map/ppermute | solution.py:52
  18.1 1.3 broadcast_in_dim.27
  19.4 4.5 %all-to-all-start = ((bf16[4,96,2048]{2,1,0:T(8,128)(2,1)}), bf16[4,96,2048]{2,1,0:T(8,128)(2,1)}, u32[]{:S(2)}, u32[]{:S(2)}) async-start(bf16[4,96,2048]{2,1,0:T(8,128)(2,1)} %broadcast_in_dim.27), calls=%async_computation | async-start | bytes 3145728 | tf_op jit(solution)/shard_map/all_to_all | solution.py:143
  24.0 2.5 %collective-permute-start.1 = (f32[12,16]{0,1:T(8,128)S(1)}, f32[12,16]{0,1:T(8,128)S(1)}, u32[]{:S(2)}, u32[]{:S(2)}) collective-permute-start(f32[12,16]{0,1:T(8,128)S(1)} %pad_maximum_fusion), channel_id=1, source_target_pairs={{0,16},{16,0},{1,17},{17,1},{2,18},{18,2},{3,19},{19,3},{4,20},{20... | collective-permute-start | bytes 2312 | tf_op jit(solution)/shard_map/ppermute | solution.py:52
  26.5 13.3 %collective-permute-done.1 = f32[12,16]{0,1:T(8,128)S(1)} collective-permute-done((f32[12,16]{0,1:T(8,128)S(1)}, f32[12,16]{0,1:T(8,128)S(1)}, u32[]{:S(2)}, u32[]{:S(2)}) %collective-permute-start.1) | collective-permute-done | bytes 800 | tf_op jit(solution)/shard_map/ppermute | solution.py:52
  39.8 0.1 pad_add_fusion.1
  39.9 0.1 copy.63
  40.0 0.1 copy.64
  40.0 0.1 sub.40
  40.2 0.6 reduce-window.6
  40.7 0.2 slice_reduce_fusion
  41.0 1.0 all-to-all-done
  42.0 2.4 %fusion.25 = bf16[4,96,512]{2,1,0:T(8,128)(2,1)S(1)} fusion(bf16[4,96,2048]{2,1,0:T(8,128)(2,1)} %all-to-all-done, bf16[2048,512]{1,0:T(8,128)(2,1)S(1)} %copy-done), kind=kOutput, calls=%fused_computation.18 | convolution fusion | flops 805502976 | bytes 4063232 | tf_op jit(solution)/shard_map/sqd,df->sqf/dot_general | solution.py:144
  44.4 0.3 copy.57
  44.7 0.9 copy.71
  45.6 8.7 %all-to-all-start.1 = ((bf16[32,12,512]{2,1,0:T(8,128)(2,1)}), bf16[32,12,512]{2,1,0:T(8,128)(2,1)S(1)}, u32[]{:S(2)}, u32[]{:S(2)}) async-start(bf16[32,12,512]{2,1,0:T(8,128)(2,1)} %bitcast.6), calls=%async_computation.1 | async-start | bytes 1048576 | tf_op jit(solution)/shard_map/all_to_all | solution.py:150
  54.3 0.1 bitcast_bitcast_fusion
  54.4 0.1 reduce_sum.72
  54.5 0.1 gt.17
  54.7 13.8 %all-to-all-done.1 = bf16[32,12,512]{2,1,0:T(8,128)(2,1)S(1)} async-done(((bf16[32,12,512]{2,1,0:T(8,128)(2,1)}), bf16[32,12,512]{2,1,0:T(8,128)(2,1)S(1)}, u32[]{:S(2)}, u32[]{:S(2)}) %all-to-all-start.1) | async-done | bytes 393248 | tf_op jit(solution)/shard_map/all_to_all | solution.py:150
  68.5 0.1 convert_reduce_fusion
  68.6 0.1 copy.60
  68.8 0.2 copy.77
  69.0 0.2 fusion.33
  69.2 0.1 fusion.35
  69.3 0.7 fusion.29
  70.1 8.0 %collective-permute-done.2 = bf16[12,4096]{1,0:T(8,128)(2,1)S(1)} collective-permute-done((bf16[12,4096]{1,0:T(8,128)(2,1)S(1)}, bf16[12,4096]{1,0:T(8,128)(2,1)S(1)}, u32[]{:S(2)}, u32[]{:S(2)}) %collective-permute-start.2) | collective-permute-done | bytes 98336 | tf_op jit(solution)/shard_map/ppermute | solution.py:52
  78.1 1.0 convolution_convert_fusion
  79.1 41.0 %all_to_all.20 = bf16[16,24,4096]{2,1,0:T(8,128)(2,1)S(1)} all-to-all(bf16[16,24,4096]{2,1,0:T(8,128)(2,1)S(1)} %convolution_convert_fusion), channel_id=1, replica_groups=mesh['zh'=2,'dl'=4,'tensor'=4] {'dl','tensor'}, dimensions={0} | all-to-all | bytes 6291456 | tf_op jit(solution)/shard_map/all_to_all | solution.py:92
  120.2 2.7 %fusion.4 = f32[16,24,768]{2,1,0:T(8,128)S(1)} fusion(bf16[16,24,4096]{2,1,0:T(8,128)(2,1)S(1)} %all_to_all.20, bf16[1,4096,768]{2,1,0:T(8,128)(2,1)S(1)} %bitcast.92), kind=kOutput, calls=%fused_computation.4 | convolution fusion | flops 2415919104 | bytes 10616832 | tf_op jit(solution)/shard_map/hcd,df->hcf/dot_general | solution.py:93
  123.0 2.8 %fusion.22 = bf16[16,24,768]{2,1,0:T(8,128)(2,1)S(1)} fusion(bf16[16,24,4096]{2,1,0:T(8,128)(2,1)S(1)} %all_to_all.20, bf16[1,4096,768]{2,1,0:T(8,128)(2,1)S(1)} %bitcast.94, f32[16,24,768]{2,1,0:T(8,128)S(1)} %fusion.4), kind=kOutput, calls=%fused_computation.17 | convolution fusion | flops 2417688576 | bytes 11206656 | tf_op jit(solution)/shard_map/hcd,df->hcf/dot_general | solution.py:94
  125.8 4.1 %fusion.6 = bf16[16,24,4096]{2,1,0:T(8,128)(2,1)} fusion(bf16[16,24,768]{2,1,0:T(8,128)(2,1)S(1)} %fusion.22, bf16[1,768,4096]{2,1,0:T(8,128)(2,1)S(1)} %bitcast.96), kind=kOutput, calls=%fused_computation.7 | convolution fusion | flops 2417491968 | bytes 10027008 | tf_op jit(solution)/shard_map/hcf,fd->hcd/dot_general | solution.py:97
  129.9 6.6 %all-to-all-start.3 = ((bf16[16,24,4096]{2,1,0:T(8,128)(2,1)}), bf16[16,24,4096]{2,1,0:T(8,128)(2,1)}, u32[]{:S(2)}, u32[]{:S(2)}) async-start(bf16[16,24,4096]{2,1,0:T(8,128)(2,1)} %fusion.6), calls=%async_computation.3 | async-start | bytes 6291456 | tf_op jit(solution)/shard_map/all_to_all | solution.py:100
  136.5 0.1 pad_maximum_fusion.2
  136.6 0.1 copy.61
  136.7 0.1 copy.62
  136.8 46.6 %all-to-all-done.3 = bf16[16,24,4096]{2,1,0:T(8,128)(2,1)} async-done(((bf16[16,24,4096]{2,1,0:T(8,128)(2,1)}), bf16[16,24,4096]{2,1,0:T(8,128)(2,1)}, u32[]{:S(2)}, u32[]{:S(2)}) %all-to-all-start.3) | async-done | bytes 3145760 | tf_op jit(solution)/shard_map/all_to_all | solution.py:100
  183.4 4.0 %fusion.14 = f32[24,4096]{1,0:T(8,128)S(1)} fusion(bf16[16,24,4096]{2,1,0:T(8,128)(2,1)} %all-to-all-done.3, f32[24,8]{1,0:T(8,128)S(1)} %broadcast_select_fusion, s32[24,8]{1,0:T(8,128)S(1)} %add_select_fusion, s32[24,16]{0,1:T(8,128)S(1)} %multiply_add_fusion.1), kind=kOutput, calls=%fused_computation.15 | convolution fusion | flops 605528064 | bytes 3542016 | tf_op jit(solution)/shard_map/hcp,hcd->pd/dot_general | solution.py:101
  187.5 1.0 collective-permute-start.3
  188.5 8.2 %collective-permute-done.3 = bf16[12,4096]{1,0:T(8,128)(2,1)S(1)} collective-permute-done((bf16[12,4096]{1,0:T(8,128)(2,1)S(1)}, bf16[12,4096]{1,0:T(8,128)(2,1)S(1)}, u32[]{:S(2)}, u32[]{:S(2)}) %collective-permute-start.3) | collective-permute-done | bytes 98336 | tf_op jit(solution)/shard_map/ppermute | solution.py:52
  196.7 0.7 add_convert_fusion
  (55 shorter events, 0.6 us)
Async XLA Ops:
  0.6 41.3 %copy-start = (bf16[2048,512]{1,0:T(8,128)(2,1)S(1)}, bf16[2048,512]{1,0:T(8,128)(2,1)}, u32[]{:S(2)}) copy-start(bf16[2048,512]{1,0:T(8,128)(2,1)} %param.21) | copy-start | bytes 6291460
  0.6 5.6 %copy-start.6 = (bf16[48,128]{1,0:T(8,128)(2,1)S(1)}, bf16[48,128]{1,0:T(8,128)(2,1)}, u32[]{:S(2)}) copy-start(bf16[48,128]{1,0:T(8,128)(2,1)} %param.16) | copy-start | bytes 36868
  0.7 5.6 %copy-start.7 = (bf16[48,128,128]{2,1,0:T(8,128)(2,1)S(1)}, bf16[48,128,128]{2,1,0:T(8,128)(2,1)}, u32[]{:S(2)}) copy-start(bf16[48,128,128]{2,1,0:T(8,128)(2,1)} %param.18) | copy-start | bytes 4718596
  6.9 17.0 %copy-start.4 = (s32[12,8]{0,1:T(8,128)S(1)}, s32[12,8]{0,1:T(8,128)}, u32[]{:S(2)}) copy-start(s32[12,8]{0,1:T(8,128)} %param.23) | copy-start | bytes 1156
  6.9 17.0 %copy-start.5 = (f32[12,8]{0,1:T(8,128)S(1)}, f32[12,8]{0,1:T(8,128)}, u32[]{:S(2)}) copy-start(f32[12,8]{0,1:T(8,128)} %param.24) | copy-start | bytes 1156
  7.0 11.0 %collective-permute-start = (bf16[48,2048]{1,0:T(8,128)(2,1)S(1)}, bf16[48,2048]{1,0:T(8,128)(2,1)S(1)}, u32[]{:S(2)}, u32[]{:S(2)}) collective-permute-start(bf16[48,2048]{1,0:T(8,128)(2,1)S(1)} %bitcast.85), channel_id=1, source_target_pairs={{0,16},{16,0},{1,17},{17,1},{2,18},{18,2},{3,19},{19,3},{4,20},{20... | collective-permute-start | bytes 589832 | tf_op jit(solution)/shard_map/ppermute | solution.py:52
  19.4 22.6 %all-to-all-start = ((bf16[4,96,2048]{2,1,0:T(8,128)(2,1)}), bf16[4,96,2048]{2,1,0:T(8,128)(2,1)}, u32[]{:S(2)}, u32[]{:S(2)}) async-start(bf16[4,96,2048]{2,1,0:T(8,128)(2,1)} %broadcast_in_dim.27), calls=%async_computation | async-start | bytes 3145728 | tf_op jit(solution)/shard_map/all_to_all | solution.py:143
  24.0 15.8 %collective-permute-start.1 = (f32[12,16]{0,1:T(8,128)S(1)}, f32[12,16]{0,1:T(8,128)S(1)}, u32[]{:S(2)}, u32[]{:S(2)}) collective-permute-start(f32[12,16]{0,1:T(8,128)S(1)} %pad_maximum_fusion), channel_id=1, source_target_pairs={{0,16},{16,0},{1,17},{17,1},{2,18},{18,2},{3,19},{19,3},{4,20},{20... | collective-permute-start | bytes 2312 | tf_op jit(solution)/shard_map/ppermute | solution.py:52
  44.3 24.6 %copy-start.2 = (bf16[12,4096]{1,0:T(8,128)(2,1)S(1)}, bf16[12,4096]{1,0:T(8,128)(2,1)}, u32[]{:S(2)}) copy-start(bf16[12,4096]{1,0:T(8,128)(2,1)} %param.20) | copy-start | bytes 294916
  44.4 24.8 %copy-start.3 = (f32[4096]{0:T(1024)S(1)}, f32[4096]{0:T(1024)}, u32[]{:S(2)}) copy-start(f32[4096]{0:T(1024)} %param.22) | copy-start | bytes 49156
  45.6 23.0 %all-to-all-start.1 = ((bf16[32,12,512]{2,1,0:T(8,128)(2,1)}), bf16[32,12,512]{2,1,0:T(8,128)(2,1)S(1)}, u32[]{:S(2)}, u32[]{:S(2)}) async-start(bf16[32,12,512]{2,1,0:T(8,128)(2,1)} %bitcast.6), calls=%async_computation.1 | async-start | bytes 1048576 | tf_op jit(solution)/shard_map/all_to_all | solution.py:150
  68.5 51.6 %slice-start = ((s8[6291456]{0:T(1024)(128)(4,1)}), s8[4194304]{0:T(1024)(128)(4,1)S(1)}, s32[]{:S(2)}) async-start(s8[6291456]{0:T(1024)(128)(4,1)} %bitcast.91), calls=%async_computation.4 | async-start | bytes 8388608
  69.1 51.0 %copy-start.1 = (bf16[12,4096]{1,0:T(8,128)(2,1)}, bf16[12,4096]{1,0:T(8,128)(2,1)S(1)}, u32[]{:S(2)}) copy-start(bf16[12,4096]{1,0:T(8,128)(2,1)S(1)} %get-tuple-element.5) | copy-start | bytes 294916
  69.3 8.8 %collective-permute-start.2 = (bf16[12,4096]{1,0:T(8,128)(2,1)S(1)}, bf16[12,4096]{1,0:T(8,128)(2,1)S(1)}, u32[]{:S(2)}, u32[]{:S(2)}) collective-permute-start(bf16[12,4096]{1,0:T(8,128)(2,1)S(1)} %fusion.35), channel_id=1, source_target_pairs={{0,16},{16,0},{1,17},{17,1},{2,18},{18,2},{3,19},{19,3},{4,20},{20... | collective-permute-start | bytes 294920 | tf_op jit(solution)/shard_map/ppermute | solution.py:52
  70.0 50.1 %slice-start.1 = ((s8[6291456]{0:T(1024)(128)(4,1)}), s8[2097152]{0:T(1024)(128)(4,1)S(1)}, s32[]{:S(2)}) async-start(s8[6291456]{0:T(1024)(128)(4,1)} %bitcast.91), calls=%async_computation.5 | async-start | bytes 4194304
  79.1 43.8 %slice-start.2 = ((s8[6291456]{0:T(1024)(128)(4,1)}), s8[4194304]{0:T(1024)(128)(4,1)S(1)}, s32[]{:S(2)}) async-start(s8[6291456]{0:T(1024)(128)(4,1)} %bitcast.93), calls=%async_computation.6 | async-start | bytes 8388608
  120.2 2.8 %slice-start.3 = ((s8[6291456]{0:T(1024)(128)(4,1)}), s8[2097152]{0:T(1024)(128)(4,1)S(1)}, s32[]{:S(2)}) async-start(s8[6291456]{0:T(1024)(128)(4,1)} %bitcast.93), calls=%async_computation.7 | async-start | bytes 4194304
  120.2 5.6 %slice-start.4 = ((s8[6291456]{0:T(1024)(128)(4,1)}), s8[4194304]{0:T(1024)(128)(4,1)S(1)}, s32[]{:S(2)}) async-start(s8[6291456]{0:T(1024)(128)(4,1)} %bitcast.95), calls=%async_computation.8 | async-start | bytes 8388608
  123.0 2.8 %slice-start.5 = ((s8[6291456]{0:T(1024)(128)(4,1)}), s8[2097152]{0:T(1024)(128)(4,1)S(1)}, s32[]{:S(2)}) async-start(s8[6291456]{0:T(1024)(128)(4,1)} %bitcast.95), calls=%async_computation.9 | async-start | bytes 4194304
  129.9 53.5 %all-to-all-start.3 = ((bf16[16,24,4096]{2,1,0:T(8,128)(2,1)}), bf16[16,24,4096]{2,1,0:T(8,128)(2,1)}, u32[]{:S(2)}, u32[]{:S(2)}) async-start(bf16[16,24,4096]{2,1,0:T(8,128)(2,1)} %fusion.6), calls=%async_computation.3 | async-start | bytes 6291456 | tf_op jit(solution)/shard_map/all_to_all | solution.py:100
  187.5 9.2 %collective-permute-start.3 = (bf16[12,4096]{1,0:T(8,128)(2,1)S(1)}, bf16[12,4096]{1,0:T(8,128)(2,1)S(1)}, u32[]{:S(2)}, u32[]{:S(2)}) collective-permute-start(bf16[12,4096]{1,0:T(8,128)(2,1)S(1)} %select_convert_fusion), channel_id=1, source_target_pairs={{0,16},{16,0},{1,17},{17,1},{2,18},{18,2},{3,19},{19,3},{4,20},{20... | collective-permute-start | bytes 294920 | tf_op jit(solution)/shard_map/ppermute | solution.py:52

commit v8 on v7

--- a/solution.py
+++ b/solution.py
@@ -133,20 +133,19 @@
     n_t = lax.axis_size("tensor")
     tok_here = hidden_in.shape[0]
     first = lax.axis_index("zh") == 0
-    other_heads = swap_halves(heads_out)
-    pair_heads = jnp.where(
-        first,
-        jnp.concatenate([heads_out, other_heads]),
-        jnp.concatenate([other_heads, heads_out]),
+
+    def project(block):
+        spread = jnp.broadcast_to(block[None], (n_dl,) + block.shape)
+        gathered = lax.all_to_all(spread, "dl", split_axis=0, concat_axis=0, tiled=True)
+        return jnp.einsum("sqd,df->sqf", gathered, out_weight, preferred_element_type=jnp.float32)
+
+    own_cols = project(heads_out)
+    other_cols = project(swap_halves(heads_out))
+    by_side = jnp.where(
+        first, jnp.stack([own_cols, other_cols]), jnp.stack([other_cols, own_cols])
     )
-    spread = jnp.broadcast_to(pair_heads[None], (n_dl,) + pair_heads.shape)
-    gathered = lax.all_to_all(spread, "dl", split_axis=0, concat_axis=0, tiled=True)
-    partial_cols = jnp.einsum(
-        "sqd,df->sqf", gathered, out_weight, preferred_element_type=jnp.float32
-    )
-    col_width = partial_cols.shape[-1]
-    by_dest = partial_cols.reshape(n_dl, 2, n_t, tok_here, col_width).transpose(1, 0, 2, 3, 4)
-    by_dest = by_dest.reshape(2 * n_dl * n_t, tok_here, col_width)
+    col_width = by_side.shape[-1]
+    by_dest = by_side.reshape(2 * n_dl * n_t, tok_here, col_width)
     arrived = lax.all_to_all(
         by_dest.astype(jnp.bfloat16), DP + ("tensor",), split_axis=0, concat_axis=0, tiled=True
     )

time: 198 us -> 193 us (0.975)
  waiting for transfers between devices: 99.6 us -> 96.2 us
  starting transfers between devices: 25.8 us -> 23.7 us
    ppermute x4, waiting for transfers between devices: 38.1 us -> 25.7 us  [swap_halves(): return lax.ppermute(x, 'zh', [(0, 1), (1, 0)])]
    all_to_all x1 -> x2, waiting for transfers between devices: 0.98 us -> 10 us  [project(): lax.all_to_all(spread, 'dl', split_axis=0, concat_axis=0, tiled=True)]
    all_to_all x1 -> x2, starting transfers between devices: 4.53 us -> 8.38 us  [project(): lax.all_to_all(spread, 'dl', split_axis=0, concat_axis=0, tiled=True)]
    all_to_all x1, starting transfers between devices: 8.75 us -> 5.18 us  [shards(): lax.all_to_all(by_dest.astype(jnp.bfloat16), DP + ('tensor',), split_axis...]
    ppermute x4, starting transfers between devices: 5.95 us -> 3.49 us  [swap_halves(): return lax.ppermute(x, 'zh', [(0, 1), (1, 0)])]
  transfers between devices with their start and end apart: 7 -> 8, of which waited for: 7 -> 7; matrix products, arithmetic and copies ran while one was open for 1% -> 2% of each run, Pallas kernels for 0% -> 0%
where the time goes in v8:
time: 193 us; the launch traced here: 192 us
  waiting for transfers between devices  96.2 us (50%)
  blocking collectives  41.1 us (21%)
  starting transfers between devices  23.7 us (12%)
  matrix products  20.9 us (11%)
  local copies, waits for them, and re-layouts  5.13 us (3%)
  other arithmetic  4.02 us (2%)
    all_to_all x1, waiting for transfers between devices, expert_layer(): lax.all_to_all(result, HALF, split_axis=0, concat_axis=0, tiled=True)  46.6 us
    all_to_all x1, blocking collectives, expert_layer(): lax.all_to_all(outgoing, HALF, split_axis=0, concat_axis=0, tiled=True)  41.1 us
    ppermute x4, waiting for transfers between devices, swap_halves(): return lax.ppermute(x, 'zh', [(0, 1), (1, 0)])  25.7 us
    all_to_all x1, waiting for transfers between devices, shards(): lax.all_to_all(by_dest.astype(jnp.bfloat16), DP + ('tensor',), split_axis...  13.8 us
    all_to_all x2, waiting for transfers between devices, project(): lax.all_to_all(spread, 'dl', split_axis=0, concat_axis=0, tiled=True)  10 us
    all_to_all x2, starting transfers between devices, project(): lax.all_to_all(spread, 'dl', split_axis=0, concat_axis=0, tiled=True)  8.38 us
    all_to_all x1, starting transfers between devices, expert_layer(): lax.all_to_all(result, HALF, split_axis=0, concat_axis=0, tiled=True)  6.59 us
    all_to_all x1, starting transfers between devices, shards(): lax.all_to_all(by_dest.astype(jnp.bfloat16), DP + ('tensor',), split_axis...  5.18 us
  transfers between devices with their start and end apart: 8, of which 7 were waited for; matrix products, arithmetic and copies ran while one was open for 2% of the time, Pallas kernels for 0%

profile of v8, /device:TPU:7, one launch (start us, length us, event | category | flops | bytes accessed | tf_op | source)
XLA Modules:
  0.0 192.0 jit_solution(15750188058736167304)
XLA Ops:
  0.7 0.9 iota_compare_fusion
  1.5 1.0 copy.53
  2.6 0.9 fusion.54
  3.5 2.4 %select_reduce_fusion = (f32[48,16]{1,0:T(8,128)S(1)}, f32[48,16,128]{2,1,0:T(8,128)S(1)}) fusion(pred[48,128]{1,0:T(8,128)(4,1)S(1)} %iota_compare_fusion, bf16[48,16,128]{2,1,0:T(8,128)(2,1)S(1)} %bitcast.90, bf16[48,128,128]{2,1,0:T(8,128)(2,1)} %param.17), kind=kOutput, calls=%fused_computation.33 | convolution fusion | flops 25459968 | bytes 2171904 | tf_op jit(solution)/shard_map/rkgd,rckd->rkgc/dot_general | solution.py:27
  5.9 0.3 fusion.38
  6.3 0.6 fusion.33
  7.0 1.0 broadcast_in_dim.29
  8.0 3.7 %all-to-all-start = ((bf16[4,48,2048]{2,1,0:T(8,128)(2,1)}), bf16[4,48,2048]{2,1,0:T(8,128)(2,1)S(1)}, u32[]{:S(2)}, u32[]{:S(2)}) async-start(bf16[4,48,2048]{2,1,0:T(8,128)(2,1)} %broadcast_in_dim.29), calls=%async_computation | async-start | bytes 1572864 | tf_op jit(solution)/shard_map/all_to_all | solution.py:139
  11.7 2.3 %collective-permute-start = (bf16[48,2048]{1,0:T(8,128)(2,1)S(1)}, bf16[48,2048]{1,0:T(8,128)(2,1)S(1)}, u32[]{:S(2)}, u32[]{:S(2)}) collective-permute-start(bf16[48,2048]{1,0:T(8,128)(2,1)S(1)} %bitcast.92), channel_id=1, source_target_pairs={{0,16},{16,0},{1,17},{17,1},{2,18},{18,2},{3,19},{19,3},{4,20},{20... | collective-permute-start | bytes 589832 | tf_op jit(solution)/shard_map/ppermute | solution.py:52
  14.0 0.1 collective-permute-start.1
  14.2 9.5 %collective-permute-done = bf16[48,2048]{1,0:T(8,128)(2,1)S(1)} collective-permute-done((bf16[48,2048]{1,0:T(8,128)(2,1)S(1)}, bf16[48,2048]{1,0:T(8,128)(2,1)S(1)}, u32[]{:S(2)}, u32[]{:S(2)}) %collective-permute-start) | collective-permute-done | bytes 196640 | tf_op jit(solution)/shard_map/ppermute | solution.py:52
  23.7 2.4 %all-to-all-done = bf16[4,48,2048]{2,1,0:T(8,128)(2,1)S(1)} async-done(((bf16[4,48,2048]{2,1,0:T(8,128)(2,1)}), bf16[4,48,2048]{2,1,0:T(8,128)(2,1)S(1)}, u32[]{:S(2)}, u32[]{:S(2)}) %all-to-all-start) | async-done | bytes 786464 | tf_op jit(solution)/shard_map/all_to_all | solution.py:139
  26.1 1.0 broadcast_in_dim.30
  27.1 4.6 %all-to-all-start.1 = ((bf16[4,48,2048]{2,1,0:T(8,128)(2,1)}), bf16[4,48,2048]{2,1,0:T(8,128)(2,1)}, u32[]{:S(2)}, u32[]{:S(2)}) async-start(bf16[4,48,2048]{2,1,0:T(8,128)(2,1)} %broadcast_in_dim.30), calls=%async_computation.1 | async-start | bytes 1572864 | tf_op jit(solution)/shard_map/all_to_all | solution.py:139
  31.7 0.1 pad_add_fusion.1
  31.8 0.1 copy.43
  31.9 0.1 copy.44
  32.0 0.1 sub.40
  32.1 0.6 reduce-window.6
  32.7 0.2 slice_reduce_fusion
  32.9 0.6 fusion.27
  33.5 7.6 %all-to-all-done.1 = bf16[4,48,2048]{2,1,0:T(8,128)(2,1)} async-done(((bf16[4,48,2048]{2,1,0:T(8,128)(2,1)}), bf16[4,48,2048]{2,1,0:T(8,128)(2,1)}, u32[]{:S(2)}, u32[]{:S(2)}) %all-to-all-start.1) | async-done | bytes 786464 | tf_op jit(solution)/shard_map/all_to_all | solution.py:139
  41.1 1.7 fusion.30
  42.9 0.9 convert_element_type.87
  43.8 5.2 %all-to-all-start.2 = ((bf16[32,12,512]{2,1,0:T(8,128)(2,1)}), bf16[32,12,512]{2,1,0:T(8,128)(2,1)S(1)}, u32[]{:S(2)}, u32[]{:S(2)}) async-start(bf16[32,12,512]{2,1,0:T(8,128)(2,1)} %convert_element_type.87), calls=%async_computation.2 | async-start | bytes 1048576 | tf_op jit(solution)/shard_map/all_to_all | solution.py:149
  49.1 0.1 reduce_sum.72
  49.2 0.1 gt.17
  49.4 13.8 %all-to-all-done.2 = bf16[32,12,512]{2,1,0:T(8,128)(2,1)S(1)} async-done(((bf16[32,12,512]{2,1,0:T(8,128)(2,1)}), bf16[32,12,512]{2,1,0:T(8,128)(2,1)S(1)}, u32[]{:S(2)}, u32[]{:S(2)}) %all-to-all-start.2) | async-done | bytes 393248 | tf_op jit(solution)/shard_map/all_to_all | solution.py:149
  63.2 0.1 convert_reduce_fusion
  63.3 0.1 copy.40
  63.4 0.2 copy.55
  63.6 0.2 fusion.39
  63.8 0.1 fusion.41
  64.0 0.7 fusion.34
  64.7 8.0 %collective-permute-done.2 = bf16[12,4096]{1,0:T(8,128)(2,1)S(1)} collective-permute-done((bf16[12,4096]{1,0:T(8,128)(2,1)S(1)}, bf16[12,4096]{1,0:T(8,128)(2,1)S(1)}, u32[]{:S(2)}, u32[]{:S(2)}) %collective-permute-start.2) | collective-permute-done | bytes 98336 | tf_op jit(solution)/shard_map/ppermute | solution.py:52
  72.7 1.0 convolution_convert_fusion
  73.7 41.1 %all_to_all.25 = bf16[16,24,4096]{2,1,0:T(8,128)(2,1)S(1)} all-to-all(bf16[16,24,4096]{2,1,0:T(8,128)(2,1)S(1)} %convolution_convert_fusion), channel_id=1, replica_groups=mesh['zh'=2,'dl'=4,'tensor'=4] {'dl','tensor'}, dimensions={0} | all-to-all | bytes 6291456 | tf_op jit(solution)/shard_map/all_to_all | solution.py:92
  114.8 2.7 %fusion.4 = f32[16,24,768]{2,1,0:T(8,128)S(1)} fusion(bf16[16,24,4096]{2,1,0:T(8,128)(2,1)S(1)} %all_to_all.25, bf16[1,4096,768]{2,1,0:T(8,128)(2,1)S(1)} %bitcast.98), kind=kOutput, calls=%fused_computation.4 | convolution fusion | flops 2415919104 | bytes 10616832 | tf_op jit(solution)/shard_map/hcd,df->hcf/dot_general | solution.py:93
  117.6 2.8 %fusion.24 = bf16[16,24,768]{2,1,0:T(8,128)(2,1)S(1)} fusion(bf16[16,24,4096]{2,1,0:T(8,128)(2,1)S(1)} %all_to_all.25, bf16[1,4096,768]{2,1,0:T(8,128)(2,1)S(1)} %bitcast.100, f32[16,24,768]{2,1,0:T(8,128)S(1)} %fusion.4), kind=kOutput, calls=%fused_computation.19 | convolution fusion | flops 2417688576 | bytes 11206656 | tf_op jit(solution)/shard_map/hcd,df->hcf/dot_general | solution.py:94
  120.4 4.1 %fusion.6 = bf16[16,24,4096]{2,1,0:T(8,128)(2,1)} fusion(bf16[16,24,768]{2,1,0:T(8,128)(2,1)S(1)} %fusion.24, bf16[1,768,4096]{2,1,0:T(8,128)(2,1)S(1)} %bitcast.102), kind=kOutput, calls=%fused_computation.7 | convolution fusion | flops 2417491968 | bytes 10027008 | tf_op jit(solution)/shard_map/hcf,fd->hcd/dot_general | solution.py:97
  124.6 6.6 %all-to-all-start.4 = ((bf16[16,24,4096]{2,1,0:T(8,128)(2,1)}), bf16[16,24,4096]{2,1,0:T(8,128)(2,1)}, u32[]{:S(2)}, u32[]{:S(2)}) async-start(bf16[16,24,4096]{2,1,0:T(8,128)(2,1)} %fusion.6), calls=%async_computation.4 | async-start | bytes 6291456 | tf_op jit(solution)/shard_map/all_to_all | solution.py:100
  131.2 0.1 pad_maximum_fusion.2
  131.3 0.1 copy.41
  131.4 46.6 %all-to-all-done.4 = bf16[16,24,4096]{2,1,0:T(8,128)(2,1)} async-done(((bf16[16,24,4096]{2,1,0:T(8,128)(2,1)}), bf16[16,24,4096]{2,1,0:T(8,128)(2,1)}, u32[]{:S(2)}, u32[]{:S(2)}) %all-to-all-start.4) | async-done | bytes 3145760 | tf_op jit(solution)/shard_map/all_to_all | solution.py:100
  178.1 4.0 %fusion.16 = f32[24,4096]{1,0:T(8,128)S(1)} fusion(bf16[16,24,4096]{2,1,0:T(8,128)(2,1)} %all-to-all-done.4, f32[24,8]{1,0:T(8,128)S(1)} %broadcast_select_fusion, s32[24,8]{1,0:T(8,128)S(1)} %add_select_fusion, s32[24,16]{0,1:T(8,128)S(1)} %multiply_add_fusion.1), kind=kOutput, calls=%fused_computation.17 | convolution fusion | flops 605528064 | bytes 3542016 | tf_op jit(solution)/shard_map/hcp,hcd->pd/dot_general | solution.py:101
  182.1 1.0 collective-permute-start.3
  183.1 8.2 %collective-permute-done.3 = bf16[12,4096]{1,0:T(8,128)(2,1)S(1)} collective-permute-done((bf16[12,4096]{1,0:T(8,128)(2,1)S(1)}, bf16[12,4096]{1,0:T(8,128)(2,1)S(1)}, u32[]{:S(2)}, u32[]{:S(2)}) %collective-permute-start.3) | collective-permute-done | bytes 98336 | tf_op jit(solution)/shard_map/ppermute | solution.py:52
  191.3 0.7 add_convert_fusion
  (58 shorter events, 0.7 us)
Async XLA Ops:
  0.6 32.3 %copy-start = (bf16[2048,512]{1,0:T(8,128)(2,1)S(1)}, bf16[2048,512]{1,0:T(8,128)(2,1)}, u32[]{:S(2)}) copy-start(bf16[2048,512]{1,0:T(8,128)(2,1)} %param.21) | copy-start | bytes 6291460
  0.6 5.7 %copy-start.6 = (bf16[48,128]{1,0:T(8,128)(2,1)S(1)}, bf16[48,128]{1,0:T(8,128)(2,1)}, u32[]{:S(2)}) copy-start(bf16[48,128]{1,0:T(8,128)(2,1)} %param.16) | copy-start | bytes 36868
  0.7 5.7 %copy-start.7 = (bf16[48,128,128]{2,1,0:T(8,128)(2,1)S(1)}, bf16[48,128,128]{2,1,0:T(8,128)(2,1)}, u32[]{:S(2)}) copy-start(bf16[48,128,128]{2,1,0:T(8,128)(2,1)} %param.18) | copy-start | bytes 4718596
  6.2 7.8 %copy-start.4 = (s32[12,8]{0,1:T(8,128)S(1)}, s32[12,8]{0,1:T(8,128)}, u32[]{:S(2)}) copy-start(s32[12,8]{0,1:T(8,128)} %param.23) | copy-start | bytes 1156
  6.3 7.8 %copy-start.5 = (f32[12,8]{0,1:T(8,128)S(1)}, f32[12,8]{0,1:T(8,128)}, u32[]{:S(2)}) copy-start(f32[12,8]{0,1:T(8,128)} %param.24) | copy-start | bytes 1156
  8.0 18.1 %all-to-all-start = ((bf16[4,48,2048]{2,1,0:T(8,128)(2,1)}), bf16[4,48,2048]{2,1,0:T(8,128)(2,1)S(1)}, u32[]{:S(2)}, u32[]{:S(2)}) async-start(bf16[4,48,2048]{2,1,0:T(8,128)(2,1)} %broadcast_in_dim.29), calls=%async_computation | async-start | bytes 1572864 | tf_op jit(solution)/shard_map/all_to_all | solution.py:139
  11.7 12.0 %collective-permute-start = (bf16[48,2048]{1,0:T(8,128)(2,1)S(1)}, bf16[48,2048]{1,0:T(8,128)(2,1)S(1)}, u32[]{:S(2)}, u32[]{:S(2)}) collective-permute-start(bf16[48,2048]{1,0:T(8,128)(2,1)S(1)} %bitcast.92), channel_id=1, source_target_pairs={{0,16},{16,0},{1,17},{17,1},{2,18},{18,2},{3,19},{19,3},{4,20},{20... | collective-permute-start | bytes 589832 | tf_op jit(solution)/shard_map/ppermute | solution.py:52
  14.0 17.7 %collective-permute-start.1 = (f32[12,16]{0,1:T(8,128)S(1)}, f32[12,16]{0,1:T(8,128)S(1)}, u32[]{:S(2)}, u32[]{:S(2)}) collective-permute-start(f32[12,16]{0,1:T(8,128)S(1)} %pad_maximum_fusion), channel_id=1, source_target_pairs={{0,16},{16,0},{1,17},{17,1},{2,18},{18,2},{3,19},{19,3},{4,20},{20... | collective-permute-start | bytes 2312 | tf_op jit(solution)/shard_map/ppermute | solution.py:52
  27.1 14.0 %all-to-all-start.1 = ((bf16[4,48,2048]{2,1,0:T(8,128)(2,1)}), bf16[4,48,2048]{2,1,0:T(8,128)(2,1)}, u32[]{:S(2)}, u32[]{:S(2)}) async-start(bf16[4,48,2048]{2,1,0:T(8,128)(2,1)} %broadcast_in_dim.30), calls=%async_computation.1 | async-start | bytes 1572864 | tf_op jit(solution)/shard_map/all_to_all | solution.py:139
  42.8 20.8 %copy-start.2 = (bf16[12,4096]{1,0:T(8,128)(2,1)S(1)}, bf16[12,4096]{1,0:T(8,128)(2,1)}, u32[]{:S(2)}) copy-start(bf16[12,4096]{1,0:T(8,128)(2,1)} %param.20) | copy-start | bytes 294916
  42.8 20.9 %copy-start.3 = (f32[4096]{0:T(1024)S(1)}, f32[4096]{0:T(1024)}, u32[]{:S(2)}) copy-start(f32[4096]{0:T(1024)} %param.22) | copy-start | bytes 49156
  43.8 19.4 %all-to-all-start.2 = ((bf16[32,12,512]{2,1,0:T(8,128)(2,1)}), bf16[32,12,512]{2,1,0:T(8,128)(2,1)S(1)}, u32[]{:S(2)}, u32[]{:S(2)}) async-start(bf16[32,12,512]{2,1,0:T(8,128)(2,1)} %convert_element_type.87), calls=%async_computation.2 | async-start | bytes 1048576 | tf_op jit(solution)/shard_map/all_to_all | solution.py:149
  63.2 51.6 %slice-start = ((s8[6291456]{0:T(1024)(128)(4,1)}), s8[4194304]{0:T(1024)(128)(4,1)S(1)}, s32[]{:S(2)}) async-start(s8[6291456]{0:T(1024)(128)(4,1)} %bitcast.97), calls=%async_computation.5 | async-start | bytes 8388608
  63.8 51.0 %copy-start.1 = (bf16[12,4096]{1,0:T(8,128)(2,1)}, bf16[12,4096]{1,0:T(8,128)(2,1)S(1)}, u32[]{:S(2)}) copy-start(bf16[12,4096]{1,0:T(8,128)(2,1)S(1)} %get-tuple-element.5) | copy-start | bytes 294916
  63.9 8.8 %collective-permute-start.2 = (bf16[12,4096]{1,0:T(8,128)(2,1)S(1)}, bf16[12,4096]{1,0:T(8,128)(2,1)S(1)}, u32[]{:S(2)}, u32[]{:S(2)}) collective-permute-start(bf16[12,4096]{1,0:T(8,128)(2,1)S(1)} %fusion.41), channel_id=1, source_target_pairs={{0,16},{16,0},{1,17},{17,1},{2,18},{18,2},{3,19},{19,3},{4,20},{20... | collective-permute-start | bytes 294920 | tf_op jit(solution)/shard_map/ppermute | solution.py:52
  64.7 50.1 %slice-start.1 = ((s8[6291456]{0:T(1024)(128)(4,1)}), s8[2097152]{0:T(1024)(128)(4,1)S(1)}, s32[]{:S(2)}) async-start(s8[6291456]{0:T(1024)(128)(4,1)} %bitcast.97), calls=%async_computation.6 | async-start | bytes 4194304
  73.7 43.9 %slice-start.2 = ((s8[6291456]{0:T(1024)(128)(4,1)}), s8[4194304]{0:T(1024)(128)(4,1)S(1)}, s32[]{:S(2)}) async-start(s8[6291456]{0:T(1024)(128)(4,1)} %bitcast.99), calls=%async_computation.7 | async-start | bytes 8388608
  114.8 2.8 %slice-start.3 = ((s8[6291456]{0:T(1024)(128)(4,1)}), s8[2097152]{0:T(1024)(128)(4,1)S(1)}, s32[]{:S(2)}) async-start(s8[6291456]{0:T(1024)(128)(4,1)} %bitcast.99), calls=%async_computation.8 | async-start | bytes 4194304
  114.8 5.6 %slice-start.4 = ((s8[6291456]{0:T(1024)(128)(4,1)}), s8[4194304]{0:T(1024)(128)(4,1)S(1)}, s32[]{:S(2)}) async-start(s8[6291456]{0:T(1024)(128)(4,1)} %bitcast.101), calls=%async_computation.9 | async-start | bytes 8388608
  117.6 2.8 %slice-start.5 = ((s8[6291456]{0:T(1024)(128)(4,1)}), s8[2097152]{0:T(1024)(128)(4,1)S(1)}, s32[]{:S(2)}) async-start(s8[6291456]{0:T(1024)(128)(4,1)} %bitcast.101), calls=%async_computation.10 | async-start | bytes 4194304
  124.6 53.5 %all-to-all-start.4 = ((bf16[16,24,4096]{2,1,0:T(8,128)(2,1)}), bf16[16,24,4096]{2,1,0:T(8,128)(2,1)}, u32[]{:S(2)}, u32[]{:S(2)}) async-start(bf16[16,24,4096]{2,1,0:T(8,128)(2,1)} %fusion.6), calls=%async_computation.4 | async-start | bytes 6291456 | tf_op jit(solution)/shard_map/all_to_all | solution.py:100
  182.1 9.2 %collective-permute-start.3 = (bf16[12,4096]{1,0:T(8,128)(2,1)S(1)}, bf16[12,4096]{1,0:T(8,128)(2,1)S(1)}, u32[]{:S(2)}, u32[]{:S(2)}) collective-permute-start(bf16[12,4096]{1,0:T(8,128)(2,1)S(1)} %select_convert_fusion), channel_id=1, source_target_pairs={{0,16},{16,0},{1,17},{17,1},{2,18},{18,2},{3,19},{19,3},{4,20},{20... | collective-permute-start | bytes 294920 | tf_op jit(solution)/shard_map/ppermute | solution.py:52

commit v9 on v8

--- a/solution.py
+++ b/solution.py
@@ -64,14 +64,8 @@
     packed = swap_halves(jnp.concatenate([route_ids.astype(jnp.float32), route_weight], axis=1))
     other_ids = packed[:, :chosen_count].astype(jnp.int32)
     other_weight = packed[:, chosen_count:]
-    first = side == 0
-    rows = jnp.where(first, jnp.concatenate([normed, other_rows]), jnp.concatenate([other_rows, normed]))
-    ids = jnp.where(first, jnp.concatenate([route_ids, other_ids]), jnp.concatenate([other_ids, route_ids]))
-    weights = jnp.where(
-        first,
-        jnp.concatenate([route_weight, other_weight]),
-        jnp.concatenate([other_weight, route_weight]),
-    )
+    rows = jnp.concatenate([normed, other_rows])
+    ids = jnp.concatenate([route_ids, other_ids])
     held = 2 * tok_here
     pair_count = held * chosen_count
     local_ids = ids.reshape(pair_count) - side * n_half
@@ -98,18 +92,17 @@
         "hcf,fd->hcd", activation, w_down[0], preferred_element_type=jnp.float32
     ).astype(jnp.bfloat16)
     returned = lax.all_to_all(result, HALF, split_axis=0, concat_axis=0, tiled=True)
-    pair_rows = jnp.einsum(
-        "hcp,hcd->pd",
-        placement.reshape(n_half, capacity, pair_count),
-        returned,
-        preferred_element_type=jnp.float32,
-    )
-    weighted = weights[..., None] * pair_rows.reshape(held, chosen_count, width)
-    partial = jnp.sum(weighted, axis=1)
-    mine = jnp.where(first, partial[:tok_here], partial[tok_here:])
-    theirs = jnp.where(first, partial[tok_here:], partial[:tok_here])
-    sent = swap_halves(theirs.astype(jnp.bfloat16)).astype(jnp.float32)
-    return (mine + sent).astype(jnp.bfloat16)
+    placement = placement.reshape(n_half, capacity, 2, tok_here * chosen_count)
+
+    def combine(block, weight):
+        pair_rows = jnp.einsum(
+            "hcp,hcd->pd", placement[:, :, block], returned, preferred_element_type=jnp.float32
+        )
+        weighted = weight[..., None] * pair_rows.reshape(tok_here, chosen_count, width)
+        return jnp.sum(weighted, axis=1)
+
+    sent = swap_halves(combine(1, other_weight).astype(jnp.bfloat16)).astype(jnp.float32)
+    return (combine(0, route_weight) + sent).astype(jnp.bfloat16)
 
 
 def shards(

time: 193 us -> 191 us (0.990)
  waiting for transfers between devices: 96.2 us -> 91.8 us
    ppermute x4, waiting for transfers between devices: 25.7 us -> 22.5 us  [swap_halves(): return lax.ppermute(x, 'zh', [(0, 1), (1, 0)])]
    dot_general x1 -> x2, matrix products: 4 us -> 5.97 us  [combine(): jnp.einsum('hcp,hcd->pd', placement[:, :, block], returned, preferred_ele...]
  transfers between devices with their start and end apart: 8 -> 8, of which waited for: 7 -> 7; matrix products, arithmetic and copies ran while one was open for 2% -> 4% of each run, Pallas kernels for 0% -> 0%
where the time goes in v9:
time: 191 us
  waiting for transfers between devices  91.8 us (48%)
  blocking collectives  41 us (21%)
  starting transfers between devices  23.7 us (12%)
  matrix products  22.8 us (12%)
  local copies, waits for them, and re-layouts  6.19 us (3%)
  other arithmetic  4.01 us (2%)
    all_to_all x1, waiting for transfers between devices, expert_layer(): lax.all_to_all(result, HALF, split_axis=0, concat_axis=0, tiled=True)  45.4 us
    all_to_all x1, blocking collectives, expert_layer(): lax.all_to_all(outgoing, HALF, split_axis=0, concat_axis=0, tiled=True)  41 us
    ppermute x4, waiting for transfers between devices, swap_halves(): return lax.ppermute(x, 'zh', [(0, 1), (1, 0)])  22.5 us
    all_to_all x1, waiting for transfers between devices, shards(): lax.all_to_all(by_dest.astype(jnp.bfloat16), DP + ('tensor',), split_axis...  13.8 us
    all_to_all x2, waiting for transfers between devices, project(): lax.all_to_all(spread, 'dl', split_axis=0, concat_axis=0, tiled=True)  10.1 us
    all_to_all x2, starting transfers between devices, project(): lax.all_to_all(spread, 'dl', split_axis=0, concat_axis=0, tiled=True)  8.39 us
    all_to_all x1, starting transfers between devices, expert_layer(): lax.all_to_all(result, HALF, split_axis=0, concat_axis=0, tiled=True)  6.6 us
    dot_general x2, matrix products, combine(): jnp.einsum('hcp,hcd->pd', placement[:, :, block], returned, preferred_ele...  5.97 us
  transfers between devices with their start and end apart: 8, of which 7 were waited for; matrix products, arithmetic and copies ran while one was open for 4% of the time, Pallas kernels for 0%

profile of v9, /device:TPU:7, one launch (start us, length us, event | category | flops | bytes accessed | tf_op | source)
XLA Modules:
  0.0 190.5 jit_solution(3895809957488062035)
XLA Ops:
  0.7 0.9 iota_compare_fusion
  1.5 1.0 copy.56
  2.6 0.9 fusion.50
  3.5 2.4 %select_reduce_fusion = (f32[48,16]{1,0:T(8,128)S(1)}, f32[48,16,128]{2,1,0:T(8,128)S(1)}) fusion(pred[48,128]{1,0:T(8,128)(4,1)S(1)} %iota_compare_fusion, bf16[48,16,128]{2,1,0:T(8,128)(2,1)S(1)} %bitcast.109, bf16[48,128,128]{2,1,0:T(8,128)(2,1)} %param.17), kind=kOutput, calls=%fused_computation.35 | convolution fusion | flops 25459968 | bytes 2171904 | tf_op jit(solution)/shard_map/rkgd,rckd->rkgc/dot_general | solution.py:27
  5.9 0.3 fusion.40
  6.3 0.6 fusion.31
  7.0 1.0 broadcast_in_dim.31
  8.0 3.7 %all-to-all-start = ((bf16[4,48,2048]{2,1,0:T(8,128)(2,1)}), bf16[4,48,2048]{2,1,0:T(8,128)(2,1)S(1)}, u32[]{:S(2)}, u32[]{:S(2)}) async-start(bf16[4,48,2048]{2,1,0:T(8,128)(2,1)} %broadcast_in_dim.31), calls=%async_computation | async-start | bytes 1572864 | tf_op jit(solution)/shard_map/all_to_all | solution.py:132
  11.7 2.3 %collective-permute-start = (bf16[48,2048]{1,0:T(8,128)(2,1)S(1)}, bf16[48,2048]{1,0:T(8,128)(2,1)S(1)}, u32[]{:S(2)}, u32[]{:S(2)}) collective-permute-start(bf16[48,2048]{1,0:T(8,128)(2,1)S(1)} %bitcast.111), channel_id=1, source_target_pairs={{0,16},{16,0},{1,17},{17,1},{2,18},{18,2},{3,19},{19,3},{4,20},{20... | collective-permute-start | bytes 589832 | tf_op jit(solution)/shard_map/ppermute | solution.py:52
  14.0 0.1 collective-permute-start.1
  14.2 9.5 %collective-permute-done = bf16[48,2048]{1,0:T(8,128)(2,1)S(1)} collective-permute-done((bf16[48,2048]{1,0:T(8,128)(2,1)S(1)}, bf16[48,2048]{1,0:T(8,128)(2,1)S(1)}, u32[]{:S(2)}, u32[]{:S(2)}) %collective-permute-start) | collective-permute-done | bytes 196640 | tf_op jit(solution)/shard_map/ppermute | solution.py:52
  23.7 2.4 %all-to-all-done = bf16[4,48,2048]{2,1,0:T(8,128)(2,1)S(1)} async-done(((bf16[4,48,2048]{2,1,0:T(8,128)(2,1)}), bf16[4,48,2048]{2,1,0:T(8,128)(2,1)S(1)}, u32[]{:S(2)}, u32[]{:S(2)}) %all-to-all-start) | async-done | bytes 786464 | tf_op jit(solution)/shard_map/all_to_all | solution.py:132
  26.1 1.0 broadcast_in_dim.32
  27.1 4.6 %all-to-all-start.1 = ((bf16[4,48,2048]{2,1,0:T(8,128)(2,1)}), bf16[4,48,2048]{2,1,0:T(8,128)(2,1)}, u32[]{:S(2)}, u32[]{:S(2)}) async-start(bf16[4,48,2048]{2,1,0:T(8,128)(2,1)} %broadcast_in_dim.32), calls=%async_computation.1 | async-start | bytes 1572864 | tf_op jit(solution)/shard_map/all_to_all | solution.py:132
  31.9 0.1 sub.40
  32.0 0.6 reduce-window.6
  32.6 0.2 slice_reduce_fusion
  32.8 0.6 fusion.25
  33.4 7.7 %all-to-all-done.1 = bf16[4,48,2048]{2,1,0:T(8,128)(2,1)} async-done(((bf16[4,48,2048]{2,1,0:T(8,128)(2,1)}), bf16[4,48,2048]{2,1,0:T(8,128)(2,1)}, u32[]{:S(2)}, u32[]{:S(2)}) %all-to-all-start.1) | async-done | bytes 786464 | tf_op jit(solution)/shard_map/all_to_all | solution.py:132
  41.1 1.7 fusion.28
  42.9 0.9 convert_element_type.87
  43.8 5.2 %all-to-all-start.2 = ((bf16[32,12,512]{2,1,0:T(8,128)(2,1)}), bf16[32,12,512]{2,1,0:T(8,128)(2,1)S(1)}, u32[]{:S(2)}, u32[]{:S(2)}) async-start(bf16[32,12,512]{2,1,0:T(8,128)(2,1)} %convert_element_type.87), calls=%async_computation.2 | async-start | bytes 1048576 | tf_op jit(solution)/shard_map/all_to_all | solution.py:142
  49.2 0.1 gt.20
  49.3 13.8 %all-to-all-done.2 = bf16[32,12,512]{2,1,0:T(8,128)(2,1)S(1)} async-done(((bf16[32,12,512]{2,1,0:T(8,128)(2,1)}), bf16[32,12,512]{2,1,0:T(8,128)(2,1)S(1)}, u32[]{:S(2)}, u32[]{:S(2)}) %all-to-all-start.2) | async-done | bytes 393248 | tf_op jit(solution)/shard_map/all_to_all | solution.py:142
  63.2 0.1 convert_reduce_fusion
  63.2 0.1 copy.39
  63.4 0.2 copy.58
  63.6 0.2 fusion.41
  63.8 0.1 fusion.43
  64.0 0.7 fusion.32
  64.7 8.0 %collective-permute-done.2 = bf16[12,4096]{1,0:T(8,128)(2,1)S(1)} collective-permute-done((bf16[12,4096]{1,0:T(8,128)(2,1)S(1)}, bf16[12,4096]{1,0:T(8,128)(2,1)S(1)}, u32[]{:S(2)}, u32[]{:S(2)}) %collective-permute-start.2) | collective-permute-done | bytes 98336 | tf_op jit(solution)/shard_map/ppermute | solution.py:52
  72.7 1.0 convolution_convert_fusion
  73.7 41.0 %all_to_all.25 = bf16[16,24,4096]{2,1,0:T(8,128)(2,1)S(1)} all-to-all(bf16[16,24,4096]{2,1,0:T(8,128)(2,1)S(1)} %convolution_convert_fusion), channel_id=1, replica_groups=mesh['zh'=2,'dl'=4,'tensor'=4] {'dl','tensor'}, dimensions={0} | all-to-all | bytes 6291456 | tf_op jit(solution)/shard_map/all_to_all | solution.py:86
  114.8 2.7 %fusion.4 = f32[16,24,768]{2,1,0:T(8,128)S(1)} fusion(bf16[16,24,4096]{2,1,0:T(8,128)(2,1)S(1)} %all_to_all.25, bf16[1,4096,768]{2,1,0:T(8,128)(2,1)S(1)} %bitcast.119), kind=kOutput, calls=%fused_computation.4 | convolution fusion | flops 2415919104 | bytes 10616832 | tf_op jit(solution)/shard_map/hcd,df->hcf/dot_general | solution.py:87
  117.6 2.8 %fusion.22 = bf16[16,24,768]{2,1,0:T(8,128)(2,1)S(1)} fusion(bf16[16,24,4096]{2,1,0:T(8,128)(2,1)S(1)} %all_to_all.25, bf16[1,4096,768]{2,1,0:T(8,128)(2,1)S(1)} %bitcast.121, f32[16,24,768]{2,1,0:T(8,128)S(1)} %fusion.4), kind=kOutput, calls=%fused_computation.21 | convolution fusion | flops 2417688576 | bytes 11206656 | tf_op jit(solution)/shard_map/hcd,df->hcf/dot_general | solution.py:88
  120.4 4.0 %fusion.6 = bf16[16,24,4096]{2,1,0:T(8,128)(2,1)} fusion(bf16[16,24,768]{2,1,0:T(8,128)(2,1)S(1)} %fusion.22, bf16[1,768,4096]{2,1,0:T(8,128)(2,1)S(1)} %bitcast.123), kind=kOutput, calls=%fused_computation.7 | convolution fusion | flops 2417491968 | bytes 10027008 | tf_op jit(solution)/shard_map/hcf,fd->hcd/dot_general | solution.py:91
  124.5 6.6 %all-to-all-start.4 = ((bf16[16,24,4096]{2,1,0:T(8,128)(2,1)}), bf16[16,24,4096]{2,1,0:T(8,128)(2,1)}, u32[]{:S(2)}, u32[]{:S(2)}) async-start(bf16[16,24,4096]{2,1,0:T(8,128)(2,1)} %fusion.6), calls=%async_computation.4 | async-start | bytes 6291456 | tf_op jit(solution)/shard_map/all_to_all | solution.py:94
  131.1 0.1 gt.19
  131.4 0.1 broadcast_compare_fusion
  131.6 0.4 copy.48
  132.0 0.1 copy.47
  132.1 0.4 copy.44
  132.5 45.4 %all-to-all-done.4 = bf16[16,24,4096]{2,1,0:T(8,128)(2,1)} async-done(((bf16[16,24,4096]{2,1,0:T(8,128)(2,1)}), bf16[16,24,4096]{2,1,0:T(8,128)(2,1)}, u32[]{:S(2)}, u32[]{:S(2)}) %all-to-all-start.4) | async-done | bytes 3145760 | tf_op jit(solution)/shard_map/all_to_all | solution.py:94
  177.9 3.0 %multiply_reduce_fusion = bf16[12,4096]{1,0:T(8,128)(2,1)S(1)} fusion(f32[12,8]{1,0:T(8,128)S(1)} %copy.47, bf16[16,24,4096]{2,1,0:T(8,128)(2,1)} %all-to-all-done.4, pred[12,8,24,16]{2,3,1,0:T(8,128)(4,1)S(1)} %bitcast.115), kind=kOutput, calls=%fused_computation.17 | convolution fusion | flops 302727168 | bytes 3281280 | tf_op jit(solution)/shard_map/hcp,hcd->pd/dot_general | solution.py:98
  180.9 1.0 collective-permute-start.3
  181.9 3.0 %fusion.19 = f32[12,4096]{1,0:T(8,128)S(1)} fusion(bf16[16,24,4096]{2,1,0:T(8,128)(2,1)} %all-to-all-done.4, f32[12,8]{1,0:T(8,128)S(1)} %copy.40, pred[12,8,24,16]{2,3,1,0:T(8,128)(4,1)S(1)} %bitcast.114), kind=kOutput, calls=%fused_computation.20 | convolution fusion | flops 302727168 | bytes 3379584 | tf_op jit(solution)/shard_map/hcp,hcd->pd/dot_general | solution.py:98
  184.9 4.9 %collective-permute-done.3 = bf16[12,4096]{1,0:T(8,128)(2,1)S(1)} collective-permute-done((bf16[12,4096]{1,0:T(8,128)(2,1)S(1)}, bf16[12,4096]{1,0:T(8,128)(2,1)S(1)}, u32[]{:S(2)}, u32[]{:S(2)}) %collective-permute-start.3) | collective-permute-done | bytes 98336 | tf_op jit(solution)/shard_map/ppermute | solution.py:52
  189.8 0.7 add_convert_fusion
  (62 shorter events, 1.1 us)
Async XLA Ops:
  0.6 32.2 %copy-start = (bf16[2048,512]{1,0:T(8,128)(2,1)S(1)}, bf16[2048,512]{1,0:T(8,128)(2,1)}, u32[]{:S(2)}) copy-start(bf16[2048,512]{1,0:T(8,128)(2,1)} %param.21) | copy-start | bytes 6291460
  0.6 5.6 %copy-start.6 = (bf16[48,128]{1,0:T(8,128)(2,1)S(1)}, bf16[48,128]{1,0:T(8,128)(2,1)}, u32[]{:S(2)}) copy-start(bf16[48,128]{1,0:T(8,128)(2,1)} %param.16) | copy-start | bytes 36868
  0.7 5.6 %copy-start.7 = (bf16[48,128,128]{2,1,0:T(8,128)(2,1)S(1)}, bf16[48,128,128]{2,1,0:T(8,128)(2,1)}, u32[]{:S(2)}) copy-start(bf16[48,128,128]{2,1,0:T(8,128)(2,1)} %param.18) | copy-start | bytes 4718596
  6.9 7.1 %copy-start.4 = (s32[12,8]{0,1:T(8,128)S(1)}, s32[12,8]{0,1:T(8,128)}, u32[]{:S(2)}) copy-start(s32[12,8]{0,1:T(8,128)} %param.23) | copy-start | bytes 1156
  6.9 7.1 %copy-start.5 = (f32[12,8]{0,1:T(8,128)S(1)}, f32[12,8]{0,1:T(8,128)}, u32[]{:S(2)}) copy-start(f32[12,8]{0,1:T(8,128)} %param.24) | copy-start | bytes 1156
  8.0 18.1 %all-to-all-start = ((bf16[4,48,2048]{2,1,0:T(8,128)(2,1)}), bf16[4,48,2048]{2,1,0:T(8,128)(2,1)S(1)}, u32[]{:S(2)}, u32[]{:S(2)}) async-start(bf16[4,48,2048]{2,1,0:T(8,128)(2,1)} %broadcast_in_dim.31), calls=%async_computation | async-start | bytes 1572864 | tf_op jit(solution)/shard_map/all_to_all | solution.py:132
  11.7 12.0 %collective-permute-start = (bf16[48,2048]{1,0:T(8,128)(2,1)S(1)}, bf16[48,2048]{1,0:T(8,128)(2,1)S(1)}, u32[]{:S(2)}, u32[]{:S(2)}) collective-permute-start(bf16[48,2048]{1,0:T(8,128)(2,1)S(1)} %bitcast.111), channel_id=1, source_target_pairs={{0,16},{16,0},{1,17},{17,1},{2,18},{18,2},{3,19},{19,3},{4,20},{20... | collective-permute-start | bytes 589832 | tf_op jit(solution)/shard_map/ppermute | solution.py:52
  14.0 17.7 %collective-permute-start.1 = (f32[12,16]{0,1:T(8,128)S(1)}, f32[12,16]{0,1:T(8,128)S(1)}, u32[]{:S(2)}, u32[]{:S(2)}) collective-permute-start(f32[12,16]{0,1:T(8,128)S(1)} %pad_maximum_fusion), channel_id=1, source_target_pairs={{0,16},{16,0},{1,17},{17,1},{2,18},{18,2},{3,19},{19,3},{4,20},{20... | collective-permute-start | bytes 2312 | tf_op jit(solution)/shard_map/ppermute | solution.py:52
  27.1 14.0 %all-to-all-start.1 = ((bf16[4,48,2048]{2,1,0:T(8,128)(2,1)}), bf16[4,48,2048]{2,1,0:T(8,128)(2,1)}, u32[]{:S(2)}, u32[]{:S(2)}) async-start(bf16[4,48,2048]{2,1,0:T(8,128)(2,1)} %broadcast_in_dim.32), calls=%async_computation.1 | async-start | bytes 1572864 | tf_op jit(solution)/shard_map/all_to_all | solution.py:132
  42.9 20.7 %copy-start.2 = (bf16[12,4096]{1,0:T(8,128)(2,1)S(1)}, bf16[12,4096]{1,0:T(8,128)(2,1)}, u32[]{:S(2)}) copy-start(bf16[12,4096]{1,0:T(8,128)(2,1)} %param.20) | copy-start | bytes 294916
  43.8 20.0 %copy-start.3 = (f32[4096]{0:T(1024)S(1)}, f32[4096]{0:T(1024)}, u32[]{:S(2)}) copy-start(f32[4096]{0:T(1024)} %param.22) | copy-start | bytes 49156
  43.8 19.4 %all-to-all-start.2 = ((bf16[32,12,512]{2,1,0:T(8,128)(2,1)}), bf16[32,12,512]{2,1,0:T(8,128)(2,1)S(1)}, u32[]{:S(2)}, u32[]{:S(2)}) async-start(bf16[32,12,512]{2,1,0:T(8,128)(2,1)} %convert_element_type.87), calls=%async_computation.2 | async-start | bytes 1048576 | tf_op jit(solution)/shard_map/all_to_all | solution.py:142
  63.2 51.6 %slice-start = ((s8[6291456]{0:T(1024)(128)(4,1)}), s8[4194304]{0:T(1024)(128)(4,1)S(1)}, s32[]{:S(2)}) async-start(s8[6291456]{0:T(1024)(128)(4,1)} %bitcast.118), calls=%async_computation.5 | async-start | bytes 8388608
  63.7 51.0 %copy-start.1 = (bf16[12,4096]{1,0:T(8,128)(2,1)}, bf16[12,4096]{1,0:T(8,128)(2,1)S(1)}, u32[]{:S(2)}) copy-start(bf16[12,4096]{1,0:T(8,128)(2,1)S(1)} %get-tuple-element.7) | copy-start | bytes 294916
  63.9 8.8 %collective-permute-start.2 = (bf16[12,4096]{1,0:T(8,128)(2,1)S(1)}, bf16[12,4096]{1,0:T(8,128)(2,1)S(1)}, u32[]{:S(2)}, u32[]{:S(2)}) collective-permute-start(bf16[12,4096]{1,0:T(8,128)(2,1)S(1)} %fusion.43), channel_id=1, source_target_pairs={{0,16},{16,0},{1,17},{17,1},{2,18},{18,2},{3,19},{19,3},{4,20},{20... | collective-permute-start | bytes 294920 | tf_op jit(solution)/shard_map/ppermute | solution.py:52
  64.7 50.1 %slice-start.1 = ((s8[6291456]{0:T(1024)(128)(4,1)}), s8[2097152]{0:T(1024)(128)(4,1)S(1)}, s32[]{:S(2)}) async-start(s8[6291456]{0:T(1024)(128)(4,1)} %bitcast.118), calls=%async_computation.6 | async-start | bytes 4194304
  73.7 43.9 %slice-start.2 = ((s8[6291456]{0:T(1024)(128)(4,1)}), s8[4194304]{0:T(1024)(128)(4,1)S(1)}, s32[]{:S(2)}) async-start(s8[6291456]{0:T(1024)(128)(4,1)} %bitcast.120), calls=%async_computation.7 | async-start | bytes 8388608
  114.8 2.8 %slice-start.3 = ((s8[6291456]{0:T(1024)(128)(4,1)}), s8[2097152]{0:T(1024)(128)(4,1)S(1)}, s32[]{:S(2)}) async-start(s8[6291456]{0:T(1024)(128)(4,1)} %bitcast.120), calls=%async_computation.8 | async-start | bytes 4194304
  114.8 5.6 %slice-start.4 = ((s8[6291456]{0:T(1024)(128)(4,1)}), s8[4194304]{0:T(1024)(128)(4,1)S(1)}, s32[]{:S(2)}) async-start(s8[6291456]{0:T(1024)(128)(4,1)} %bitcast.122), calls=%async_computation.9 | async-start | bytes 8388608
  117.6 2.8 %slice-start.5 = ((s8[6291456]{0:T(1024)(128)(4,1)}), s8[2097152]{0:T(1024)(128)(4,1)S(1)}, s32[]{:S(2)}) async-start(s8[6291456]{0:T(1024)(128)(4,1)} %bitcast.122), calls=%async_computation.10 | async-start | bytes 4194304
  124.5 53.5 %all-to-all-start.4 = ((bf16[16,24,4096]{2,1,0:T(8,128)(2,1)}), bf16[16,24,4096]{2,1,0:T(8,128)(2,1)}, u32[]{:S(2)}, u32[]{:S(2)}) async-start(bf16[16,24,4096]{2,1,0:T(8,128)(2,1)} %fusion.6), calls=%async_computation.4 | async-start | bytes 6291456 | tf_op jit(solution)/shard_map/all_to_all | solution.py:94
  180.9 8.9 %collective-permute-start.3 = (bf16[12,4096]{1,0:T(8,128)(2,1)S(1)}, bf16[12,4096]{1,0:T(8,128)(2,1)S(1)}, u32[]{:S(2)}, u32[]{:S(2)}) collective-permute-start(bf16[12,4096]{1,0:T(8,128)(2,1)S(1)} %multiply_reduce_fusion), channel_id=1, source_target_pairs={{0,16},{16,0},{1,17},{17,1},{2,18},{18,2},{3,19},{19,3},{4,20},{20... | collective-permute-start | bytes 294920 | tf_op jit(solution)/shard_map/ppermute | solution.py:52

commit v10 on v9

--- a/solution.py
+++ b/solution.py
@@ -91,13 +91,17 @@
     result = jnp.einsum(
         "hcf,fd->hcd", activation, w_down[0], preferred_element_type=jnp.float32
     ).astype(jnp.bfloat16)
-    returned = lax.all_to_all(result, HALF, split_axis=0, concat_axis=0, tiled=True)
-    placement = placement.reshape(n_half, capacity, 2, tok_here * chosen_count)
+    lanes = 128
+    used = min(capacity, 2 * max(2, 3 * tok_here * chosen_count // experts_all))
+    back = result[:, :used].reshape(n_half, used * (width // lanes), lanes)
+    returned = lax.all_to_all(back, HALF, split_axis=0, concat_axis=0, tiled=True)
+    returned = returned.reshape(n_half, used, width // lanes, lanes)
+    placement = placement.reshape(n_half, capacity, 2, tok_here * chosen_count)[:, :used]
 
     def combine(block, weight):
         pair_rows = jnp.einsum(
-            "hcp,hcd->pd", placement[:, :, block], returned, preferred_element_type=jnp.float32
-        )
+            "hcp,hcql->pql", placement[:, :, block], returned, preferred_element_type=jnp.float32
+        ).reshape(tok_here * chosen_count, width)
         weighted = weight[..., None] * pair_rows.reshape(tok_here, chosen_count, width)
         return jnp.sum(weighted, axis=1)
 

time: 191 us -> 191 us (level)
  local copies, waits for them, and re-layouts: 6.19 us -> 21 us
  waiting for transfers between devices: 91.8 us -> 78.9 us
  matrix products: 22.8 us -> 20.7 us
    all_to_all x1, waiting for transfers between devices: 45.4 us -> 31.1 us  [expert_layer(): lax.all_to_all(back, HALF, split_axis=0, concat_axis=0, tiled=True)]
    reshape x0 -> x2, local copies, waits for them, and re-layouts: none -> 8.32 us  [the longest x1 4.62 us: expert_layer(): back = result[:, :used].reshape(n_half, used * (width // lanes), lanes)]
    dot_general x3 -> x6, local copies, waits for them, and re-layouts: 0.89 us -> 7.29 us  [combine(): jnp.einsum('hcp,hcql->pql', placement[:, :, block], returned, preferred_e...]
    dot_general x2, matrix products: 5.97 us -> 3.88 us  [combine(): jnp.einsum('hcp,hcql->pql', placement[:, :, block], returned, preferred_e...]
where the time goes in v10:
time: 191 us; the launch traced here: 190 us
  waiting for transfers between devices  78.9 us (41%)
  blocking collectives  41 us (21%)
  starting transfers between devices  23.6 us (12%)
  local copies, waits for them, and re-layouts  21 us (11%)
  matrix products  20.7 us (11%)
  other arithmetic  4.01 us (2%)
    all_to_all x1, blocking collectives, expert_layer(): lax.all_to_all(outgoing, HALF, split_axis=0, concat_axis=0, tiled=True)  41 us
    all_to_all x1, waiting for transfers between devices, expert_layer(): lax.all_to_all(back, HALF, split_axis=0, concat_axis=0, tiled=True)  31.1 us
    ppermute x4, waiting for transfers between devices, swap_halves(): return lax.ppermute(x, 'zh', [(0, 1), (1, 0)])  24 us
    all_to_all x1, waiting for transfers between devices, shards(): lax.all_to_all(by_dest.astype(jnp.bfloat16), DP + ('tensor',), split_axis...  13.8 us
    all_to_all x2, waiting for transfers between devices, project(): lax.all_to_all(spread, 'dl', split_axis=0, concat_axis=0, tiled=True)  10.1 us
    all_to_all x2, starting transfers between devices, project(): lax.all_to_all(spread, 'dl', split_axis=0, concat_axis=0, tiled=True)  8.39 us
    dot_general x6, local copies, waits for them, and re-layouts, combine(): jnp.einsum('hcp,hcql->pql', placement[:, :, block], returned, preferred_e...  7.29 us
    all_to_all x1, starting transfers between devices, expert_layer(): lax.all_to_all(back, HALF, split_axis=0, concat_axis=0, tiled=True)  6.56 us
  transfers between devices with their start and end apart: 8, of which 7 were waited for; matrix products, arithmetic and copies ran while one was open for 4% of the time, Pallas kernels for 0%

profile of v10, /device:TPU:7, one launch (start us, length us, event | category | flops | bytes accessed | tf_op | source)
XLA Modules:
  0.0 190.5 jit_solution(781083788636098968)
XLA Ops:
  0.7 0.9 iota_compare_fusion
  1.5 1.0 copy.76
  2.6 0.9 fusion.41
  3.5 2.4 %select_reduce_fusion = (f32[48,16]{1,0:T(8,128)S(1)}, f32[48,16,128]{2,1,0:T(8,128)S(1)}) fusion(pred[48,128]{1,0:T(8,128)(4,1)S(1)} %iota_compare_fusion, bf16[48,16,128]{2,1,0:T(8,128)(2,1)S(1)} %bitcast.119, bf16[48,128,128]{2,1,0:T(8,128)(2,1)} %param.17), kind=kOutput, calls=%fused_computation.34 | convolution fusion | flops 25459968 | bytes 2171904 | tf_op jit(solution)/shard_map/rkgd,rckd->rkgc/dot_general | solution.py:27
  5.9 0.3 fusion.31
  6.3 0.6 fusion.28
  7.0 1.0 broadcast_in_dim.31
  8.0 3.7 %all-to-all-start = ((bf16[4,48,2048]{2,1,0:T(8,128)(2,1)}), bf16[4,48,2048]{2,1,0:T(8,128)(2,1)S(1)}, u32[]{:S(2)}, u32[]{:S(2)}) async-start(bf16[4,48,2048]{2,1,0:T(8,128)(2,1)} %broadcast_in_dim.31), calls=%async_computation | async-start | bytes 1572864 | tf_op jit(solution)/shard_map/all_to_all | solution.py:136
  11.7 2.3 %collective-permute-start = (bf16[48,2048]{1,0:T(8,128)(2,1)S(1)}, bf16[48,2048]{1,0:T(8,128)(2,1)S(1)}, u32[]{:S(2)}, u32[]{:S(2)}) collective-permute-start(bf16[48,2048]{1,0:T(8,128)(2,1)S(1)} %bitcast.123), channel_id=1, source_target_pairs={{0,16},{16,0},{1,17},{17,1},{2,18},{18,2},{3,19},{19,3},{4,20},{20... | collective-permute-start | bytes 589832 | tf_op jit(solution)/shard_map/ppermute | solution.py:52
  14.1 0.1 collective-permute-start.1
  14.3 9.5 %collective-permute-done = bf16[48,2048]{1,0:T(8,128)(2,1)S(1)} collective-permute-done((bf16[48,2048]{1,0:T(8,128)(2,1)S(1)}, bf16[48,2048]{1,0:T(8,128)(2,1)S(1)}, u32[]{:S(2)}, u32[]{:S(2)}) %collective-permute-start) | collective-permute-done | bytes 196640 | tf_op jit(solution)/shard_map/ppermute | solution.py:52
  23.7 2.4 %all-to-all-done = bf16[4,48,2048]{2,1,0:T(8,128)(2,1)S(1)} async-done(((bf16[4,48,2048]{2,1,0:T(8,128)(2,1)}), bf16[4,48,2048]{2,1,0:T(8,128)(2,1)S(1)}, u32[]{:S(2)}, u32[]{:S(2)}) %all-to-all-start) | async-done | bytes 786464 | tf_op jit(solution)/shard_map/all_to_all | solution.py:136
  26.1 1.0 broadcast_in_dim.32
  27.1 4.6 %all-to-all-start.1 = ((bf16[4,48,2048]{2,1,0:T(8,128)(2,1)}), bf16[4,48,2048]{2,1,0:T(8,128)(2,1)}, u32[]{:S(2)}, u32[]{:S(2)}) async-start(bf16[4,48,2048]{2,1,0:T(8,128)(2,1)} %broadcast_in_dim.32), calls=%async_computation.1 | async-start | bytes 1572864 | tf_op jit(solution)/shard_map/all_to_all | solution.py:136
  32.1 0.6 reduce-window.6
  32.6 0.2 slice_reduce_fusion
  32.9 0.6 fusion.22
  33.5 7.7 %all-to-all-done.1 = bf16[4,48,2048]{2,1,0:T(8,128)(2,1)} async-done(((bf16[4,48,2048]{2,1,0:T(8,128)(2,1)}), bf16[4,48,2048]{2,1,0:T(8,128)(2,1)}, u32[]{:S(2)}, u32[]{:S(2)}) %all-to-all-start.1) | async-done | bytes 786464 | tf_op jit(solution)/shard_map/all_to_all | solution.py:136
  41.1 1.7 fusion.25
  42.9 0.9 convert_element_type.87
  43.8 5.2 %all-to-all-start.2 = ((bf16[32,12,512]{2,1,0:T(8,128)(2,1)}), bf16[32,12,512]{2,1,0:T(8,128)(2,1)S(1)}, u32[]{:S(2)}, u32[]{:S(2)}) async-start(bf16[32,12,512]{2,1,0:T(8,128)(2,1)} %convert_element_type.87), calls=%async_computation.2 | async-start | bytes 1048576 | tf_op jit(solution)/shard_map/all_to_all | solution.py:146
  49.4 13.8 %all-to-all-done.2 = bf16[32,12,512]{2,1,0:T(8,128)(2,1)S(1)} async-done(((bf16[32,12,512]{2,1,0:T(8,128)(2,1)}), bf16[32,12,512]{2,1,0:T(8,128)(2,1)S(1)}, u32[]{:S(2)}, u32[]{:S(2)}) %all-to-all-start.2) | async-done | bytes 393248 | tf_op jit(solution)/shard_map/all_to_all | solution.py:146
  63.3 0.1 copy.47
  63.5 0.2 copy.78
  63.6 0.2 fusion.32
  63.8 0.1 fusion.34
  64.0 0.7 fusion.29
  64.7 8.0 %collective-permute-done.2 = bf16[12,4096]{1,0:T(8,128)(2,1)S(1)} collective-permute-done((bf16[12,4096]{1,0:T(8,128)(2,1)S(1)}, bf16[12,4096]{1,0:T(8,128)(2,1)S(1)}, u32[]{:S(2)}, u32[]{:S(2)}) %collective-permute-start.2) | collective-permute-done | bytes 98336 | tf_op jit(solution)/shard_map/ppermute | solution.py:52
  72.8 1.0 convolution_convert_fusion
  73.8 41.0 %all_to_all.25 = bf16[16,24,4096]{2,1,0:T(8,128)(2,1)S(1)} all-to-all(bf16[16,24,4096]{2,1,0:T(8,128)(2,1)S(1)} %convolution_convert_fusion), channel_id=1, replica_groups=mesh['zh'=2,'dl'=4,'tensor'=4] {'dl','tensor'}, dimensions={0} | all-to-all | bytes 6291456 | tf_op jit(solution)/shard_map/all_to_all | solution.py:86
  114.8 2.7 %fusion.4 = f32[16,24,768]{2,1,0:T(8,128)S(1)} fusion(bf16[16,24,4096]{2,1,0:T(8,128)(2,1)S(1)} %all_to_all.25, bf16[1,4096,768]{2,1,0:T(8,128)(2,1)S(1)} %bitcast.129), kind=kOutput, calls=%fused_computation.5 | convolution fusion | flops 2415919104 | bytes 10616832 | tf_op jit(solution)/shard_map/hcd,df->hcf/dot_general | solution.py:87
  117.6 2.8 %fusion.19 = bf16[16,24,768]{2,1,0:T(8,128)(2,1)S(1)} fusion(bf16[16,24,4096]{2,1,0:T(8,128)(2,1)S(1)} %all_to_all.25, bf16[1,4096,768]{2,1,0:T(8,128)(2,1)S(1)} %bitcast.131, f32[16,24,768]{2,1,0:T(8,128)S(1)} %fusion.4), kind=kOutput, calls=%fused_computation.22 | convolution fusion | flops 2417688576 | bytes 11206656 | tf_op jit(solution)/shard_map/hcd,df->hcf/dot_general | solution.py:88
  120.5 4.1 %fusion = bf16[16,24,4096]{2,1,0:T(8,128)(2,1)} fusion(bf16[16,24,768]{2,1,0:T(8,128)(2,1)S(1)} %fusion.19, bf16[1,768,4096]{2,1,0:T(8,128)(2,1)S(1)} %bitcast.133), kind=kOutput, calls=%fused_computation.1 | convolution fusion | flops 2415919104 | bytes 10027008 | tf_op jit(solution)/shard_map/hcf,fd->hcd/dot_general | solution.py:91
  124.6 4.6 %reshape.205 = bf16[16,576,128]{2,1,0:T(8,128)(2,1)} reshape(bf16[16,18,4096]{2,1,0:T(8,128)(2,1)} %bitcast.114) | data formatting | bytes 4718592 | tf_op jit(solution)/shard_map/reshape | solution.py:96
  129.2 6.6 %all-to-all-start.4 = ((bf16[16,576,128]{2,1,0:T(8,128)(2,1)}), bf16[16,576,128]{2,1,0:T(8,128)(2,1)}, u32[]{:S(2)}, u32[]{:S(2)}) async-start(bf16[16,576,128]{2,1,0:T(8,128)(2,1)} %reshape.205), calls=%async_computation.4 | async-start | bytes 4718592 | tf_op jit(solution)/shard_map/all_to_all | solution.py:97
  136.1 0.1 broadcast_compare_fusion
  136.3 0.5 copy.59
  136.7 0.7 copy.67
  137.5 0.5 copy.52
  138.0 0.7 copy.64
  138.7 31.1 %all-to-all-done.4 = bf16[16,576,128]{2,1,0:T(8,128)(2,1)} async-done(((bf16[16,576,128]{2,1,0:T(8,128)(2,1)}), bf16[16,576,128]{2,1,0:T(8,128)(2,1)}, u32[]{:S(2)}, u32[]{:S(2)}) %all-to-all-start.4) | async-done | bytes 2359328 | tf_op jit(solution)/shard_map/all_to_all | solution.py:97
  169.8 3.7 %copy.85 = bf16[16,18,32,128]{3,2,0,1:T(8,128)(2,1)} copy(bf16[16,18,32,128]{3,2,1,0:T(8,128)(2,1)} %bitcast.19) | data formatting | bytes 4718592 | tf_op jit(solution)/shard_map/reshape | solution.py:98
  173.5 4.9 %dot_general.57 = bf16[4096,18,16]{0,2,1:T(8,128)(2,1)} reshape(bf16[32,128,18,16]{1,0,3,2:T(8,128)(2,1)} %bitcast.113) | data formatting | bytes 4718592 | tf_op jit(solution)/shard_map/hcp,hcql->pql/dot_general | solution.py:102
  178.4 2.8 %multiply_reduce_fusion = bf16[12,4096]{1,0:T(8,128)(2,1)S(1)} fusion(f32[12,8]{1,0:T(8,128)S(1)} %copy.58, pred[12,8,18,16]{3,1,2,0:T(8,128)(4,1)S(1)} %copy.67, bf16[4096,18,16]{0,2,1:T(8,128)(2,1)} %dot_general.57), kind=kOutput, calls=%fused_computation.18 | convolution fusion | flops 227229696 | bytes 2485632 | tf_op jit(solution)/shard_map/hcp,hcql->pql/dot_general | solution.py:102
  181.2 1.0 collective-permute-start.3
  182.2 1.1 fusion.16
  183.3 6.5 %collective-permute-done.3 = bf16[12,4096]{1,0:T(8,128)(2,1)S(1)} collective-permute-done((bf16[12,4096]{1,0:T(8,128)(2,1)S(1)}, bf16[12,4096]{1,0:T(8,128)(2,1)S(1)}, u32[]{:S(2)}, u32[]{:S(2)}) %collective-permute-start.3) | collective-permute-done | bytes 98336 | tf_op jit(solution)/shard_map/ppermute | solution.py:52
  189.8 0.7 add_convert_fusion
  (70 shorter events, 1.6 us)
Async XLA Ops:
  0.6 32.2 %copy-start = (bf16[2048,512]{1,0:T(8,128)(2,1)S(1)}, bf16[2048,512]{1,0:T(8,128)(2,1)}, u32[]{:S(2)}) copy-start(bf16[2048,512]{1,0:T(8,128)(2,1)} %param.21) | copy-start | bytes 6291460
  0.6 5.6 %copy-start.7 = (bf16[48,128]{1,0:T(8,128)(2,1)S(1)}, bf16[48,128]{1,0:T(8,128)(2,1)}, u32[]{:S(2)}) copy-start(bf16[48,128]{1,0:T(8,128)(2,1)} %param.16) | copy-start | bytes 36868
  0.7 5.6 %copy-start.8 = (bf16[48,128,128]{2,1,0:T(8,128)(2,1)S(1)}, bf16[48,128,128]{2,1,0:T(8,128)(2,1)}, u32[]{:S(2)}) copy-start(bf16[48,128,128]{2,1,0:T(8,128)(2,1)} %param.18) | copy-start | bytes 4718596
  6.3 7.7 %copy-start.5 = (s32[12,8]{0,1:T(8,128)S(1)}, s32[12,8]{0,1:T(8,128)}, u32[]{:S(2)}) copy-start(s32[12,8]{0,1:T(8,128)} %param.23) | copy-start | bytes 1156
  6.3 7.7 %copy-start.6 = (f32[12,8]{0,1:T(8,128)S(1)}, f32[12,8]{0,1:T(8,128)}, u32[]{:S(2)}) copy-start(f32[12,8]{0,1:T(8,128)} %param.24) | copy-start | bytes 1156
  8.0 18.1 %all-to-all-start = ((bf16[4,48,2048]{2,1,0:T(8,128)(2,1)}), bf16[4,48,2048]{2,1,0:T(8,128)(2,1)S(1)}, u32[]{:S(2)}, u32[]{:S(2)}) async-start(bf16[4,48,2048]{2,1,0:T(8,128)(2,1)} %broadcast_in_dim.31), calls=%async_computation | async-start | bytes 1572864 | tf_op jit(solution)/shard_map/all_to_all | solution.py:136
  11.7 12.0 %collective-permute-start = (bf16[48,2048]{1,0:T(8,128)(2,1)S(1)}, bf16[48,2048]{1,0:T(8,128)(2,1)S(1)}, u32[]{:S(2)}, u32[]{:S(2)}) collective-permute-start(bf16[48,2048]{1,0:T(8,128)(2,1)S(1)} %bitcast.123), channel_id=1, source_target_pairs={{0,16},{16,0},{1,17},{17,1},{2,18},{18,2},{3,19},{19,3},{4,20},{20... | collective-permute-start | bytes 589832 | tf_op jit(solution)/shard_map/ppermute | solution.py:52
  14.1 17.7 %collective-permute-start.1 = (f32[12,16]{0,1:T(8,128)S(1)}, f32[12,16]{0,1:T(8,128)S(1)}, u32[]{:S(2)}, u32[]{:S(2)}) collective-permute-start(f32[12,16]{0,1:T(8,128)S(1)} %pad_maximum_fusion), channel_id=1, source_target_pairs={{0,16},{16,0},{1,17},{17,1},{2,18},{18,2},{3,19},{19,3},{4,20},{20... | collective-permute-start | bytes 2312 | tf_op jit(solution)/shard_map/ppermute | solution.py:52
  27.1 14.0 %all-to-all-start.1 = ((bf16[4,48,2048]{2,1,0:T(8,128)(2,1)}), bf16[4,48,2048]{2,1,0:T(8,128)(2,1)}, u32[]{:S(2)}, u32[]{:S(2)}) async-start(bf16[4,48,2048]{2,1,0:T(8,128)(2,1)} %broadcast_in_dim.32), calls=%async_computation.1 | async-start | bytes 1572864 | tf_op jit(solution)/shard_map/all_to_all | solution.py:136
  42.9 20.7 %copy-start.3 = (bf16[12,4096]{1,0:T(8,128)(2,1)S(1)}, bf16[12,4096]{1,0:T(8,128)(2,1)}, u32[]{:S(2)}) copy-start(bf16[12,4096]{1,0:T(8,128)(2,1)} %param.20) | copy-start | bytes 294916
  42.9 20.9 %copy-start.4 = (f32[4096]{0:T(1024)S(1)}, f32[4096]{0:T(1024)}, u32[]{:S(2)}) copy-start(f32[4096]{0:T(1024)} %param.22) | copy-start | bytes 49156
  43.8 19.4 %all-to-all-start.2 = ((bf16[32,12,512]{2,1,0:T(8,128)(2,1)}), bf16[32,12,512]{2,1,0:T(8,128)(2,1)S(1)}, u32[]{:S(2)}, u32[]{:S(2)}) async-start(bf16[32,12,512]{2,1,0:T(8,128)(2,1)} %convert_element_type.87), calls=%async_computation.2 | async-start | bytes 1048576 | tf_op jit(solution)/shard_map/all_to_all | solution.py:146
  63.2 51.6 %slice-start = ((s8[6291456]{0:T(1024)(128)(4,1)}), s8[4194304]{0:T(1024)(128)(4,1)S(1)}, s32[]{:S(2)}) async-start(s8[6291456]{0:T(1024)(128)(4,1)} %bitcast.128), calls=%async_computation.5 | async-start | bytes 8388608
  63.8 51.0 %copy-start.2 = (bf16[12,4096]{1,0:T(8,128)(2,1)}, bf16[12,4096]{1,0:T(8,128)(2,1)S(1)}, u32[]{:S(2)}) copy-start(bf16[12,4096]{1,0:T(8,128)(2,1)S(1)} %get-tuple-element.5) | copy-start | bytes 294916
  63.9 8.8 %collective-permute-start.2 = (bf16[12,4096]{1,0:T(8,128)(2,1)S(1)}, bf16[12,4096]{1,0:T(8,128)(2,1)S(1)}, u32[]{:S(2)}, u32[]{:S(2)}) collective-permute-start(bf16[12,4096]{1,0:T(8,128)(2,1)S(1)} %fusion.34), channel_id=1, source_target_pairs={{0,16},{16,0},{1,17},{17,1},{2,18},{18,2},{3,19},{19,3},{4,20},{20... | collective-permute-start | bytes 294920 | tf_op jit(solution)/shard_map/ppermute | solution.py:52
  64.7 50.1 %slice-start.1 = ((s8[6291456]{0:T(1024)(128)(4,1)}), s8[2097152]{0:T(1024)(128)(4,1)S(1)}, s32[]{:S(2)}) async-start(s8[6291456]{0:T(1024)(128)(4,1)} %bitcast.128), calls=%async_computation.6 | async-start | bytes 4194304
  73.7 43.9 %slice-start.2 = ((s8[6291456]{0:T(1024)(128)(4,1)}), s8[4194304]{0:T(1024)(128)(4,1)S(1)}, s32[]{:S(2)}) async-start(s8[6291456]{0:T(1024)(128)(4,1)} %bitcast.130), calls=%async_computation.7 | async-start | bytes 8388608
  114.8 2.8 %slice-start.3 = ((s8[6291456]{0:T(1024)(128)(4,1)}), s8[2097152]{0:T(1024)(128)(4,1)S(1)}, s32[]{:S(2)}) async-start(s8[6291456]{0:T(1024)(128)(4,1)} %bitcast.130), calls=%async_computation.8 | async-start | bytes 4194304
  114.8 5.6 %slice-start.4 = ((s8[6291456]{0:T(1024)(128)(4,1)}), s8[4194304]{0:T(1024)(128)(4,1)S(1)}, s32[]{:S(2)}) async-start(s8[6291456]{0:T(1024)(128)(4,1)} %bitcast.132), calls=%async_computation.9 | async-start | bytes 8388608
  117.6 2.8 %slice-start.5 = ((s8[6291456]{0:T(1024)(128)(4,1)}), s8[2097152]{0:T(1024)(128)(4,1)S(1)}, s32[]{:S(2)}) async-start(s8[6291456]{0:T(1024)(128)(4,1)} %bitcast.132), calls=%async_computation.10 | async-start | bytes 4194304
  129.2 40.6 %all-to-all-start.4 = ((bf16[16,576,128]{2,1,0:T(8,128)(2,1)}), bf16[16,576,128]{2,1,0:T(8,128)(2,1)}, u32[]{:S(2)}, u32[]{:S(2)}) async-start(bf16[16,576,128]{2,1,0:T(8,128)(2,1)} %reshape.205), calls=%async_computation.4 | async-start | bytes 4718592 | tf_op jit(solution)/shard_map/all_to_all | solution.py:97
  178.4 3.8 %copy-start.1 = (bf16[4096,18,16]{0,2,1:T(8,128)(2,1)S(1)}, bf16[4096,18,16]{0,2,1:T(8,128)(2,1)}, u32[]{:S(2)}) copy-start(bf16[4096,18,16]{0,2,1:T(8,128)(2,1)} %dot_general.57) | copy-start | bytes 7077892
  181.2 8.5 %collective-permute-start.3 = (bf16[12,4096]{1,0:T(8,128)(2,1)S(1)}, bf16[12,4096]{1,0:T(8,128)(2,1)S(1)}, u32[]{:S(2)}, u32[]{:S(2)}) collective-permute-start(bf16[12,4096]{1,0:T(8,128)(2,1)S(1)} %multiply_reduce_fusion), channel_id=1, source_target_pairs={{0,16},{16,0},{1,17},{17,1},{2,18},{18,2},{3,19},{19,3},{4,20},{20... | collective-permute-start | bytes 294920 | tf_op jit(solution)/shard_map/ppermute | solution.py:52

commit v11 on v10

--- a/solution.py
+++ b/solution.py
@@ -95,13 +95,14 @@
     used = min(capacity, 2 * max(2, 3 * tok_here * chosen_count // experts_all))
     back = result[:, :used].reshape(n_half, used * (width // lanes), lanes)
     returned = lax.all_to_all(back, HALF, split_axis=0, concat_axis=0, tiled=True)
-    returned = returned.reshape(n_half, used, width // lanes, lanes)
+    returned = returned.reshape(n_half * used, width)
     placement = placement.reshape(n_half, capacity, 2, tok_here * chosen_count)[:, :used]
+    placement = placement.reshape(n_half * used, 2, tok_here * chosen_count)
 
     def combine(block, weight):
         pair_rows = jnp.einsum(
-            "hcp,hcql->pql", placement[:, :, block], returned, preferred_element_type=jnp.float32
-        ).reshape(tok_here * chosen_count, width)
+            "sp,sd->pd", placement[:, block], returned, preferred_element_type=jnp.float32
+        )
         weighted = weight[..., None] * pair_rows.reshape(tok_here, chosen_count, width)
         return jnp.sum(weighted, axis=1)
 

time: 191 us -> 187 us (0.979)
  local copies, waits for them, and re-layouts: 21 us -> 15.3 us
  waiting for transfers between devices: 78.9 us -> 81.1 us
    dot_general x6 -> x3, local copies, waits for them, and re-layouts: 7.29 us -> 0.3 us  [combine(): jnp.einsum('sp,sd->pd', placement[:, block], returned, preferred_element_...]
    all_to_all x1, waiting for transfers between devices: 31.1 us -> 33.1 us  [expert_layer(): lax.all_to_all(back, HALF, split_axis=0, concat_axis=0, tiled=True)]
    reshape x1 -> x2, local copies, waits for them, and re-layouts: 3.71 us -> 5.04 us  [the longest x1 4.97 us: expert_layer(): returned = returned.reshape(n_half * used, width)]
  transfers between devices with their start and end apart: 8 -> 8, of which waited for: 7 -> 7; matrix products, arithmetic and copies ran while one was open for 4% -> 3% of each run, Pallas kernels for 0% -> 0%
where the time goes in v11:
time: 187 us
  waiting for transfers between devices  81.1 us (43%)
  blocking collectives  41 us (22%)
  starting transfers between devices  23.6 us (13%)
  matrix products  20.5 us (11%)
  local copies, waits for them, and re-layouts  15.3 us (8%)
  other arithmetic  4.01 us (2%)
    all_to_all x1, blocking collectives, expert_layer(): lax.all_to_all(outgoing, HALF, split_axis=0, concat_axis=0, tiled=True)  41 us
    all_to_all x1, waiting for transfers between devices, expert_layer(): lax.all_to_all(back, HALF, split_axis=0, concat_axis=0, tiled=True)  33.1 us
    ppermute x4, waiting for transfers between devices, swap_halves(): return lax.ppermute(x, 'zh', [(0, 1), (1, 0)])  24.2 us
    all_to_all x1, waiting for transfers between devices, shards(): lax.all_to_all(by_dest.astype(jnp.bfloat16), DP + ('tensor',), split_axis...  13.8 us
    all_to_all x2, waiting for transfers between devices, project(): lax.all_to_all(spread, 'dl', split_axis=0, concat_axis=0, tiled=True)  10.1 us
    all_to_all x2, starting transfers between devices, project(): lax.all_to_all(spread, 'dl', split_axis=0, concat_axis=0, tiled=True)  8.39 us
    all_to_all x1, starting transfers between devices, expert_layer(): lax.all_to_all(back, HALF, split_axis=0, concat_axis=0, tiled=True)  6.55 us
    all_to_all x1, starting transfers between devices, shards(): lax.all_to_all(by_dest.astype(jnp.bfloat16), DP + ('tensor',), split_axis...  5.19 us
  transfers between devices with their start and end apart: 8, of which 7 were waited for; matrix products, arithmetic and copies ran while one was open for 3% of the time, Pallas kernels for 0%

profile of v11, /device:TPU:7, one launch (start us, length us, event | category | flops | bytes accessed | tf_op | source)
XLA Modules:
  0.0 186.7 jit_solution(4575222652031653361)
XLA Ops:
  0.7 0.9 iota_compare_fusion
  1.5 1.0 copy.48
  2.6 0.9 fusion.41
  3.5 2.4 %select_reduce_fusion = (f32[48,16]{1,0:T(8,128)S(1)}, f32[48,16,128]{2,1,0:T(8,128)S(1)}) fusion(pred[48,128]{1,0:T(8,128)(4,1)S(1)} %iota_compare_fusion, bf16[48,16,128]{2,1,0:T(8,128)(2,1)S(1)} %bitcast.99, bf16[48,128,128]{2,1,0:T(8,128)(2,1)} %param.17), kind=kOutput, calls=%fused_computation.29 | convolution fusion | flops 25459968 | bytes 2171904 | tf_op jit(solution)/shard_map/rkgd,rckd->rkgc/dot_general | solution.py:27
  5.9 0.3 fusion.26
  6.3 0.6 fusion.23
  7.0 1.0 broadcast_in_dim.31
  8.0 3.7 %all-to-all-start = ((bf16[4,48,2048]{2,1,0:T(8,128)(2,1)}), bf16[4,48,2048]{2,1,0:T(8,128)(2,1)S(1)}, u32[]{:S(2)}, u32[]{:S(2)}) async-start(bf16[4,48,2048]{2,1,0:T(8,128)(2,1)} %broadcast_in_dim.31), calls=%async_computation | async-start | bytes 1572864 | tf_op jit(solution)/shard_map/all_to_all | solution.py:137
  11.7 2.3 %collective-permute-start = (bf16[48,2048]{1,0:T(8,128)(2,1)S(1)}, bf16[48,2048]{1,0:T(8,128)(2,1)S(1)}, u32[]{:S(2)}, u32[]{:S(2)}) collective-permute-start(bf16[48,2048]{1,0:T(8,128)(2,1)S(1)} %bitcast.101), channel_id=1, source_target_pairs={{0,16},{16,0},{1,17},{17,1},{2,18},{18,2},{3,19},{19,3},{4,20},{20... | collective-permute-start | bytes 589832 | tf_op jit(solution)/shard_map/ppermute | solution.py:52
  14.0 0.1 collective-permute-start.1
  14.2 9.5 %collective-permute-done = bf16[48,2048]{1,0:T(8,128)(2,1)S(1)} collective-permute-done((bf16[48,2048]{1,0:T(8,128)(2,1)S(1)}, bf16[48,2048]{1,0:T(8,128)(2,1)S(1)}, u32[]{:S(2)}, u32[]{:S(2)}) %collective-permute-start) | collective-permute-done | bytes 196640 | tf_op jit(solution)/shard_map/ppermute | solution.py:52
  23.7 2.4 %all-to-all-done = bf16[4,48,2048]{2,1,0:T(8,128)(2,1)S(1)} async-done(((bf16[4,48,2048]{2,1,0:T(8,128)(2,1)}), bf16[4,48,2048]{2,1,0:T(8,128)(2,1)S(1)}, u32[]{:S(2)}, u32[]{:S(2)}) %all-to-all-start) | async-done | bytes 786464 | tf_op jit(solution)/shard_map/all_to_all | solution.py:137
  26.1 1.0 broadcast_in_dim.32
  27.1 4.6 %all-to-all-start.1 = ((bf16[4,48,2048]{2,1,0:T(8,128)(2,1)}), bf16[4,48,2048]{2,1,0:T(8,128)(2,1)}, u32[]{:S(2)}, u32[]{:S(2)}) async-start(bf16[4,48,2048]{2,1,0:T(8,128)(2,1)} %broadcast_in_dim.32), calls=%async_computation.1 | async-start | bytes 1572864 | tf_op jit(solution)/shard_map/all_to_all | solution.py:137
  31.9 0.1 sub.40
  32.0 0.6 reduce-window.6
  32.6 0.2 slice_reduce_fusion
  32.9 0.6 fusion.17
  33.4 7.7 %all-to-all-done.1 = bf16[4,48,2048]{2,1,0:T(8,128)(2,1)} async-done(((bf16[4,48,2048]{2,1,0:T(8,128)(2,1)}), bf16[4,48,2048]{2,1,0:T(8,128)(2,1)}, u32[]{:S(2)}, u32[]{:S(2)}) %all-to-all-start.1) | async-done | bytes 786464 | tf_op jit(solution)/shard_map/all_to_all | solution.py:137
  41.1 1.7 fusion.20
  42.9 0.9 convert_element_type.87
  43.8 5.2 %all-to-all-start.2 = ((bf16[32,12,512]{2,1,0:T(8,128)(2,1)}), bf16[32,12,512]{2,1,0:T(8,128)(2,1)S(1)}, u32[]{:S(2)}, u32[]{:S(2)}) async-start(bf16[32,12,512]{2,1,0:T(8,128)(2,1)} %convert_element_type.87), calls=%async_computation.2 | async-start | bytes 1048576 | tf_op jit(solution)/shard_map/all_to_all | solution.py:147
  49.2 0.1 gt.20
  49.4 13.8 %all-to-all-done.2 = bf16[32,12,512]{2,1,0:T(8,128)(2,1)S(1)} async-done(((bf16[32,12,512]{2,1,0:T(8,128)(2,1)}), bf16[32,12,512]{2,1,0:T(8,128)(2,1)S(1)}, u32[]{:S(2)}, u32[]{:S(2)}) %all-to-all-start.2) | async-done | bytes 393248 | tf_op jit(solution)/shard_map/all_to_all | solution.py:147
  63.2 0.1 convert_reduce_fusion
  63.3 0.1 copy.35
  63.4 0.2 copy.50
  63.6 0.2 fusion.27
  63.8 0.1 fusion.29
  64.0 0.7 fusion.24
  64.7 8.0 %collective-permute-done.2 = bf16[12,4096]{1,0:T(8,128)(2,1)S(1)} collective-permute-done((bf16[12,4096]{1,0:T(8,128)(2,1)S(1)}, bf16[12,4096]{1,0:T(8,128)(2,1)S(1)}, u32[]{:S(2)}, u32[]{:S(2)}) %collective-permute-start.2) | collective-permute-done | bytes 98336 | tf_op jit(solution)/shard_map/ppermute | solution.py:52
  72.7 1.0 convolution_convert_fusion
  73.7 41.0 %all_to_all.25 = bf16[16,24,4096]{2,1,0:T(8,128)(2,1)S(1)} all-to-all(bf16[16,24,4096]{2,1,0:T(8,128)(2,1)S(1)} %convolution_convert_fusion), channel_id=1, replica_groups=mesh['zh'=2,'dl'=4,'tensor'=4] {'dl','tensor'}, dimensions={0} | all-to-all | bytes 6291456 | tf_op jit(solution)/shard_map/all_to_all | solution.py:86
  114.8 2.7 %fusion.4 = f32[16,24,768]{2,1,0:T(8,128)S(1)} fusion(bf16[16,24,4096]{2,1,0:T(8,128)(2,1)S(1)} %all_to_all.25, bf16[1,4096,768]{2,1,0:T(8,128)(2,1)S(1)} %bitcast.108), kind=kOutput, calls=%fused_computation.5 | convolution fusion | flops 2415919104 | bytes 10616832 | tf_op jit(solution)/shard_map/hcd,df->hcf/dot_general | solution.py:87
  117.6 2.8 %fusion.14 = bf16[16,24,768]{2,1,0:T(8,128)(2,1)S(1)} fusion(bf16[16,24,4096]{2,1,0:T(8,128)(2,1)S(1)} %all_to_all.25, bf16[1,4096,768]{2,1,0:T(8,128)(2,1)S(1)} %bitcast.110, f32[16,24,768]{2,1,0:T(8,128)S(1)} %fusion.4), kind=kOutput, calls=%fused_computation.17 | convolution fusion | flops 2417688576 | bytes 11206656 | tf_op jit(solution)/shard_map/hcd,df->hcf/dot_general | solution.py:88
  120.4 4.1 %fusion = bf16[16,24,4096]{2,1,0:T(8,128)(2,1)} fusion(bf16[16,24,768]{2,1,0:T(8,128)(2,1)S(1)} %fusion.14, bf16[1,768,4096]{2,1,0:T(8,128)(2,1)S(1)} %bitcast.112), kind=kOutput, calls=%fused_computation.1 | convolution fusion | flops 2415919104 | bytes 10027008 | tf_op jit(solution)/shard_map/hcf,fd->hcd/dot_general | solution.py:91
  124.6 4.6 %reshape.209 = bf16[16,576,128]{2,1,0:T(8,128)(2,1)} reshape(bf16[16,18,4096]{2,1,0:T(8,128)(2,1)} %bitcast.94) | data formatting | bytes 4718592 | tf_op jit(solution)/shard_map/reshape | solution.py:96
  129.2 6.5 %all-to-all-start.4 = ((bf16[16,576,128]{2,1,0:T(8,128)(2,1)}), bf16[16,576,128]{2,1,0:T(8,128)(2,1)}, u32[]{:S(2)}, u32[]{:S(2)}) async-start(bf16[16,576,128]{2,1,0:T(8,128)(2,1)} %reshape.209), calls=%async_computation.4 | async-start | bytes 4718592 | tf_op jit(solution)/shard_map/all_to_all | solution.py:97
  136.1 0.1 broadcast_compare_fusion
  136.3 0.1 copy.43
  136.5 0.1 copy.40
  136.7 33.1 %all-to-all-done.4 = bf16[16,576,128]{2,1,0:T(8,128)(2,1)} async-done(((bf16[16,576,128]{2,1,0:T(8,128)(2,1)}), bf16[16,576,128]{2,1,0:T(8,128)(2,1)}, u32[]{:S(2)}, u32[]{:S(2)}) %all-to-all-start.4) | async-done | bytes 2359328 | tf_op jit(solution)/shard_map/all_to_all | solution.py:97
  169.7 5.0 %reshape.221 = bf16[288,4096,1]{1,0,2:T(8,128)(2,1)} reshape(bf16[16,576,128]{2,1,0:T(8,128)(2,1)} %all-to-all-done.4) | data formatting | bytes 4718592 | tf_op jit(solution)/shard_map/reshape | solution.py:98
  174.7 2.7 %multiply_reduce_fusion = bf16[12,4096]{1,0:T(8,128)(2,1)S(1)} fusion(f32[12,8]{1,0:T(8,128)S(1)} %copy.42, bf16[288,4096,1]{1,0,2:T(8,128)(2,1)} %reshape.221, pred[96,288]{1,0:T(8,128)(4,1)S(1)} %copy.43), kind=kOutput, calls=%fused_computation.13 | convolution fusion | flops 227229696 | bytes 2485632 | tf_op jit(solution)/shard_map/sp,sd->pd/dot_general | solution.py:103
  177.5 1.0 collective-permute-start.3
  178.5 0.9 fusion.13
  179.4 6.6 %collective-permute-done.3 = bf16[12,4096]{1,0:T(8,128)(2,1)S(1)} collective-permute-done((bf16[12,4096]{1,0:T(8,128)(2,1)S(1)}, bf16[12,4096]{1,0:T(8,128)(2,1)S(1)}, u32[]{:S(2)}, u32[]{:S(2)}) %collective-permute-start.3) | collective-permute-done | bytes 98336 | tf_op jit(solution)/shard_map/ppermute | solution.py:52
  186.0 0.7 add_convert_fusion
  (67 shorter events, 1.3 us)
Async XLA Ops:
  0.6 32.2 %copy-start = (bf16[2048,512]{1,0:T(8,128)(2,1)S(1)}, bf16[2048,512]{1,0:T(8,128)(2,1)}, u32[]{:S(2)}) copy-start(bf16[2048,512]{1,0:T(8,128)(2,1)} %param.21) | copy-start | bytes 6291460
  0.6 5.6 %copy-start.7 = (bf16[48,128]{1,0:T(8,128)(2,1)S(1)}, bf16[48,128]{1,0:T(8,128)(2,1)}, u32[]{:S(2)}) copy-start(bf16[48,128]{1,0:T(8,128)(2,1)} %param.16) | copy-start | bytes 36868
  0.7 5.6 %copy-start.8 = (bf16[48,128,128]{2,1,0:T(8,128)(2,1)S(1)}, bf16[48,128,128]{2,1,0:T(8,128)(2,1)}, u32[]{:S(2)}) copy-start(bf16[48,128,128]{2,1,0:T(8,128)(2,1)} %param.18) | copy-start | bytes 4718596
  6.9 7.1 %copy-start.5 = (s32[12,8]{0,1:T(8,128)S(1)}, s32[12,8]{0,1:T(8,128)}, u32[]{:S(2)}) copy-start(s32[12,8]{0,1:T(8,128)} %param.23) | copy-start | bytes 1156
  6.9 7.1 %copy-start.6 = (f32[12,8]{0,1:T(8,128)S(1)}, f32[12,8]{0,1:T(8,128)}, u32[]{:S(2)}) copy-start(f32[12,8]{0,1:T(8,128)} %param.24) | copy-start | bytes 1156
  8.0 18.1 %all-to-all-start = ((bf16[4,48,2048]{2,1,0:T(8,128)(2,1)}), bf16[4,48,2048]{2,1,0:T(8,128)(2,1)S(1)}, u32[]{:S(2)}, u32[]{:S(2)}) async-start(bf16[4,48,2048]{2,1,0:T(8,128)(2,1)} %broadcast_in_dim.31), calls=%async_computation | async-start | bytes 1572864 | tf_op jit(solution)/shard_map/all_to_all | solution.py:137
  11.7 12.0 %collective-permute-start = (bf16[48,2048]{1,0:T(8,128)(2,1)S(1)}, bf16[48,2048]{1,0:T(8,128)(2,1)S(1)}, u32[]{:S(2)}, u32[]{:S(2)}) collective-permute-start(bf16[48,2048]{1,0:T(8,128)(2,1)S(1)} %bitcast.101), channel_id=1, source_target_pairs={{0,16},{16,0},{1,17},{17,1},{2,18},{18,2},{3,19},{19,3},{4,20},{20... | collective-permute-start | bytes 589832 | tf_op jit(solution)/shard_map/ppermute | solution.py:52
  14.0 17.7 %collective-permute-start.1 = (f32[12,16]{0,1:T(8,128)S(1)}, f32[12,16]{0,1:T(8,128)S(1)}, u32[]{:S(2)}, u32[]{:S(2)}) collective-permute-start(f32[12,16]{0,1:T(8,128)S(1)} %pad_maximum_fusion), channel_id=1, source_target_pairs={{0,16},{16,0},{1,17},{17,1},{2,18},{18,2},{3,19},{19,3},{4,20},{20... | collective-permute-start | bytes 2312 | tf_op jit(solution)/shard_map/ppermute | solution.py:52
  27.1 14.0 %all-to-all-start.1 = ((bf16[4,48,2048]{2,1,0:T(8,128)(2,1)}), bf16[4,48,2048]{2,1,0:T(8,128)(2,1)}, u32[]{:S(2)}, u32[]{:S(2)}) async-start(bf16[4,48,2048]{2,1,0:T(8,128)(2,1)} %broadcast_in_dim.32), calls=%async_computation.1 | async-start | bytes 1572864 | tf_op jit(solution)/shard_map/all_to_all | solution.py:137
  42.9 20.7 %copy-start.3 = (bf16[12,4096]{1,0:T(8,128)(2,1)S(1)}, bf16[12,4096]{1,0:T(8,128)(2,1)}, u32[]{:S(2)}) copy-start(bf16[12,4096]{1,0:T(8,128)(2,1)} %param.20) | copy-start | bytes 294916
  43.8 20.0 %copy-start.4 = (f32[4096]{0:T(1024)S(1)}, f32[4096]{0:T(1024)}, u32[]{:S(2)}) copy-start(f32[4096]{0:T(1024)} %param.22) | copy-start | bytes 49156
  43.8 19.4 %all-to-all-start.2 = ((bf16[32,12,512]{2,1,0:T(8,128)(2,1)}), bf16[32,12,512]{2,1,0:T(8,128)(2,1)S(1)}, u32[]{:S(2)}, u32[]{:S(2)}) async-start(bf16[32,12,512]{2,1,0:T(8,128)(2,1)} %convert_element_type.87), calls=%async_computation.2 | async-start | bytes 1048576 | tf_op jit(solution)/shard_map/all_to_all | solution.py:147
  63.2 51.6 %slice-start = ((s8[6291456]{0:T(1024)(128)(4,1)}), s8[4194304]{0:T(1024)(128)(4,1)S(1)}, s32[]{:S(2)}) async-start(s8[6291456]{0:T(1024)(128)(4,1)} %bitcast.107), calls=%async_computation.5 | async-start | bytes 8388608
  63.8 51.0 %copy-start.2 = (bf16[12,4096]{1,0:T(8,128)(2,1)}, bf16[12,4096]{1,0:T(8,128)(2,1)S(1)}, u32[]{:S(2)}) copy-start(bf16[12,4096]{1,0:T(8,128)(2,1)S(1)} %get-tuple-element.7) | copy-start | bytes 294916
  63.9 8.8 %collective-permute-start.2 = (bf16[12,4096]{1,0:T(8,128)(2,1)S(1)}, bf16[12,4096]{1,0:T(8,128)(2,1)S(1)}, u32[]{:S(2)}, u32[]{:S(2)}) collective-permute-start(bf16[12,4096]{1,0:T(8,128)(2,1)S(1)} %fusion.29), channel_id=1, source_target_pairs={{0,16},{16,0},{1,17},{17,1},{2,18},{18,2},{3,19},{19,3},{4,20},{20... | collective-permute-start | bytes 294920 | tf_op jit(solution)/shard_map/ppermute | solution.py:52
  64.7 50.1 %slice-start.1 = ((s8[6291456]{0:T(1024)(128)(4,1)}), s8[2097152]{0:T(1024)(128)(4,1)S(1)}, s32[]{:S(2)}) async-start(s8[6291456]{0:T(1024)(128)(4,1)} %bitcast.107), calls=%async_computation.6 | async-start | bytes 4194304
  73.7 43.9 %slice-start.2 = ((s8[6291456]{0:T(1024)(128)(4,1)}), s8[4194304]{0:T(1024)(128)(4,1)S(1)}, s32[]{:S(2)}) async-start(s8[6291456]{0:T(1024)(128)(4,1)} %bitcast.109), calls=%async_computation.7 | async-start | bytes 8388608
  114.8 2.8 %slice-start.3 = ((s8[6291456]{0:T(1024)(128)(4,1)}), s8[2097152]{0:T(1024)(128)(4,1)S(1)}, s32[]{:S(2)}) async-start(s8[6291456]{0:T(1024)(128)(4,1)} %bitcast.109), calls=%async_computation.8 | async-start | bytes 4194304
  114.8 5.6 %slice-start.4 = ((s8[6291456]{0:T(1024)(128)(4,1)}), s8[4194304]{0:T(1024)(128)(4,1)S(1)}, s32[]{:S(2)}) async-start(s8[6291456]{0:T(1024)(128)(4,1)} %bitcast.111), calls=%async_computation.9 | async-start | bytes 8388608
  117.6 2.8 %slice-start.5 = ((s8[6291456]{0:T(1024)(128)(4,1)}), s8[2097152]{0:T(1024)(128)(4,1)S(1)}, s32[]{:S(2)}) async-start(s8[6291456]{0:T(1024)(128)(4,1)} %bitcast.111), calls=%async_computation.10 | async-start | bytes 4194304
  129.2 40.6 %all-to-all-start.4 = ((bf16[16,576,128]{2,1,0:T(8,128)(2,1)}), bf16[16,576,128]{2,1,0:T(8,128)(2,1)}, u32[]{:S(2)}, u32[]{:S(2)}) async-start(bf16[16,576,128]{2,1,0:T(8,128)(2,1)} %reshape.209), calls=%async_computation.4 | async-start | bytes 4718592 | tf_op jit(solution)/shard_map/all_to_all | solution.py:97
  174.7 3.8 %copy-start.1 = (bf16[288,4096,1]{1,0,2:T(8,128)(2,1)S(1)}, bf16[288,4096,1]{1,0,2:T(8,128)(2,1)}, u32[]{:S(2)}) copy-start(bf16[288,4096,1]{1,0,2:T(8,128)(2,1)} %reshape.221) | copy-start | bytes 7077892
  177.5 8.5 %collective-permute-start.3 = (bf16[12,4096]{1,0:T(8,128)(2,1)S(1)}, bf16[12,4096]{1,0:T(8,128)(2,1)S(1)}, u32[]{:S(2)}, u32[]{:S(2)}) collective-permute-start(bf16[12,4096]{1,0:T(8,128)(2,1)S(1)} %multiply_reduce_fusion), channel_id=1, source_target_pairs={{0,16},{16,0},{1,17},{17,1},{2,18},{18,2},{3,19},{19,3},{4,20},{20... | collective-permute-start | bytes 294920 | tf_op jit(solution)/shard_map/ppermute | solution.py:52

commit v12 on v9

--- a/solution.py
+++ b/solution.py
@@ -58,7 +58,6 @@
     n_half = lax.axis_size("dl") * lax.axis_size("tensor")
     experts_all = 2 * n_half
     capacity = 2 * max(2, 3 * tok_here * chosen_count // experts_all)
-    capacity = -(-capacity // 8) * 8
     side = lax.axis_index("zh")
     other_rows = swap_halves(normed)
     packed = swap_halves(jnp.concatenate([route_ids.astype(jnp.float32), route_weight], axis=1))
@@ -79,24 +78,28 @@
     placement = (
         jnp.arange(n_half * capacity, dtype=jnp.int32)[:, None] == target[None, :]
     ).astype(jnp.bfloat16)
-    token_place = jnp.sum(placement.reshape(n_half, capacity, held, chosen_count), axis=3)
-    outgoing = jnp.einsum(
-        "hcp,pd->hcd", token_place, rows, preferred_element_type=jnp.float32
-    ).astype(jnp.bfloat16)
-    received = lax.all_to_all(outgoing, HALF, split_axis=0, concat_axis=0, tiled=True)
-    gate_part = jnp.einsum("hcd,df->hcf", received, w_gate[0], preferred_element_type=jnp.float32)
-    up_part = jnp.einsum("hcd,df->hcf", received, w_up[0], preferred_element_type=jnp.float32)
+    token_place = jnp.sum(placement.reshape(n_half * capacity, held, chosen_count), axis=2)
+    outgoing = jnp.dot(token_place, rows, preferred_element_type=jnp.float32).astype(jnp.bfloat16)
+    lanes = 128
+    packed_shape = (n_half, capacity * (width // lanes), lanes)
+    received = lax.all_to_all(
+        outgoing.reshape(packed_shape), HALF, split_axis=0, concat_axis=0, tiled=True
+    )
+    flat_rows = received.reshape(n_half * capacity, width)
+    gate_part = jnp.dot(flat_rows, w_gate[0], preferred_element_type=jnp.float32)
+    up_part = jnp.dot(flat_rows, w_up[0], preferred_element_type=jnp.float32)
     activation = (jax.nn.silu(gate_part) * up_part).astype(jnp.bfloat16)
     activation = lax.optimization_barrier(activation)
-    result = jnp.einsum(
-        "hcf,fd->hcd", activation, w_down[0], preferred_element_type=jnp.float32
-    ).astype(jnp.bfloat16)
-    returned = lax.all_to_all(result, HALF, split_axis=0, concat_axis=0, tiled=True)
-    placement = placement.reshape(n_half, capacity, 2, tok_here * chosen_count)
+    result = jnp.dot(activation, w_down[0], preferred_element_type=jnp.float32).astype(jnp.bfloat16)
+    returned = lax.all_to_all(
+        result.reshape(packed_shape), HALF, split_axis=0, concat_axis=0, tiled=True
+    )
+    returned = returned.reshape(n_half * capacity, width)
+    placement = placement.reshape(n_half * capacity, 2, tok_here * chosen_count)
 
     def combine(block, weight):
         pair_rows = jnp.einsum(
-            "hcp,hcd->pd", placement[:, :, block], returned, preferred_element_type=jnp.float32
+            "sp,sd->pd", placement[:, block], returned, preferred_element_type=jnp.float32
         )
         weighted = weight[..., None] * pair_rows.reshape(tok_here, chosen_count, width)
         return jnp.sum(weighted, axis=1)

time: 191 us -> 197 us (1.031)
  local copies, waits for them, and re-layouts: 6.19 us -> 25.1 us
  waiting for transfers between devices: 91.8 us -> 83.7 us
  blocking collectives: 41 us -> 34 us
  matrix products: 22.8 us -> 26.1 us
    reshape x0 -> x4, local copies, waits for them, and re-layouts: none -> 19.9 us  [the longest x1 5.01 us: expert_layer(): outgoing.reshape(packed_shape)]
    all_to_all x1, waiting for transfers between devices: 45.4 us -> 33.5 us  [expert_layer(): lax.all_to_all(result.reshape(packed_shape), HALF, split_axis=0, concat_a...]
    all_to_all x1, blocking collectives: 41 us -> 34 us  [expert_layer(): lax.all_to_all(outgoing.reshape(packed_shape), HALF, split_axis=0, concat...]
    ppermute x4, waiting for transfers between devices: 22.5 us -> 26.3 us  [swap_halves(): return lax.ppermute(x, 'zh', [(0, 1), (1, 0)])]
    dot_general x6, matrix products: 16.5 us -> 19.9 us  [the longest x1 5.62 us: expert_layer(): jnp.dot(flat_rows, w_gate[0], preferred_element_type=jnp.float32)]
  transfers between devices with their start and end apart: 8 -> 8, of which waited for: 7 -> 7; matrix products, arithmetic and copies ran while one was open for 4% -> 2% of each run, Pallas kernels for 0% -> 0%
where the time goes in v12:
time: 197 us; the launch traced here: 196 us
  waiting for transfers between devices  83.7 us (42%)
  blocking collectives  34 us (17%)
  matrix products  26.1 us (13%)
  local copies, waits for them, and re-layouts  25.1 us (13%)
  starting transfers between devices  22.9 us (12%)
  other arithmetic  3.45 us (2%)
    all_to_all x1, blocking collectives, expert_layer(): lax.all_to_all(outgoing.reshape(packed_shape), HALF, split_axis=0, concat...  34 us
    all_to_all x1, waiting for transfers between devices, expert_layer(): lax.all_to_all(result.reshape(packed_shape), HALF, split_axis=0, concat_a...  33.5 us
    ppermute x4, waiting for transfers between devices, swap_halves(): return lax.ppermute(x, 'zh', [(0, 1), (1, 0)])  26.3 us
    all_to_all x1, waiting for transfers between devices, shards(): lax.all_to_all(by_dest.astype(jnp.bfloat16), DP + ('tensor',), split_axis...  13.9 us
    all_to_all x2, waiting for transfers between devices, project(): lax.all_to_all(spread, 'dl', split_axis=0, concat_axis=0, tiled=True)  10.1 us
    all_to_all x2, starting transfers between devices, project(): lax.all_to_all(spread, 'dl', split_axis=0, concat_axis=0, tiled=True)  8.39 us
    all_to_all x1, starting transfers between devices, expert_layer(): lax.all_to_all(result.reshape(packed_shape), HALF, split_axis=0, concat_a...  6.73 us
    dot_general x1, matrix products, expert_layer(): jnp.dot(flat_rows, w_gate[0], preferred_element_type=jnp.float32)  5.62 us
  transfers between devices with their start and end apart: 8, of which 7 were waited for; matrix products, arithmetic and copies ran while one was open for 2% of the time, Pallas kernels for 0%

profile of v12, /device:TPU:7, one launch (start us, length us, event | category | flops | bytes accessed | tf_op | source)
XLA Modules:
  0.0 196.3 jit_solution(11928980875533210595)
XLA Ops:
  0.7 0.9 iota_compare_fusion.2
  1.5 1.0 copy.46
  2.6 0.9 fusion.42
  3.5 2.4 %select_reduce_fusion = (f32[48,16]{1,0:T(8,128)S(1)}, f32[48,16,128]{2,1,0:T(8,128)S(1)}) fusion(pred[48,128]{1,0:T(8,128)(4,1)S(1)} %iota_compare_fusion.2, bf16[48,16,128]{2,1,0:T(8,128)(2,1)S(1)} %bitcast.90, bf16[48,128,128]{2,1,0:T(8,128)(2,1)} %param.17), kind=kOutput, calls=%fused_computation.27 | convolution fusion | flops 25459968 | bytes 2171904 | tf_op jit(solution)/shard_map/rkgd,rckd->rkgc/dot_general | solution.py:27
  5.9 0.3 fusion.28
  6.3 0.6 fusion.26
  7.0 1.0 broadcast_in_dim.31
  8.0 3.7 %all-to-all-start = ((bf16[4,48,2048]{2,1,0:T(8,128)(2,1)}), bf16[4,48,2048]{2,1,0:T(8,128)(2,1)S(1)}, u32[]{:S(2)}, u32[]{:S(2)}) async-start(bf16[4,48,2048]{2,1,0:T(8,128)(2,1)} %broadcast_in_dim.31), calls=%async_computation | async-start | bytes 1572864 | tf_op jit(solution)/shard_map/all_to_all | solution.py:135
  11.7 2.3 %collective-permute-start = (bf16[48,2048]{1,0:T(8,128)(2,1)S(1)}, bf16[48,2048]{1,0:T(8,128)(2,1)S(1)}, u32[]{:S(2)}, u32[]{:S(2)}) collective-permute-start(bf16[48,2048]{1,0:T(8,128)(2,1)S(1)} %bitcast.92), channel_id=1, source_target_pairs={{0,16},{16,0},{1,17},{17,1},{2,18},{18,2},{3,19},{19,3},{4,20},{20... | collective-permute-start | bytes 589832 | tf_op jit(solution)/shard_map/ppermute | solution.py:52
  14.1 0.1 collective-permute-start.1
  14.2 9.5 %collective-permute-done = bf16[48,2048]{1,0:T(8,128)(2,1)S(1)} collective-permute-done((bf16[48,2048]{1,0:T(8,128)(2,1)S(1)}, bf16[48,2048]{1,0:T(8,128)(2,1)S(1)}, u32[]{:S(2)}, u32[]{:S(2)}) %collective-permute-start) | collective-permute-done | bytes 196640 | tf_op jit(solution)/shard_map/ppermute | solution.py:52
  23.7 2.4 %all-to-all-done = bf16[4,48,2048]{2,1,0:T(8,128)(2,1)S(1)} async-done(((bf16[4,48,2048]{2,1,0:T(8,128)(2,1)}), bf16[4,48,2048]{2,1,0:T(8,128)(2,1)S(1)}, u32[]{:S(2)}, u32[]{:S(2)}) %all-to-all-start) | async-done | bytes 786464 | tf_op jit(solution)/shard_map/all_to_all | solution.py:135
  26.1 1.0 broadcast_in_dim.32
  27.1 4.6 %all-to-all-start.1 = ((bf16[4,48,2048]{2,1,0:T(8,128)(2,1)}), bf16[4,48,2048]{2,1,0:T(8,128)(2,1)}, u32[]{:S(2)}, u32[]{:S(2)}) async-start(bf16[4,48,2048]{2,1,0:T(8,128)(2,1)} %broadcast_in_dim.32), calls=%async_computation.1 | async-start | bytes 1572864 | tf_op jit(solution)/shard_map/all_to_all | solution.py:135
  31.9 0.1 sub.40
  32.0 0.6 reduce-window.6
  32.6 0.2 slice_reduce_fusion
  32.9 0.6 fusion.20
  33.4 7.7 %all-to-all-done.1 = bf16[4,48,2048]{2,1,0:T(8,128)(2,1)} async-done(((bf16[4,48,2048]{2,1,0:T(8,128)(2,1)}), bf16[4,48,2048]{2,1,0:T(8,128)(2,1)}, u32[]{:S(2)}, u32[]{:S(2)}) %all-to-all-start.1) | async-done | bytes 786464 | tf_op jit(solution)/shard_map/all_to_all | solution.py:135
  41.1 1.7 fusion.23
  42.9 0.9 convert_element_type.87
  43.8 5.2 %all-to-all-start.2 = ((bf16[32,12,512]{2,1,0:T(8,128)(2,1)}), bf16[32,12,512]{2,1,0:T(8,128)(2,1)S(1)}, u32[]{:S(2)}, u32[]{:S(2)}) async-start(bf16[32,12,512]{2,1,0:T(8,128)(2,1)} %convert_element_type.87), calls=%async_computation.2 | async-start | bytes 1048576 | tf_op jit(solution)/shard_map/all_to_all | solution.py:145
  49.2 0.1 gt.20
  49.3 13.9 %all-to-all-done.2 = bf16[32,12,512]{2,1,0:T(8,128)(2,1)S(1)} async-done(((bf16[32,12,512]{2,1,0:T(8,128)(2,1)}), bf16[32,12,512]{2,1,0:T(8,128)(2,1)S(1)}, u32[]{:S(2)}, u32[]{:S(2)}) %all-to-all-start.2) | async-done | bytes 393248 | tf_op jit(solution)/shard_map/all_to_all | solution.py:145
  63.2 0.1 convert_reduce_fusion
  63.3 0.1 copy.36
  63.4 0.2 copy.48
  63.6 0.2 fusion.30
  63.8 0.1 fusion.32
  64.0 0.2 fusion.40
  64.2 8.6 %collective-permute-done.2 = bf16[12,4096]{1,0:T(8,128)(2,1)S(1)} collective-permute-done((bf16[12,4096]{1,0:T(8,128)(2,1)S(1)}, bf16[12,4096]{1,0:T(8,128)(2,1)S(1)}, u32[]{:S(2)}, u32[]{:S(2)}) %collective-permute-start.2) | collective-permute-done | bytes 98336 | tf_op jit(solution)/shard_map/ppermute | solution.py:52
  72.8 2.2 %convolution_convert_fusion = bf16[288,4096]{1,0:T(8,128)(2,1)} fusion(bf16[288,24]{0,1:T(8,128)(2,1)S(1)} %fusion.40, bf16[12,4096]{1,0:T(8,128)(2,1)S(1)} %collective-permute-done.2, bf16[12,4096]{1,0:T(8,128)(2,1)S(1)} %fusion.32), kind=kOutput, calls=%fused_computation.7 | convolution fusion | flops 58195968 | bytes 2569728 | tf_op jit(solution)/shard_map/dot_general | solution.py:82
  74.9 5.0 %reshape.205 = bf16[16,576,128]{2,1,0:T(8,128)(2,1)} reshape(bf16[288,4096]{1,0:T(8,128)(2,1)} %convolution_convert_fusion) | data formatting | bytes 4718592 | tf_op jit(solution)/shard_map/reshape | solution.py:86
  80.0 34.0 %all_to_all.25 = bf16[16,576,128]{2,1,0:T(8,128)(2,1)} all-to-all(bf16[16,576,128]{2,1,0:T(8,128)(2,1)} %reshape.205), channel_id=1, replica_groups=mesh['zh'=2,'dl'=4,'tensor'=4] {'dl','tensor'}, dimensions={0} | all-to-all | bytes 4718592 | tf_op jit(solution)/shard_map/all_to_all | solution.py:85
  113.9 5.0 %reshape.206 = bf16[288,4096]{1,0:T(8,128)(2,1)} reshape(bf16[16,576,128]{2,1,0:T(8,128)(2,1)} %all_to_all.25) | data formatting | bytes 4718592 | tf_op jit(solution)/shard_map/reshape | solution.py:88
  118.9 5.6 %fusion.4 = f32[288,768]{1,0:T(8,128)S(1)} fusion(bf16[288,4096]{1,0:T(8,128)(2,1)} %reshape.206, bf16[1,4096,768]{2,1,0:T(8,128)(2,1)} %param.25), kind=kOutput, calls=%fused_computation.4 | convolution fusion | flops 1811939328 | bytes 9535488 | tf_op jit(solution)/shard_map/dot_general | solution.py:89
  124.6 5.0 %fusion.17 = bf16[288,768]{1,0:T(8,128)(2,1)S(1)} fusion(bf16[288,4096]{1,0:T(8,128)(2,1)S(1)} %copy-done.2, bf16[1,4096,768]{2,1,0:T(8,128)(2,1)} %param.26, f32[288,768]{1,0:T(8,128)S(1)} %fusion.4), kind=kOutput, calls=%fused_computation.16 | convolution fusion | flops 1813266432 | bytes 9977856 | tf_op jit(solution)/shard_map/dot_general | solution.py:90
  129.6 3.4 %fusion.6 = bf16[288,4096]{1,0:T(8,128)(2,1)} fusion(bf16[288,768]{1,0:T(8,128)(2,1)S(1)} %fusion.17, bf16[1,768,4096]{2,1,0:T(8,128)(2,1)S(1)} %bitcast.98), kind=kOutput, calls=%fused_computation.6 | convolution fusion | flops 1813118976 | bytes 9093120 | tf_op jit(solution)/shard_map/dot_general | solution.py:93
  133.0 5.0 %reshape.207 = bf16[16,576,128]{2,1,0:T(8,128)(2,1)} reshape(bf16[288,4096]{1,0:T(8,128)(2,1)} %fusion.6) | data formatting | bytes 4718592 | tf_op jit(solution)/shard_map/reshape | solution.py:95
  138.0 6.7 %all-to-all-start.4 = ((bf16[16,576,128]{2,1,0:T(8,128)(2,1)}), bf16[16,576,128]{2,1,0:T(8,128)(2,1)}, u32[]{:S(2)}, u32[]{:S(2)}) async-start(bf16[16,576,128]{2,1,0:T(8,128)(2,1)} %reshape.207), calls=%async_computation.4 | async-start | bytes 4718592 | tf_op jit(solution)/shard_map/all_to_all | solution.py:94
  144.8 0.1 gt.19
  145.1 0.1 iota_compare_fusion.1
  145.3 33.5 %all-to-all-done.4 = bf16[16,576,128]{2,1,0:T(8,128)(2,1)} async-done(((bf16[16,576,128]{2,1,0:T(8,128)(2,1)}), bf16[16,576,128]{2,1,0:T(8,128)(2,1)}, u32[]{:S(2)}, u32[]{:S(2)}) %all-to-all-start.4) | async-done | bytes 2359328 | tf_op jit(solution)/shard_map/all_to_all | solution.py:94
  178.7 4.9 %reshape.215 = bf16[288,4096,1]{1,0,2:T(8,128)(2,1)} reshape(bf16[16,576,128]{2,1,0:T(8,128)(2,1)} %all-to-all-done.4) | data formatting | bytes 4718592 | tf_op jit(solution)/shard_map/reshape | solution.py:97
  183.7 2.8 %multiply_reduce_fusion = bf16[12,4096]{1,0:T(8,128)(2,1)S(1)} fusion(f32[12,8]{1,0:T(8,128)S(1)} %copy.41, bf16[288,4096,1]{1,0,2:T(8,128)(2,1)} %reshape.215, pred[288,2,96]{0,2,1:T(32,128)(4,1)S(1)} %iota_compare_fusion.1), kind=kOutput, calls=%fused_computation.13 | convolution fusion | flops 227229696 | bytes 2502656 | tf_op jit(solution)/shard_map/sp,sd->pd/dot_general | solution.py:101
  186.5 0.9 fusion.13
  187.5 8.2 %collective-permute-done.3 = bf16[12,4096]{1,0:T(8,128)(2,1)S(1)} collective-permute-done((bf16[12,4096]{1,0:T(8,128)(2,1)S(1)}, bf16[12,4096]{1,0:T(8,128)(2,1)S(1)}, u32[]{:S(2)}, u32[]{:S(2)}) %collective-permute-start.3) | collective-permute-done | bytes 98336 | tf_op jit(solution)/shard_map/ppermute | solution.py:52
  195.6 0.7 add_convert_fusion
  (55 shorter events, 1.1 us)
Async XLA Ops:
  0.6 32.2 %copy-start = (bf16[2048,512]{1,0:T(8,128)(2,1)S(1)}, bf16[2048,512]{1,0:T(8,128)(2,1)}, u32[]{:S(2)}) copy-start(bf16[2048,512]{1,0:T(8,128)(2,1)} %param.21) | copy-start | bytes 6291460
  0.6 5.6 %copy-start.8 = (bf16[48,128]{1,0:T(8,128)(2,1)S(1)}, bf16[48,128]{1,0:T(8,128)(2,1)}, u32[]{:S(2)}) copy-start(bf16[48,128]{1,0:T(8,128)(2,1)} %param.16) | copy-start | bytes 36868
  0.7 5.6 %copy-start.9 = (bf16[48,128,128]{2,1,0:T(8,128)(2,1)S(1)}, bf16[48,128,128]{2,1,0:T(8,128)(2,1)}, u32[]{:S(2)}) copy-start(bf16[48,128,128]{2,1,0:T(8,128)(2,1)} %param.18) | copy-start | bytes 4718596
  6.3 7.7 %copy-start.6 = (s32[12,8]{0,1:T(8,128)S(1)}, s32[12,8]{0,1:T(8,128)}, u32[]{:S(2)}) copy-start(s32[12,8]{0,1:T(8,128)} %param.23) | copy-start | bytes 1156
  6.3 7.7 %copy-start.7 = (f32[12,8]{0,1:T(8,128)S(1)}, f32[12,8]{0,1:T(8,128)}, u32[]{:S(2)}) copy-start(f32[12,8]{0,1:T(8,128)} %param.24) | copy-start | bytes 1156
  8.0 18.1 %all-to-all-start = ((bf16[4,48,2048]{2,1,0:T(8,128)(2,1)}), bf16[4,48,2048]{2,1,0:T(8,128)(2,1)S(1)}, u32[]{:S(2)}, u32[]{:S(2)}) async-start(bf16[4,48,2048]{2,1,0:T(8,128)(2,1)} %broadcast_in_dim.31), calls=%async_computation | async-start | bytes 1572864 | tf_op jit(solution)/shard_map/all_to_all | solution.py:135
  11.7 12.0 %collective-permute-start = (bf16[48,2048]{1,0:T(8,128)(2,1)S(1)}, bf16[48,2048]{1,0:T(8,128)(2,1)S(1)}, u32[]{:S(2)}, u32[]{:S(2)}) collective-permute-start(bf16[48,2048]{1,0:T(8,128)(2,1)S(1)} %bitcast.92), channel_id=1, source_target_pairs={{0,16},{16,0},{1,17},{17,1},{2,18},{18,2},{3,19},{19,3},{4,20},{20... | collective-permute-start | bytes 589832 | tf_op jit(solution)/shard_map/ppermute | solution.py:52
  14.1 17.7 %collective-permute-start.1 = (f32[12,16]{0,1:T(8,128)S(1)}, f32[12,16]{0,1:T(8,128)S(1)}, u32[]{:S(2)}, u32[]{:S(2)}) collective-permute-start(f32[12,16]{0,1:T(8,128)S(1)} %pad_maximum_fusion), channel_id=1, source_target_pairs={{0,16},{16,0},{1,17},{17,1},{2,18},{18,2},{3,19},{19,3},{4,20},{20... | collective-permute-start | bytes 2312 | tf_op jit(solution)/shard_map/ppermute | solution.py:52
  27.1 14.0 %all-to-all-start.1 = ((bf16[4,48,2048]{2,1,0:T(8,128)(2,1)}), bf16[4,48,2048]{2,1,0:T(8,128)(2,1)}, u32[]{:S(2)}, u32[]{:S(2)}) async-start(bf16[4,48,2048]{2,1,0:T(8,128)(2,1)} %broadcast_in_dim.32), calls=%async_computation.1 | async-start | bytes 1572864 | tf_op jit(solution)/shard_map/all_to_all | solution.py:135
  42.8 20.8 %copy-start.4 = (bf16[12,4096]{1,0:T(8,128)(2,1)S(1)}, bf16[12,4096]{1,0:T(8,128)(2,1)}, u32[]{:S(2)}) copy-start(bf16[12,4096]{1,0:T(8,128)(2,1)} %param.20) | copy-start | bytes 294916
  42.9 20.9 %copy-start.5 = (f32[4096]{0:T(1024)S(1)}, f32[4096]{0:T(1024)}, u32[]{:S(2)}) copy-start(f32[4096]{0:T(1024)} %param.22) | copy-start | bytes 49156
  43.8 19.4 %all-to-all-start.2 = ((bf16[32,12,512]{2,1,0:T(8,128)(2,1)}), bf16[32,12,512]{2,1,0:T(8,128)(2,1)S(1)}, u32[]{:S(2)}, u32[]{:S(2)}) async-start(bf16[32,12,512]{2,1,0:T(8,128)(2,1)} %convert_element_type.87), calls=%async_computation.2 | async-start | bytes 1048576 | tf_op jit(solution)/shard_map/all_to_all | solution.py:145
  63.8 11.2 %copy-start.3 = (bf16[12,4096]{1,0:T(8,128)(2,1)}, bf16[12,4096]{1,0:T(8,128)(2,1)S(1)}, u32[]{:S(2)}) copy-start(bf16[12,4096]{1,0:T(8,128)(2,1)S(1)} %get-tuple-element.7) | copy-start | bytes 294916
  63.9 8.8 %collective-permute-start.2 = (bf16[12,4096]{1,0:T(8,128)(2,1)S(1)}, bf16[12,4096]{1,0:T(8,128)(2,1)S(1)}, u32[]{:S(2)}, u32[]{:S(2)}) collective-permute-start(bf16[12,4096]{1,0:T(8,128)(2,1)S(1)} %fusion.32), channel_id=1, source_target_pairs={{0,16},{16,0},{1,17},{17,1},{2,18},{18,2},{3,19},{19,3},{4,20},{20... | collective-permute-start | bytes 294920 | tf_op jit(solution)/shard_map/ppermute | solution.py:52
  118.9 5.6 %copy-start.2 = (bf16[288,4096]{1,0:T(8,128)(2,1)S(1)}, bf16[288,4096]{1,0:T(8,128)(2,1)}, u32[]{:S(2)}) copy-start(bf16[288,4096]{1,0:T(8,128)(2,1)} %reshape.206) | copy-start | bytes 7077892
  118.9 10.6 %slice-start = ((s8[6291456]{0:T(1024)(128)(4,1)}), s8[4194304]{0:T(1024)(128)(4,1)S(1)}, s32[]{:S(2)}) async-start(s8[6291456]{0:T(1024)(128)(4,1)} %bitcast.97), calls=%async_computation.5 | async-start | bytes 8388608
  124.6 5.0 %slice-start.1 = ((s8[6291456]{0:T(1024)(128)(4,1)}), s8[2097152]{0:T(1024)(128)(4,1)S(1)}, s32[]{:S(2)}) async-start(s8[6291456]{0:T(1024)(128)(4,1)} %bitcast.97), calls=%async_computation.6 | async-start | bytes 4194304
  138.0 40.7 %all-to-all-start.4 = ((bf16[16,576,128]{2,1,0:T(8,128)(2,1)}), bf16[16,576,128]{2,1,0:T(8,128)(2,1)}, u32[]{:S(2)}, u32[]{:S(2)}) async-start(bf16[16,576,128]{2,1,0:T(8,128)(2,1)} %reshape.207), calls=%async_computation.4 | async-start | bytes 4718592 | tf_op jit(solution)/shard_map/all_to_all | solution.py:94
  183.7 2.8 %copy-start.1 = (bf16[288,4096,1]{1,0,2:T(8,128)(2,1)S(1)}, bf16[288,4096,1]{1,0,2:T(8,128)(2,1)}, u32[]{:S(2)}) copy-start(bf16[288,4096,1]{1,0,2:T(8,128)(2,1)} %reshape.215) | copy-start | bytes 7077892
  186.4 9.2 %collective-permute-start.3 = (bf16[12,4096]{1,0:T(8,128)(2,1)S(1)}, bf16[12,4096]{1,0:T(8,128)(2,1)S(1)}, u32[]{:S(2)}, u32[]{:S(2)}) collective-permute-start(bf16[12,4096]{1,0:T(8,128)(2,1)S(1)} %multiply_reduce_fusion), channel_id=1, source_target_pairs={{0,16},{16,0},{1,17},{17,1},{2,18},{18,2},{3,19},{19,3},{4,20},{20... | collective-permute-start | bytes 294920 | tf_op jit(solution)/shard_map/ppermute | solution.py:52

commit v13 on v11

--- a/solution.py
+++ b/solution.py
@@ -80,9 +80,13 @@
         jnp.arange(n_half * capacity, dtype=jnp.int32)[:, None] == target[None, :]
     ).astype(jnp.bfloat16)
     token_place = jnp.sum(placement.reshape(n_half, capacity, held, chosen_count), axis=3)
-    outgoing = jnp.einsum(
-        "hcp,pd->hcd", token_place, rows, preferred_element_type=jnp.float32
-    ).astype(jnp.bfloat16)
+    own_part = jnp.einsum(
+        "hcp,pd->hcd", token_place[:, :, :tok_here], normed, preferred_element_type=jnp.float32
+    )
+    other_part = jnp.einsum(
+        "hcp,pd->hcd", token_place[:, :, tok_here:], other_rows, preferred_element_type=jnp.float32
+    )
+    outgoing = (own_part + other_part).astype(jnp.bfloat16)
     received = lax.all_to_all(outgoing, HALF, split_axis=0, concat_axis=0, tiled=True)
     gate_part = jnp.einsum("hcd,df->hcf", received, w_gate[0], preferred_element_type=jnp.float32)
     up_part = jnp.einsum("hcd,df->hcf", received, w_up[0], preferred_element_type=jnp.float32)

time: 187 us -> 188 us (level)
  no operation moved by 1% of the time
where the time goes in v13:
time: 188 us; the launch traced here: 187 us
  waiting for transfers between devices  80.8 us (43%)
  blocking collectives  41 us (22%)
  starting transfers between devices  23.6 us (13%)
  matrix products  21.4 us (11%)
  local copies, waits for them, and re-layouts  15.3 us (8%)
  other arithmetic  4.02 us (2%)
    all_to_all x1, blocking collectives, expert_layer(): lax.all_to_all(outgoing, HALF, split_axis=0, concat_axis=0, tiled=True)  41 us
    all_to_all x1, waiting for transfers between devices, expert_layer(): lax.all_to_all(back, HALF, split_axis=0, concat_axis=0, tiled=True)  33.1 us
    ppermute x4, waiting for transfers between devices, swap_halves(): return lax.ppermute(x, 'zh', [(0, 1), (1, 0)])  24.6 us
    all_to_all x1, waiting for transfers between devices, shards(): lax.all_to_all(by_dest.astype(jnp.bfloat16), DP + ('tensor',), split_axis...  13.1 us
    all_to_all x2, waiting for transfers between devices, project(): lax.all_to_all(spread, 'dl', split_axis=0, concat_axis=0, tiled=True)  10.1 us
    all_to_all x2, starting transfers between devices, project(): lax.all_to_all(spread, 'dl', split_axis=0, concat_axis=0, tiled=True)  8.39 us
    all_to_all x1, starting transfers between devices, expert_layer(): lax.all_to_all(back, HALF, split_axis=0, concat_axis=0, tiled=True)  6.56 us
    all_to_all x1, starting transfers between devices, shards(): lax.all_to_all(by_dest.astype(jnp.bfloat16), DP + ('tensor',), split_axis...  5.19 us
  transfers between devices with their start and end apart: 8, of which 7 were waited for; matrix products, arithmetic and copies ran while one was open for 3% of the time, Pallas kernels for 0%

profile of v13, /device:TPU:7, one launch (start us, length us, event | category | flops | bytes accessed | tf_op | source)
XLA Modules:
  0.0 187.3 jit_solution(15495479198684064826)
XLA Ops:
  0.7 0.9 iota_compare_fusion
  1.5 1.0 copy.52
  2.6 0.9 fusion.44
  3.5 2.4 %select_reduce_fusion = (f32[48,16]{1,0:T(8,128)S(1)}, f32[48,16,128]{2,1,0:T(8,128)S(1)}) fusion(pred[48,128]{1,0:T(8,128)(4,1)S(1)} %iota_compare_fusion, bf16[48,16,128]{2,1,0:T(8,128)(2,1)S(1)} %bitcast.101, bf16[48,128,128]{2,1,0:T(8,128)(2,1)} %param.17), kind=kOutput, calls=%fused_computation.29 | convolution fusion | flops 25459968 | bytes 2171904 | tf_op jit(solution)/shard_map/rkgd,rckd->rkgc/dot_general | solution.py:27
  5.9 0.3 fusion.26
  6.3 0.6 fusion.23
  7.0 1.0 broadcast_in_dim.31
  8.0 3.7 %all-to-all-start = ((bf16[4,48,2048]{2,1,0:T(8,128)(2,1)}), bf16[4,48,2048]{2,1,0:T(8,128)(2,1)S(1)}, u32[]{:S(2)}, u32[]{:S(2)}) async-start(bf16[4,48,2048]{2,1,0:T(8,128)(2,1)} %broadcast_in_dim.31), calls=%async_computation | async-start | bytes 1572864 | tf_op jit(solution)/shard_map/all_to_all | solution.py:141
  11.7 2.3 %collective-permute-start = (bf16[48,2048]{1,0:T(8,128)(2,1)S(1)}, bf16[48,2048]{1,0:T(8,128)(2,1)S(1)}, u32[]{:S(2)}, u32[]{:S(2)}) collective-permute-start(bf16[48,2048]{1,0:T(8,128)(2,1)S(1)} %bitcast.103), channel_id=1, source_target_pairs={{0,16},{16,0},{1,17},{17,1},{2,18},{18,2},{3,19},{19,3},{4,20},{20... | collective-permute-start | bytes 589832 | tf_op jit(solution)/shard_map/ppermute | solution.py:52
  14.1 0.1 collective-permute-start.1
  14.2 9.5 %collective-permute-done = bf16[48,2048]{1,0:T(8,128)(2,1)S(1)} collective-permute-done((bf16[48,2048]{1,0:T(8,128)(2,1)S(1)}, bf16[48,2048]{1,0:T(8,128)(2,1)S(1)}, u32[]{:S(2)}, u32[]{:S(2)}) %collective-permute-start) | collective-permute-done | bytes 196640 | tf_op jit(solution)/shard_map/ppermute | solution.py:52
  23.7 2.4 %all-to-all-done = bf16[4,48,2048]{2,1,0:T(8,128)(2,1)S(1)} async-done(((bf16[4,48,2048]{2,1,0:T(8,128)(2,1)}), bf16[4,48,2048]{2,1,0:T(8,128)(2,1)S(1)}, u32[]{:S(2)}, u32[]{:S(2)}) %all-to-all-start) | async-done | bytes 786464 | tf_op jit(solution)/shard_map/all_to_all | solution.py:141
  26.1 1.0 broadcast_in_dim.32
  27.1 4.6 %all-to-all-start.1 = ((bf16[4,48,2048]{2,1,0:T(8,128)(2,1)}), bf16[4,48,2048]{2,1,0:T(8,128)(2,1)}, u32[]{:S(2)}, u32[]{:S(2)}) async-start(bf16[4,48,2048]{2,1,0:T(8,128)(2,1)} %broadcast_in_dim.32), calls=%async_computation.1 | async-start | bytes 1572864 | tf_op jit(solution)/shard_map/all_to_all | solution.py:141
  32.1 0.6 reduce-window.6
  32.6 0.2 slice_reduce_fusion
  32.9 0.6 fusion.17
  33.5 7.7 %all-to-all-done.1 = bf16[4,48,2048]{2,1,0:T(8,128)(2,1)} async-done(((bf16[4,48,2048]{2,1,0:T(8,128)(2,1)}), bf16[4,48,2048]{2,1,0:T(8,128)(2,1)}, u32[]{:S(2)}, u32[]{:S(2)}) %all-to-all-start.1) | async-done | bytes 786464 | tf_op jit(solution)/shard_map/all_to_all | solution.py:141
  41.1 1.7 fusion.20
  42.9 0.9 convert_element_type.87
  43.8 5.2 %all-to-all-start.2 = ((bf16[32,12,512]{2,1,0:T(8,128)(2,1)}), bf16[32,12,512]{2,1,0:T(8,128)(2,1)S(1)}, u32[]{:S(2)}, u32[]{:S(2)}) async-start(bf16[32,12,512]{2,1,0:T(8,128)(2,1)} %convert_element_type.87), calls=%async_computation.2 | async-start | bytes 1048576 | tf_op jit(solution)/shard_map/all_to_all | solution.py:151
  49.2 0.1 gt.20
  49.4 0.7 fusion.24
  50.1 13.1 %all-to-all-done.2 = bf16[32,12,512]{2,1,0:T(8,128)(2,1)S(1)} async-done(((bf16[32,12,512]{2,1,0:T(8,128)(2,1)}), bf16[32,12,512]{2,1,0:T(8,128)(2,1)S(1)}, u32[]{:S(2)}, u32[]{:S(2)}) %all-to-all-start.2) | async-done | bytes 393248 | tf_op jit(solution)/shard_map/all_to_all | solution.py:151
  63.2 0.1 convert_reduce_fusion
  63.3 0.1 copy.35
  63.5 0.2 copy.54
  63.6 0.2 fusion.27
  63.8 0.1 fusion.29
  64.0 0.9 fusion.40
  65.0 7.8 %collective-permute-done.2 = bf16[12,4096]{1,0:T(8,128)(2,1)S(1)} collective-permute-done((bf16[12,4096]{1,0:T(8,128)(2,1)S(1)}, bf16[12,4096]{1,0:T(8,128)(2,1)S(1)}, u32[]{:S(2)}, u32[]{:S(2)}) %collective-permute-start.2) | collective-permute-done | bytes 98336 | tf_op jit(solution)/shard_map/ppermute | solution.py:52
  72.8 1.0 add_convert_fusion
  73.8 41.0 %all_to_all.25 = bf16[16,24,4096]{2,1,0:T(8,128)(2,1)S(1)} all-to-all(bf16[16,24,4096]{2,1,0:T(8,128)(2,1)S(1)} %add_convert_fusion), channel_id=1, replica_groups=mesh['zh'=2,'dl'=4,'tensor'=4] {'dl','tensor'}, dimensions={0} | all-to-all | bytes 6291456 | tf_op jit(solution)/shard_map/all_to_all | solution.py:90
  114.9 2.7 %fusion.4 = f32[16,24,768]{2,1,0:T(8,128)S(1)} fusion(bf16[16,24,4096]{2,1,0:T(8,128)(2,1)S(1)} %all_to_all.25, bf16[1,4096,768]{2,1,0:T(8,128)(2,1)S(1)} %bitcast.110), kind=kOutput, calls=%fused_computation.5 | convolution fusion | flops 2415919104 | bytes 10616832 | tf_op jit(solution)/shard_map/hcd,df->hcf/dot_general | solution.py:91
  117.7 2.8 %fusion.14 = bf16[16,24,768]{2,1,0:T(8,128)(2,1)S(1)} fusion(bf16[16,24,4096]{2,1,0:T(8,128)(2,1)S(1)} %all_to_all.25, bf16[1,4096,768]{2,1,0:T(8,128)(2,1)S(1)} %bitcast.112, f32[16,24,768]{2,1,0:T(8,128)S(1)} %fusion.4), kind=kOutput, calls=%fused_computation.17 | convolution fusion | flops 2417688576 | bytes 11206656 | tf_op jit(solution)/shard_map/hcd,df->hcf/dot_general | solution.py:92
  120.5 4.0 %fusion = bf16[16,24,4096]{2,1,0:T(8,128)(2,1)} fusion(bf16[16,24,768]{2,1,0:T(8,128)(2,1)S(1)} %fusion.14, bf16[1,768,4096]{2,1,0:T(8,128)(2,1)S(1)} %bitcast.114), kind=kOutput, calls=%fused_computation.1 | convolution fusion | flops 2415919104 | bytes 10027008 | tf_op jit(solution)/shard_map/hcf,fd->hcd/dot_general | solution.py:95
  124.5 4.6 %reshape.209 = bf16[16,576,128]{2,1,0:T(8,128)(2,1)} reshape(bf16[16,18,4096]{2,1,0:T(8,128)(2,1)} %bitcast.96) | data formatting | bytes 4718592 | tf_op jit(solution)/shard_map/reshape | solution.py:100
  129.2 6.6 %all-to-all-start.4 = ((bf16[16,576,128]{2,1,0:T(8,128)(2,1)}), bf16[16,576,128]{2,1,0:T(8,128)(2,1)}, u32[]{:S(2)}, u32[]{:S(2)}) async-start(bf16[16,576,128]{2,1,0:T(8,128)(2,1)} %reshape.209), calls=%async_computation.4 | async-start | bytes 4718592 | tf_op jit(solution)/shard_map/all_to_all | solution.py:101
  136.1 0.1 broadcast_compare_fusion
  136.3 0.1 copy.45
  136.5 0.1 copy.40
  136.7 33.1 %all-to-all-done.4 = bf16[16,576,128]{2,1,0:T(8,128)(2,1)} async-done(((bf16[16,576,128]{2,1,0:T(8,128)(2,1)}), bf16[16,576,128]{2,1,0:T(8,128)(2,1)}, u32[]{:S(2)}, u32[]{:S(2)}) %all-to-all-start.4) | async-done | bytes 2359328 | tf_op jit(solution)/shard_map/all_to_all | solution.py:101
  169.7 5.0 %reshape.222 = bf16[288,4096,1]{1,0,2:T(8,128)(2,1)} reshape(bf16[16,576,128]{2,1,0:T(8,128)(2,1)} %all-to-all-done.4) | data formatting | bytes 4718592 | tf_op jit(solution)/shard_map/reshape | solution.py:102
  174.7 2.7 %multiply_reduce_fusion = bf16[12,4096]{1,0:T(8,128)(2,1)S(1)} fusion(f32[12,8]{1,0:T(8,128)S(1)} %copy.44, bf16[288,4096,1]{1,0,2:T(8,128)(2,1)} %reshape.222, pred[96,288]{1,0:T(8,128)(4,1)S(1)} %copy.45), kind=kOutput, calls=%fused_computation.13 | convolution fusion | flops 227229696 | bytes 2485632 | tf_op jit(solution)/shard_map/sp,sd->pd/dot_general | solution.py:107
  177.4 1.0 collective-permute-start.3
  178.4 0.9 fusion.13
  179.4 7.3 %collective-permute-done.3 = bf16[12,4096]{1,0:T(8,128)(2,1)S(1)} collective-permute-done((bf16[12,4096]{1,0:T(8,128)(2,1)S(1)}, bf16[12,4096]{1,0:T(8,128)(2,1)S(1)}, u32[]{:S(2)}, u32[]{:S(2)}) %collective-permute-start.3) | collective-permute-done | bytes 98336 | tf_op jit(solution)/shard_map/ppermute | solution.py:52
  186.7 0.7 add_convert_fusion.1
  (68 shorter events, 1.4 us)
Async XLA Ops:
  0.6 32.2 %copy-start = (bf16[2048,512]{1,0:T(8,128)(2,1)S(1)}, bf16[2048,512]{1,0:T(8,128)(2,1)}, u32[]{:S(2)}) copy-start(bf16[2048,512]{1,0:T(8,128)(2,1)} %param.21) | copy-start | bytes 6291460
  0.6 5.6 %copy-start.7 = (bf16[48,128]{1,0:T(8,128)(2,1)S(1)}, bf16[48,128]{1,0:T(8,128)(2,1)}, u32[]{:S(2)}) copy-start(bf16[48,128]{1,0:T(8,128)(2,1)} %param.16) | copy-start | bytes 36868
  0.7 5.6 %copy-start.8 = (bf16[48,128,128]{2,1,0:T(8,128)(2,1)S(1)}, bf16[48,128,128]{2,1,0:T(8,128)(2,1)}, u32[]{:S(2)}) copy-start(bf16[48,128,128]{2,1,0:T(8,128)(2,1)} %param.18) | copy-start | bytes 4718596
  6.3 7.7 %copy-start.5 = (s32[12,8]{0,1:T(8,128)S(1)}, s32[12,8]{0,1:T(8,128)}, u32[]{:S(2)}) copy-start(s32[12,8]{0,1:T(8,128)} %param.23) | copy-start | bytes 1156
  6.3 7.7 %copy-start.6 = (f32[12,8]{0,1:T(8,128)S(1)}, f32[12,8]{0,1:T(8,128)}, u32[]{:S(2)}) copy-start(f32[12,8]{0,1:T(8,128)} %param.24) | copy-start | bytes 1156
  8.0 18.1 %all-to-all-start = ((bf16[4,48,2048]{2,1,0:T(8,128)(2,1)}), bf16[4,48,2048]{2,1,0:T(8,128)(2,1)S(1)}, u32[]{:S(2)}, u32[]{:S(2)}) async-start(bf16[4,48,2048]{2,1,0:T(8,128)(2,1)} %broadcast_in_dim.31), calls=%async_computation | async-start | bytes 1572864 | tf_op jit(solution)/shard_map/all_to_all | solution.py:141
  11.7 12.0 %collective-permute-start = (bf16[48,2048]{1,0:T(8,128)(2,1)S(1)}, bf16[48,2048]{1,0:T(8,128)(2,1)S(1)}, u32[]{:S(2)}, u32[]{:S(2)}) collective-permute-start(bf16[48,2048]{1,0:T(8,128)(2,1)S(1)} %bitcast.103), channel_id=1, source_target_pairs={{0,16},{16,0},{1,17},{17,1},{2,18},{18,2},{3,19},{19,3},{4,20},{20... | collective-permute-start | bytes 589832 | tf_op jit(solution)/shard_map/ppermute | solution.py:52
  14.1 17.7 %collective-permute-start.1 = (f32[12,16]{0,1:T(8,128)S(1)}, f32[12,16]{0,1:T(8,128)S(1)}, u32[]{:S(2)}, u32[]{:S(2)}) collective-permute-start(f32[12,16]{0,1:T(8,128)S(1)} %pad_maximum_fusion), channel_id=1, source_target_pairs={{0,16},{16,0},{1,17},{17,1},{2,18},{18,2},{3,19},{19,3},{4,20},{20... | collective-permute-start | bytes 2312 | tf_op jit(solution)/shard_map/ppermute | solution.py:52
  27.1 14.0 %all-to-all-start.1 = ((bf16[4,48,2048]{2,1,0:T(8,128)(2,1)}), bf16[4,48,2048]{2,1,0:T(8,128)(2,1)}, u32[]{:S(2)}, u32[]{:S(2)}) async-start(bf16[4,48,2048]{2,1,0:T(8,128)(2,1)} %broadcast_in_dim.32), calls=%async_computation.1 | async-start | bytes 1572864 | tf_op jit(solution)/shard_map/all_to_all | solution.py:141
  42.9 20.7 %copy-start.3 = (bf16[12,4096]{1,0:T(8,128)(2,1)S(1)}, bf16[12,4096]{1,0:T(8,128)(2,1)}, u32[]{:S(2)}) copy-start(bf16[12,4096]{1,0:T(8,128)(2,1)} %param.20) | copy-start | bytes 294916
  42.9 20.9 %copy-start.4 = (f32[4096]{0:T(1024)S(1)}, f32[4096]{0:T(1024)}, u32[]{:S(2)}) copy-start(f32[4096]{0:T(1024)} %param.22) | copy-start | bytes 49156
  43.8 19.4 %all-to-all-start.2 = ((bf16[32,12,512]{2,1,0:T(8,128)(2,1)}), bf16[32,12,512]{2,1,0:T(8,128)(2,1)S(1)}, u32[]{:S(2)}, u32[]{:S(2)}) async-start(bf16[32,12,512]{2,1,0:T(8,128)(2,1)} %convert_element_type.87), calls=%async_computation.2 | async-start | bytes 1048576 | tf_op jit(solution)/shard_map/all_to_all | solution.py:151
  63.8 1.2 copy-start.2
  63.9 8.8 %collective-permute-start.2 = (bf16[12,4096]{1,0:T(8,128)(2,1)S(1)}, bf16[12,4096]{1,0:T(8,128)(2,1)S(1)}, u32[]{:S(2)}, u32[]{:S(2)}) collective-permute-start(bf16[12,4096]{1,0:T(8,128)(2,1)S(1)} %fusion.29), channel_id=1, source_target_pairs={{0,16},{16,0},{1,17},{17,1},{2,18},{18,2},{3,19},{19,3},{4,20},{20... | collective-permute-start | bytes 294920 | tf_op jit(solution)/shard_map/ppermute | solution.py:52
  64.0 50.9 %slice-start = ((s8[6291456]{0:T(1024)(128)(4,1)}), s8[4194304]{0:T(1024)(128)(4,1)S(1)}, s32[]{:S(2)}) async-start(s8[6291456]{0:T(1024)(128)(4,1)} %bitcast.109), calls=%async_computation.5 | async-start | bytes 8388608
  65.0 49.9 %slice-start.1 = ((s8[6291456]{0:T(1024)(128)(4,1)}), s8[2097152]{0:T(1024)(128)(4,1)S(1)}, s32[]{:S(2)}) async-start(s8[6291456]{0:T(1024)(128)(4,1)} %bitcast.109), calls=%async_computation.6 | async-start | bytes 4194304
  73.8 43.8 %slice-start.2 = ((s8[6291456]{0:T(1024)(128)(4,1)}), s8[4194304]{0:T(1024)(128)(4,1)S(1)}, s32[]{:S(2)}) async-start(s8[6291456]{0:T(1024)(128)(4,1)} %bitcast.111), calls=%async_computation.7 | async-start | bytes 8388608
  114.9 2.8 %slice-start.3 = ((s8[6291456]{0:T(1024)(128)(4,1)}), s8[2097152]{0:T(1024)(128)(4,1)S(1)}, s32[]{:S(2)}) async-start(s8[6291456]{0:T(1024)(128)(4,1)} %bitcast.111), calls=%async_computation.8 | async-start | bytes 4194304
  114.9 5.6 %slice-start.4 = ((s8[6291456]{0:T(1024)(128)(4,1)}), s8[2097152]{0:T(1024)(128)(4,1)S(1)}, s32[]{:S(2)}) async-start(s8[6291456]{0:T(1024)(128)(4,1)} %bitcast.113), calls=%async_computation.9 | async-start | bytes 4194304
  117.6 2.8 %slice-start.5 = ((s8[6291456]{0:T(1024)(128)(4,1)}), s8[4194304]{0:T(1024)(128)(4,1)S(1)}, s32[]{:S(2)}) async-start(s8[6291456]{0:T(1024)(128)(4,1)} %bitcast.113), calls=%async_computation.10 | async-start | bytes 8388608
  129.2 40.6 %all-to-all-start.4 = ((bf16[16,576,128]{2,1,0:T(8,128)(2,1)}), bf16[16,576,128]{2,1,0:T(8,128)(2,1)}, u32[]{:S(2)}, u32[]{:S(2)}) async-start(bf16[16,576,128]{2,1,0:T(8,128)(2,1)} %reshape.209), calls=%async_computation.4 | async-start | bytes 4718592 | tf_op jit(solution)/shard_map/all_to_all | solution.py:101
  174.7 3.8 %copy-start.1 = (bf16[288,4096,1]{1,0,2:T(8,128)(2,1)S(1)}, bf16[288,4096,1]{1,0,2:T(8,128)(2,1)}, u32[]{:S(2)}) copy-start(bf16[288,4096,1]{1,0,2:T(8,128)(2,1)} %reshape.222) | copy-start | bytes 7077892
  177.4 9.2 %collective-permute-start.3 = (bf16[12,4096]{1,0:T(8,128)(2,1)S(1)}, bf16[12,4096]{1,0:T(8,128)(2,1)S(1)}, u32[]{:S(2)}, u32[]{:S(2)}) collective-permute-start(bf16[12,4096]{1,0:T(8,128)(2,1)S(1)} %multiply_reduce_fusion), channel_id=1, source_target_pairs={{0,16},{16,0},{1,17},{17,1},{2,18},{18,2},{3,19},{19,3},{4,20},{20... | collective-permute-start | bytes 294920 | tf_op jit(solution)/shard_map/ppermute | solution.py:52

commit v14 on v11

--- a/solution.py
+++ b/solution.py
@@ -99,10 +99,13 @@
     placement = placement.reshape(n_half, capacity, 2, tok_here * chosen_count)[:, :used]
     placement = placement.reshape(n_half * used, 2, tok_here * chosen_count)
 
+    slot_of = target.reshape(2, tok_here * chosen_count)
+
     def combine(block, weight):
-        pair_rows = jnp.einsum(
-            "sp,sd->pd", placement[:, block], returned, preferred_element_type=jnp.float32
-        )
+        slot = slot_of[block]
+        slot = jnp.where(slot >= 0, (slot // capacity) * used + slot % capacity, -1)
+        picked = jnp.take(returned, jnp.maximum(slot, 0), axis=0)
+        pair_rows = jnp.where((slot >= 0)[:, None], picked.astype(jnp.float32), 0.0)
         weighted = weight[..., None] * pair_rows.reshape(tok_here, chosen_count, width)
         return jnp.sum(weighted, axis=1)
 

time: 187 us -> 189 us (1.011)
  local copies, waits for them, and re-layouts: 15.3 us -> 22.1 us
  matrix products: 20.5 us -> 16.8 us
  waiting for transfers between devices: 81.1 us -> 78.2 us
    gather x0 -> x2, local copies, waits for them, and re-layouts: none -> 7.51 us  [combine(): picked = jnp.take(returned, jnp.maximum(slot, 0), axis=0)]
    dot_general x2 -> x0, matrix products: 3.68 us -> none  [combine(): jnp.einsum('sp,sd->pd', placement[:, block], returned, preferred_element_...]
    ppermute x4, waiting for transfers between devices: 24.2 us -> 20.7 us  [swap_halves(): return lax.ppermute(x, 'zh', [(0, 1), (1, 0)])]
  transfers between devices with their start and end apart: 8 -> 8, of which waited for: 7 -> 7; matrix products, arithmetic and copies ran while one was open for 3% -> 4% of each run, Pallas kernels for 0% -> 0%
where the time goes in v14:
time: 189 us; the launch traced here: 188 us
  waiting for transfers between devices  78.2 us (41%)
  blocking collectives  41 us (22%)
  starting transfers between devices  23.6 us (12%)
  local copies, waits for them, and re-layouts  22.1 us (12%)
  matrix products  16.8 us (9%)
  other arithmetic  5.38 us (3%)
    all_to_all x1, blocking collectives, expert_layer(): lax.all_to_all(outgoing, HALF, split_axis=0, concat_axis=0, tiled=True)  41 us
    all_to_all x1, waiting for transfers between devices, expert_layer(): lax.all_to_all(back, HALF, split_axis=0, concat_axis=0, tiled=True)  33.7 us
    ppermute x4, waiting for transfers between devices, swap_halves(): return lax.ppermute(x, 'zh', [(0, 1), (1, 0)])  20.7 us
    all_to_all x1, waiting for transfers between devices, shards(): lax.all_to_all(by_dest.astype(jnp.bfloat16), DP + ('tensor',), split_axis...  13.8 us
    all_to_all x2, waiting for transfers between devices, project(): lax.all_to_all(spread, 'dl', split_axis=0, concat_axis=0, tiled=True)  10.1 us
    all_to_all x2, starting transfers between devices, project(): lax.all_to_all(spread, 'dl', split_axis=0, concat_axis=0, tiled=True)  8.39 us
    gather x2, local copies, waits for them, and re-layouts, combine(): picked = jnp.take(returned, jnp.maximum(slot, 0), axis=0)  7.51 us
    all_to_all x1, starting transfers between devices, expert_layer(): lax.all_to_all(back, HALF, split_axis=0, concat_axis=0, tiled=True)  6.56 us
  transfers between devices with their start and end apart: 8, of which 7 were waited for; matrix products, arithmetic and copies ran while one was open for 4% of the time, Pallas kernels for 0%

profile of v14, /device:TPU:7, one launch (start us, length us, event | category | flops | bytes accessed | tf_op | source)
XLA Modules:
  0.0 188.3 jit_solution(16263535997969984753)
XLA Ops:
  0.7 0.9 iota_compare_fusion
  1.5 1.0 copy.42
  2.6 0.9 fusion.37
  3.5 2.4 %select_reduce_fusion = (f32[48,16]{1,0:T(8,128)S(1)}, f32[48,16,128]{2,1,0:T(8,128)S(1)}) fusion(pred[48,128]{1,0:T(8,128)(4,1)S(1)} %iota_compare_fusion, bf16[48,16,128]{2,1,0:T(8,128)(2,1)S(1)} %bitcast.86, bf16[48,128,128]{2,1,0:T(8,128)(2,1)} %param.19), kind=kOutput, calls=%fused_computation.32 | convolution fusion | flops 25459968 | bytes 2171904 | tf_op jit(solution)/shard_map/rkgd,rckd->rkgc/dot_general | solution.py:27
  5.9 0.3 fusion.27
  6.3 0.6 fusion.24
  7.0 1.0 broadcast_in_dim.86
  8.0 3.7 %all-to-all-start = ((bf16[4,48,2048]{2,1,0:T(8,128)(2,1)}), bf16[4,48,2048]{2,1,0:T(8,128)(2,1)S(1)}, u32[]{:S(2)}, u32[]{:S(2)}) async-start(bf16[4,48,2048]{2,1,0:T(8,128)(2,1)} %broadcast_in_dim.86), calls=%async_computation | async-start | bytes 1572864 | tf_op jit(solution)/shard_map/all_to_all | solution.py:140
  11.7 2.3 %collective-permute-start = (bf16[48,2048]{1,0:T(8,128)(2,1)S(1)}, bf16[48,2048]{1,0:T(8,128)(2,1)S(1)}, u32[]{:S(2)}, u32[]{:S(2)}) collective-permute-start(bf16[48,2048]{1,0:T(8,128)(2,1)S(1)} %bitcast.88), channel_id=1, source_target_pairs={{0,16},{16,0},{1,17},{17,1},{2,18},{18,2},{3,19},{19,3},{4,20},{20... | collective-permute-start | bytes 589832 | tf_op jit(solution)/shard_map/ppermute | solution.py:52
  14.0 0.1 collective-permute-start.1
  14.2 9.5 %collective-permute-done = bf16[48,2048]{1,0:T(8,128)(2,1)S(1)} collective-permute-done((bf16[48,2048]{1,0:T(8,128)(2,1)S(1)}, bf16[48,2048]{1,0:T(8,128)(2,1)S(1)}, u32[]{:S(2)}, u32[]{:S(2)}) %collective-permute-start) | collective-permute-done | bytes 196640 | tf_op jit(solution)/shard_map/ppermute | solution.py:52
  23.7 2.4 %all-to-all-done = bf16[4,48,2048]{2,1,0:T(8,128)(2,1)S(1)} async-done(((bf16[4,48,2048]{2,1,0:T(8,128)(2,1)}), bf16[4,48,2048]{2,1,0:T(8,128)(2,1)S(1)}, u32[]{:S(2)}, u32[]{:S(2)}) %all-to-all-start) | async-done | bytes 786464 | tf_op jit(solution)/shard_map/all_to_all | solution.py:140
  26.1 1.0 broadcast_in_dim.87
  27.1 4.6 %all-to-all-start.1 = ((bf16[4,48,2048]{2,1,0:T(8,128)(2,1)}), bf16[4,48,2048]{2,1,0:T(8,128)(2,1)}, u32[]{:S(2)}, u32[]{:S(2)}) async-start(bf16[4,48,2048]{2,1,0:T(8,128)(2,1)} %broadcast_in_dim.87), calls=%async_computation.1 | async-start | bytes 1572864 | tf_op jit(solution)/shard_map/all_to_all | solution.py:140
  31.9 0.1 sub.48
  32.0 0.6 reduce-window.6
  32.6 0.2 slice_reduce_fusion
  32.8 0.6 fusion.18
  33.4 7.7 %all-to-all-done.1 = bf16[4,48,2048]{2,1,0:T(8,128)(2,1)} async-done(((bf16[4,48,2048]{2,1,0:T(8,128)(2,1)}), bf16[4,48,2048]{2,1,0:T(8,128)(2,1)}, u32[]{:S(2)}, u32[]{:S(2)}) %all-to-all-start.1) | async-done | bytes 786464 | tf_op jit(solution)/shard_map/all_to_all | solution.py:140
  41.1 1.7 fusion.21
  42.9 0.9 convert_element_type.93
  43.8 5.2 %all-to-all-start.2 = ((bf16[32,12,512]{2,1,0:T(8,128)(2,1)}), bf16[32,12,512]{2,1,0:T(8,128)(2,1)S(1)}, u32[]{:S(2)}, u32[]{:S(2)}) async-start(bf16[32,12,512]{2,1,0:T(8,128)(2,1)} %convert_element_type.93), calls=%async_computation.2 | async-start | bytes 1048576 | tf_op jit(solution)/shard_map/all_to_all | solution.py:150
  49.2 0.1 gt.15
  49.3 13.8 %all-to-all-done.2 = bf16[32,12,512]{2,1,0:T(8,128)(2,1)S(1)} async-done(((bf16[32,12,512]{2,1,0:T(8,128)(2,1)}), bf16[32,12,512]{2,1,0:T(8,128)(2,1)S(1)}, u32[]{:S(2)}, u32[]{:S(2)}) %all-to-all-start.2) | async-done | bytes 393248 | tf_op jit(solution)/shard_map/all_to_all | solution.py:150
  63.2 0.1 convert_reduce_fusion
  63.2 0.1 copy.31
  63.4 0.2 copy.44
  63.6 0.2 fusion.28
  63.8 0.1 fusion.30
  64.0 0.7 fusion.25
  64.7 8.0 %collective-permute-done.2 = bf16[12,4096]{1,0:T(8,128)(2,1)S(1)} collective-permute-done((bf16[12,4096]{1,0:T(8,128)(2,1)S(1)}, bf16[12,4096]{1,0:T(8,128)(2,1)S(1)}, u32[]{:S(2)}, u32[]{:S(2)}) %collective-permute-start.2) | collective-permute-done | bytes 98336 | tf_op jit(solution)/shard_map/ppermute | solution.py:52
  72.7 1.0 convolution_convert_fusion
  73.7 41.0 %all_to_all.25 = bf16[16,24,4096]{2,1,0:T(8,128)(2,1)S(1)} all-to-all(bf16[16,24,4096]{2,1,0:T(8,128)(2,1)S(1)} %convolution_convert_fusion), channel_id=1, replica_groups=mesh['zh'=2,'dl'=4,'tensor'=4] {'dl','tensor'}, dimensions={0} | all-to-all | bytes 6291456 | tf_op jit(solution)/shard_map/all_to_all | solution.py:86
  114.8 2.7 %fusion.4 = f32[16,24,768]{2,1,0:T(8,128)S(1)} fusion(bf16[16,24,4096]{2,1,0:T(8,128)(2,1)S(1)} %all_to_all.25, bf16[1,4096,768]{2,1,0:T(8,128)(2,1)S(1)} %bitcast.94), kind=kOutput, calls=%fused_computation.7 | convolution fusion | flops 2415919104 | bytes 10616832 | tf_op jit(solution)/shard_map/hcd,df->hcf/dot_general | solution.py:87
  117.6 2.8 %fusion.15 = bf16[16,24,768]{2,1,0:T(8,128)(2,1)S(1)} fusion(bf16[16,24,4096]{2,1,0:T(8,128)(2,1)S(1)} %all_to_all.25, bf16[1,4096,768]{2,1,0:T(8,128)(2,1)S(1)} %bitcast.96, f32[16,24,768]{2,1,0:T(8,128)S(1)} %fusion.4), kind=kOutput, calls=%fused_computation.20 | convolution fusion | flops 2417688576 | bytes 11206656 | tf_op jit(solution)/shard_map/hcd,df->hcf/dot_general | solution.py:88
  120.4 4.1 %fusion = bf16[16,24,4096]{2,1,0:T(8,128)(2,1)} fusion(bf16[16,24,768]{2,1,0:T(8,128)(2,1)S(1)} %fusion.15, bf16[1,768,4096]{2,1,0:T(8,128)(2,1)S(1)} %bitcast.98), kind=kOutput, calls=%fused_computation.3 | convolution fusion | flops 2415919104 | bytes 10027008 | tf_op jit(solution)/shard_map/hcf,fd->hcd/dot_general | solution.py:91
  124.5 4.6 %reshape.201 = bf16[16,576,128]{2,1,0:T(8,128)(2,1)} reshape(bf16[16,18,4096]{2,1,0:T(8,128)(2,1)} %bitcast.81) | data formatting | bytes 4718592 | tf_op jit(solution)/shard_map/reshape | solution.py:96
  129.1 6.6 %all-to-all-start.4 = ((bf16[16,576,128]{2,1,0:T(8,128)(2,1)}), bf16[16,576,128]{2,1,0:T(8,128)(2,1)}, u32[]{:S(2)}, u32[]{:S(2)}) async-start(bf16[16,576,128]{2,1,0:T(8,128)(2,1)} %reshape.201), calls=%async_computation.4 | async-start | bytes 4718592 | tf_op jit(solution)/shard_map/all_to_all | solution.py:97
  135.8 0.1 broadcast_compare_fusion.4
  136.0 33.7 %all-to-all-done.4 = bf16[16,576,128]{2,1,0:T(8,128)(2,1)} async-done(((bf16[16,576,128]{2,1,0:T(8,128)(2,1)}), bf16[16,576,128]{2,1,0:T(8,128)(2,1)}, u32[]{:S(2)}, u32[]{:S(2)}) %all-to-all-start.4) | async-done | bytes 2359328 | tf_op jit(solution)/shard_map/all_to_all | solution.py:97
  169.7 5.0 %reshape.202 = bf16[288,4096]{1,0:T(8,128)(2,1)} reshape(bf16[16,576,128]{2,1,0:T(8,128)(2,1)} %all-to-all-done.4) | data formatting | bytes 4718592 | tf_op jit(solution)/shard_map/reshape | solution.py:98
  174.6 3.8 %gather_fusion.1 = bf16[96,4096]{1,0:T(8,128)(2,1)S(1)} fusion(bf16[288,4096]{1,0:T(8,128)(2,1)} %reshape.202, s32[1024]{0:T(1024)S(1)} %pad_clamp_fusion), kind=kCustom, calls=%fused_computation.1.clone | custom fusion | bytes 1573248 | tf_op jit(solution)/shard_map/jit(_take)/gather | solution.py:107
  178.4 0.7 fusion.10
  179.1 1.0 collective-permute-start.3
  180.1 3.8 %gather_fusion = bf16[96,4096]{1,0:T(8,128)(2,1)S(1)} fusion(bf16[288,4096]{1,0:T(8,128)(2,1)} %reshape.202, s32[1024]{0:T(1024)S(1)} %pad_clamp_fusion.1), kind=kCustom, calls=%fused_computation.clone | custom fusion | bytes 1573248 | tf_op jit(solution)/shard_map/jit(_take)/gather | solution.py:107
  183.8 0.7 fusion.11
  184.5 3.1 %collective-permute-done.3 = bf16[12,4096]{1,0:T(8,128)(2,1)S(1)} collective-permute-done((bf16[12,4096]{1,0:T(8,128)(2,1)S(1)}, bf16[12,4096]{1,0:T(8,128)(2,1)S(1)}, u32[]{:S(2)}, u32[]{:S(2)}) %collective-permute-start.3) | collective-permute-done | bytes 98336 | tf_op jit(solution)/shard_map/ppermute | solution.py:52
  187.6 0.7 add_convert_fusion
  (65 shorter events, 1.0 us)
Async XLA Ops:
  0.6 32.2 %copy-start = (bf16[2048,512]{1,0:T(8,128)(2,1)S(1)}, bf16[2048,512]{1,0:T(8,128)(2,1)}, u32[]{:S(2)}) copy-start(bf16[2048,512]{1,0:T(8,128)(2,1)} %param.23) | copy-start | bytes 6291460
  0.6 5.6 %copy-start.6 = (bf16[48,128]{1,0:T(8,128)(2,1)S(1)}, bf16[48,128]{1,0:T(8,128)(2,1)}, u32[]{:S(2)}) copy-start(bf16[48,128]{1,0:T(8,128)(2,1)} %param.18) | copy-start | bytes 36868
  0.7 5.6 %copy-start.7 = (bf16[48,128,128]{2,1,0:T(8,128)(2,1)S(1)}, bf16[48,128,128]{2,1,0:T(8,128)(2,1)}, u32[]{:S(2)}) copy-start(bf16[48,128,128]{2,1,0:T(8,128)(2,1)} %param.20) | copy-start | bytes 4718596
  6.9 7.1 %copy-start.4 = (s32[12,8]{0,1:T(8,128)S(1)}, s32[12,8]{0,1:T(8,128)}, u32[]{:S(2)}) copy-start(s32[12,8]{0,1:T(8,128)} %param.25) | copy-start | bytes 1156
  6.9 7.1 %copy-start.5 = (f32[12,8]{0,1:T(8,128)S(1)}, f32[12,8]{0,1:T(8,128)}, u32[]{:S(2)}) copy-start(f32[12,8]{0,1:T(8,128)} %param.26) | copy-start | bytes 1156
  8.0 18.1 %all-to-all-start = ((bf16[4,48,2048]{2,1,0:T(8,128)(2,1)}), bf16[4,48,2048]{2,1,0:T(8,128)(2,1)S(1)}, u32[]{:S(2)}, u32[]{:S(2)}) async-start(bf16[4,48,2048]{2,1,0:T(8,128)(2,1)} %broadcast_in_dim.86), calls=%async_computation | async-start | bytes 1572864 | tf_op jit(solution)/shard_map/all_to_all | solution.py:140
  11.7 12.0 %collective-permute-start = (bf16[48,2048]{1,0:T(8,128)(2,1)S(1)}, bf16[48,2048]{1,0:T(8,128)(2,1)S(1)}, u32[]{:S(2)}, u32[]{:S(2)}) collective-permute-start(bf16[48,2048]{1,0:T(8,128)(2,1)S(1)} %bitcast.88), channel_id=1, source_target_pairs={{0,16},{16,0},{1,17},{17,1},{2,18},{18,2},{3,19},{19,3},{4,20},{20... | collective-permute-start | bytes 589832 | tf_op jit(solution)/shard_map/ppermute | solution.py:52
  14.0 17.7 %collective-permute-start.1 = (f32[12,16]{0,1:T(8,128)S(1)}, f32[12,16]{0,1:T(8,128)S(1)}, u32[]{:S(2)}, u32[]{:S(2)}) collective-permute-start(f32[12,16]{0,1:T(8,128)S(1)} %pad_maximum_fusion), channel_id=1, source_target_pairs={{0,16},{16,0},{1,17},{17,1},{2,18},{18,2},{3,19},{19,3},{4,20},{20... | collective-permute-start | bytes 2312 | tf_op jit(solution)/shard_map/ppermute | solution.py:52
  27.1 14.0 %all-to-all-start.1 = ((bf16[4,48,2048]{2,1,0:T(8,128)(2,1)}), bf16[4,48,2048]{2,1,0:T(8,128)(2,1)}, u32[]{:S(2)}, u32[]{:S(2)}) async-start(bf16[4,48,2048]{2,1,0:T(8,128)(2,1)} %broadcast_in_dim.87), calls=%async_computation.1 | async-start | bytes 1572864 | tf_op jit(solution)/shard_map/all_to_all | solution.py:140
  42.9 20.7 %copy-start.2 = (bf16[12,4096]{1,0:T(8,128)(2,1)S(1)}, bf16[12,4096]{1,0:T(8,128)(2,1)}, u32[]{:S(2)}) copy-start(bf16[12,4096]{1,0:T(8,128)(2,1)} %param.22) | copy-start | bytes 294916
  43.8 20.0 %copy-start.3 = (f32[4096]{0:T(1024)S(1)}, f32[4096]{0:T(1024)}, u32[]{:S(2)}) copy-start(f32[4096]{0:T(1024)} %param.24) | copy-start | bytes 49156
  43.8 19.4 %all-to-all-start.2 = ((bf16[32,12,512]{2,1,0:T(8,128)(2,1)}), bf16[32,12,512]{2,1,0:T(8,128)(2,1)S(1)}, u32[]{:S(2)}, u32[]{:S(2)}) async-start(bf16[32,12,512]{2,1,0:T(8,128)(2,1)} %convert_element_type.93), calls=%async_computation.2 | async-start | bytes 1048576 | tf_op jit(solution)/shard_map/all_to_all | solution.py:150
  63.2 51.6 %slice-start = ((s8[6291456]{0:T(1024)(128)(4,1)}), s8[4194304]{0:T(1024)(128)(4,1)S(1)}, s32[]{:S(2)}) async-start(s8[6291456]{0:T(1024)(128)(4,1)} %bitcast.93), calls=%async_computation.5 | async-start | bytes 8388608
  63.7 51.0 %copy-start.1 = (bf16[12,4096]{1,0:T(8,128)(2,1)}, bf16[12,4096]{1,0:T(8,128)(2,1)S(1)}, u32[]{:S(2)}) copy-start(bf16[12,4096]{1,0:T(8,128)(2,1)S(1)} %get-tuple-element.12) | copy-start | bytes 294916
  63.9 8.8 %collective-permute-start.2 = (bf16[12,4096]{1,0:T(8,128)(2,1)S(1)}, bf16[12,4096]{1,0:T(8,128)(2,1)S(1)}, u32[]{:S(2)}, u32[]{:S(2)}) collective-permute-start(bf16[12,4096]{1,0:T(8,128)(2,1)S(1)} %fusion.30), channel_id=1, source_target_pairs={{0,16},{16,0},{1,17},{17,1},{2,18},{18,2},{3,19},{19,3},{4,20},{20... | collective-permute-start | bytes 294920 | tf_op jit(solution)/shard_map/ppermute | solution.py:52
  64.7 50.1 %slice-start.1 = ((s8[6291456]{0:T(1024)(128)(4,1)}), s8[2097152]{0:T(1024)(128)(4,1)S(1)}, s32[]{:S(2)}) async-start(s8[6291456]{0:T(1024)(128)(4,1)} %bitcast.93), calls=%async_computation.6 | async-start | bytes 4194304
  73.7 43.9 %slice-start.2 = ((s8[6291456]{0:T(1024)(128)(4,1)}), s8[4194304]{0:T(1024)(128)(4,1)S(1)}, s32[]{:S(2)}) async-start(s8[6291456]{0:T(1024)(128)(4,1)} %bitcast.95), calls=%async_computation.7 | async-start | bytes 8388608
  114.8 2.8 %slice-start.3 = ((s8[6291456]{0:T(1024)(128)(4,1)}), s8[2097152]{0:T(1024)(128)(4,1)S(1)}, s32[]{:S(2)}) async-start(s8[6291456]{0:T(1024)(128)(4,1)} %bitcast.95), calls=%async_computation.8 | async-start | bytes 4194304
  114.8 5.6 %slice-start.4 = ((s8[6291456]{0:T(1024)(128)(4,1)}), s8[4194304]{0:T(1024)(128)(4,1)S(1)}, s32[]{:S(2)}) async-start(s8[6291456]{0:T(1024)(128)(4,1)} %bitcast.97), calls=%async_computation.9 | async-start | bytes 8388608
  117.6 2.8 %slice-start.5 = ((s8[6291456]{0:T(1024)(128)(4,1)}), s8[2097152]{0:T(1024)(128)(4,1)S(1)}, s32[]{:S(2)}) async-start(s8[6291456]{0:T(1024)(128)(4,1)} %bitcast.97), calls=%async_computation.10 | async-start | bytes 4194304
  129.1 40.6 %all-to-all-start.4 = ((bf16[16,576,128]{2,1,0:T(8,128)(2,1)}), bf16[16,576,128]{2,1,0:T(8,128)(2,1)}, u32[]{:S(2)}, u32[]{:S(2)}) async-start(bf16[16,576,128]{2,1,0:T(8,128)(2,1)} %reshape.201), calls=%async_computation.4 | async-start | bytes 4718592 | tf_op jit(solution)/shard_map/all_to_all | solution.py:97
  179.1 8.5 %collective-permute-start.3 = (bf16[12,4096]{1,0:T(8,128)(2,1)S(1)}, bf16[12,4096]{1,0:T(8,128)(2,1)S(1)}, u32[]{:S(2)}, u32[]{:S(2)}) collective-permute-start(bf16[12,4096]{1,0:T(8,128)(2,1)S(1)} %fusion.10), channel_id=1, source_target_pairs={{0,16},{16,0},{1,17},{17,1},{2,18},{18,2},{3,19},{19,3},{4,20},{20... | collective-permute-start | bytes 294920 | tf_op jit(solution)/shard_map/ppermute | solution.py:52
